TPU v7x, 1024 devices: a whole 4x8x16 slice. The times are simulated.
1024 devices in a mesh: tm: 8 (over x, core), rows: 128 (over z, y).
Axes of the slice: x: 4, y: 8, z: 16, core: 2. Of those that a mesh axis runs over, the one named last changes fastest.
Arguments:
- video: bfloat16 [16, 256, 128, 128], P('tm', 'rows'), may hold values from -6 to 6
- kernel: bfloat16 [3, 3, 3, 128, 128], replicated, may hold values from -0.109375 to 0.109375
- cotangent: bfloat16 [16, 256, 128, 128], P('tm', 'rows'), may hold values from -24 to 24
Outputs:
- activated: bfloat16 [16, 256, 128, 128], P('tm', 'rows')
- input_grad: bfloat16 [16, 256, 128, 128], P('tm', 'rows')
- kernel_grad: float32 [128, 3456], P('rows', 'tm')
All inputs are finite; a program needn't handle non-finite values.
Results may differ from a plain program's by a relative error of at most 0.0049.
Values may be sent and summed in bfloat16 or wider, within the bound.
No kernel may reach another device: no remote copies, remote signals or barrier semaphores. Data moves between devices by JAX's collectives and lax.ppermute only.
A program may use at most 32 MiB of HBM per device.

v0:
```python
import jax
import jax.numpy as jnp
from jax import lax
from jax.sharding import PartitionSpec as P


def passed_along(x, axis, by):
    devices = lax.axis_size(axis)
    pairs = [(i, i + by) for i in range(devices) if 0 <= i + by < devices]
    return lax.ppermute(x, axis, pairs)


def padded(block, sides, width):
    for axis, dim in sides:
        count = lax.axis_size(axis)
        forward = [(i, i + 1) for i in range(count - 1)]
        backward = [(target, source) for source, target in forward]
        low = lax.ppermute(
            lax.slice_in_dim(block, block.shape[dim] - width, None, axis=dim), axis, forward
        )
        high = lax.ppermute(lax.slice_in_dim(block, 0, width, axis=dim), axis, backward)
        block = jnp.concatenate([low, block, high], axis=dim)
    return block


def make_patches(extended):
    frames = extended.shape[0] - 2
    height = extended.shape[1] - 2
    width = extended.shape[2]
    chans = extended.shape[3]
    wide = jnp.pad(extended, ((0, 0), (0, 0), (1, 1), (0, 0)))
    patches = []
    for a in range(3):
        for b in range(3):
            parts = [wide[a : a + frames, b : b + height, c : c + width] for c in range(3)]
            patches.append(
                jnp.concatenate(parts, axis=-1).reshape(frames * height * width, 3 * chans)
            )
    return patches


def apply_taps(patches, kmat):
    total = jnp.dot(patches[0], kmat[0, 0], preferred_element_type=jnp.float32)
    for index in range(1, 9):
        total = total + jnp.dot(
            patches[index], kmat[index // 3, index % 3], preferred_element_type=jnp.float32
        )
    return total


def local(video, kernel, cotangent):
    frames, height, width, chans = video.shape
    forward_mat = kernel.reshape(3, 3, 3 * chans, chans)
    earlier = passed_along(video, "tm", 1)
    extended = padded(jnp.concatenate([earlier, video], axis=0), (("rows", 1),), 1)
    patches = make_patches(extended)
    pre = apply_taps(patches, forward_mat)
    sig = 1.0 / (1.0 + jnp.exp(-pre))
    activated = (pre * sig).astype(jnp.bfloat16).reshape(frames, height, width, chans)
    grad_flat = cotangent.reshape(frames * height * width, chans).astype(jnp.float32)
    pre_grad = (grad_flat * sig * (1.0 + pre * (1.0 - sig))).astype(jnp.bfloat16)
    pre_grid = pre_grad.reshape(frames, height, width, chans)
    later = passed_along(pre_grid, "tm", -1)
    grad_ext = padded(jnp.concatenate([pre_grid, later], axis=0), (("rows", 1),), 1)
    flipped = jnp.transpose(kernel[::-1, ::-1, ::-1], (0, 1, 2, 4, 3)).reshape(
        3, 3, 3 * chans, chans
    )
    input_grad = (
        apply_taps(make_patches(grad_ext), flipped)
        .astype(jnp.bfloat16)
        .reshape(frames, height, width, chans)
    )
    blocks = [
        lax.dot_general(
            pre_grad, piece, (((0,), (0,)), ((), ())), preferred_element_type=jnp.float32
        )
        for piece in patches
    ]
    partial_grad = jnp.concatenate(blocks, axis=1)
    owned = lax.psum_scatter(partial_grad, "rows", scatter_dimension=0, tiled=True)
    kernel_grad = lax.psum_scatter(owned, "tm", scatter_dimension=1, tiled=True)
    return (activated, input_grad, kernel_grad)


def solution(mesh):
    in_specs = (P("tm", "rows", None, None), P(), P("tm", "rows", None, None))
    out_specs = (P("tm", "rows", None, None), P("tm", "rows", None, None), P("rows", "tm"))
    return jax.shard_map(local, mesh=mesh, in_specs=in_specs, out_specs=out_specs, check_vma=False)
```

profile of v0, /device:TPU:56, one launch (start us, length us, event | category | flops | bytes accessed | tf_op | source)
XLA Modules:
  0.0 396.6 jit_solution(9770795556046254894)
XLA Ops:
  7.2 1.7 collective-permute-start
  9.0 1.2 collective-permute-done
  10.1 0.9 constant_dynamic-update-slice_fusion
  11.1 3.5 collective-permute-start.1
  14.6 2.4 collective-permute-start.2
  17.0 2.0 copy.7
  19.1 1.3 dynamic-slice
  20.3 3.2 collective-permute-done.2
  23.7 0.5 fusion.26
  24.5 0.9 copy-done
  25.4 0.3 fusion.23
  25.8 0.3 convolution_add_fusion.15
  26.1 0.3 convolution_add_fusion.14
  26.5 0.3 convolution_add_fusion.13
  26.7 0.3 convolution_add_fusion.12
  27.4 0.3 convolution_add_fusion.11
  27.6 0.3 convolution_add_fusion.10
  27.9 0.3 convolution_add_fusion.9
  28.3 1.0 fusion.15
  29.3 1.0 convolution_dynamic-update-slice_fusion.8
  30.2 1.0 convolution_dynamic-update-slice_fusion.7
  31.2 0.9 convolution_dynamic-update-slice_fusion.6
  32.2 0.9 convolution_dynamic-update-slice_fusion.5
  33.1 0.9 convolution_dynamic-update-slice_fusion.4
  34.0 1.0 convolution_dynamic-update-slice_fusion.3
  35.0 0.9 convolution_dynamic-update-slice_fusion.2
  35.9 1.3 collective-permute-start.3
  37.2 0.9 convolution_dynamic-update-slice_fusion.1
  38.2 1.9 collective-permute-done.3
  40.1 3.2 collective-permute-start.4
  43.4 2.6 collective-permute-start.5
  46.0 1.0 convolution_dynamic-update-slice_fusion
  47.0 5.3 %collective-permute-done.5 = bf16[4,1,128,128]{3,2,1,0:T(8,128)(2,1)S(1)} collective-permute-done((bf16[4,1,128,128]{3,2,1,0:T(8,128)(2,1)S(1)}, bf16[4,1,128,128]{3,2,1,0:T(8,128)(2,1)S(1)}, u32[]{:S(2)}, u32[]{:S(2)}) %collective-permute-start.5) | collective-permute-done | bytes 131104 | tf_op jit(solution)/shard_map/ppermute | solution.py:21
  52.6 0.5 fusion.25
  53.2 0.3 fusion.22
  53.9 0.3 convolution_add_fusion.7
  54.2 0.3 convolution_add_fusion.6
  54.5 0.3 convolution_add_fusion.5
  54.7 0.3 convolution_add_fusion.4
  55.0 0.3 convolution_add_fusion.3
  55.3 0.3 convolution_add_fusion.2
  55.5 0.3 convolution_add_fusion.1
  55.8 289.5 %all-reduce.5.cloned.1.call-done = f32[128,3456]{1,0:T(8,128)} async-done(((f32[128,3456]{1,0:T(8,128)}), f32[128,3456]{1,0:T(8,128)}) %all-reduce.5.cloned.1.call-update) | async-done | bytes 1769488
  345.4 1.6 constant_dynamic-slice_fusion
  346.9 1.8 copy.8
  348.7 0.9 fusion
  349.7 38.5 %reduce-scatter.4.cloned.1.call-done = f32[432,1]{1,0:T(8,128)} async-done(((f32[3456,1]{1,0:T(8,128)}), f32[432,1]{1,0:T(8,128)}) %reduce-scatter.4.cloned.1.call-update) | async-done | bytes 1744
  388.1 1.6 copy.9
  (32 shorter events, 2.0 us)
Async XLA Ops:
  7.2 338.2 %all-reduce.5.cloned.1.call-start = ((), (), s32[]{:S(2)}) async-start(), calls=%async_computation.2 | async-start | bytes 3538944
  7.2 2.9 collective-permute-start
  11.1 9.2 %collective-permute-start.1 = (bf16[4,1,128,128]{3,2,1,0:T(8,128)(2,1)S(1)}, bf16[4,1,128,128]{3,2,1,0:T(8,128)(2,1)S(1)}, u32[]{:S(2)}, u32[]{:S(2)}) collective-permute-start(bf16[4,1,128,128]{3,2,1,0:T(8,128)(2,1)S(1)} %get-tuple-element.60), channel_id=1, source_target_pairs={{0,1},{1,2},{2,3},{3,4},{4,5},{5,6},{6,7},{7,8},{8,9},{9,10},{10,1... | collective-permute-start | bytes 393224 | tf_op jit(solution)/shard_map/ppermute | solution.py:18
  14.6 9.0 %collective-permute-start.2 = (bf16[4,1,128,128]{3,2,1,0:T(8,128)(2,1)S(1)}, bf16[4,1,128,128]{3,2,1,0:T(8,128)(2,1)S(1)}, u32[]{:S(2)}, u32[]{:S(2)}) collective-permute-start(bf16[4,1,128,128]{3,2,1,0:T(8,128)(2,1)S(1)} %get-tuple-element.61), channel_id=1, source_target_pairs={{1,0},{2,1},{3,2},{4,3},{5,4},{6,5},{7,6},{8,7},{9,8},{10,9},{11,1... | collective-permute-start | bytes 393224 | tf_op jit(solution)/shard_map/ppermute | solution.py:21
  24.3 1.2 copy-start
  26.3 0.9 copy-start.1
  27.4 0.9 copy-start.2
  35.9 4.1 %collective-permute-start.3 = (bf16[2,2,128,128]{3,2,1,0:T(8,128)(2,1)S(1)}, bf16[2,2,128,128]{3,2,1,0:T(8,128)(2,1)S(1)}, u32[]{:S(2)}, u32[]{:S(2)}) collective-permute-start(bf16[2,2,128,128]{3,2,1,0:T(8,128)(2,1)S(1)} %bitcast.123), channel_id=1, source_target_pairs={{128,0},{256,128},{384,256},{512,384},{640,512},{768,640},{896,768... | collective-permute-start | bytes 393224 | tf_op jit(solution)/shard_map/ppermute | solution.py:10
  40.1 6.9 %collective-permute-start.4 = (bf16[4,1,128,128]{3,2,1,0:T(8,128)(2,1)S(1)}, bf16[4,1,128,128]{3,2,1,0:T(8,128)(2,1)S(1)}, u32[]{:S(2)}, u32[]{:S(2)}) collective-permute-start(bf16[4,1,128,128]{3,2,1,0:T(8,128)(2,1)S(1)} %get-tuple-element.51), channel_id=1, source_target_pairs={{0,1},{1,2},{2,3},{3,4},{4,5},{5,6},{6,7},{7,8},{8,9},{9,10},{10,1... | collective-permute-start | bytes 393224 | tf_op jit(solution)/shard_map/ppermute | solution.py:18
  43.4 9.0 %collective-permute-start.5 = (bf16[4,1,128,128]{3,2,1,0:T(8,128)(2,1)S(1)}, bf16[4,1,128,128]{3,2,1,0:T(8,128)(2,1)S(1)}, u32[]{:S(2)}, u32[]{:S(2)}) collective-permute-start(bf16[4,1,128,128]{3,2,1,0:T(8,128)(2,1)S(1)} %get-tuple-element.52), channel_id=1, source_target_pairs={{1,0},{2,1},{3,2},{4,3},{5,4},{6,5},{7,6},{8,7},{9,8},{10,9},{11,1... | collective-permute-start | bytes 393224 | tf_op jit(solution)/shard_map/ppermute | solution.py:21
  46.9 341.2 %reduce-scatter.4.cloned.1.call-start = ((), (), s32[]{:S(2)}) async-start(), calls=%async_computation.1 | async-start | bytes 1990656
Sparse Core Ops, SparseCore 0:
  47.1 298.2 all-reduce.4
  348.9 39.2 reduce-scatter.3
where the time goes:
time: 398 us; the launch traced here: 397 us
  waiting for transfers between devices  340 us (85%)
  starting transfers between devices  14.8 us (4%)
  matrix products  14.7 us (4%)
  between operations  14.4 us (4%)
  local copies, waits for them, and re-layouts  11.6 us (3%)
    unnamed x4, waiting for transfers between devices  328 us
    unnamed x12, local copies, waits for them, and re-layouts  9.54 us
    dot_general x9, matrix products, local(): lax.dot_general(pre_grad, piece, (((0,), (0,)), ((), ())), preferred_elem...  8.56 us
    ppermute x2, waiting for transfers between devices, padded(): lax.ppermute(lax.slice_in_dim(block, 0, width, axis=dim), axis, backward)  8.56 us
  transfers between devices with their start and end apart: 8, of which 6 were waited for; matrix products, arithmetic and copies ran while one was open for 2% of the time, Pallas kernels for 0%

commit v1 on v0

--- a/solution.py
+++ b/solution.py
@@ -77,8 +77,8 @@
         for piece in patches
     ]
     partial_grad = jnp.concatenate(blocks, axis=1)
-    owned = lax.psum_scatter(partial_grad, "rows", scatter_dimension=0, tiled=True)
-    kernel_grad = lax.psum_scatter(owned, "tm", scatter_dimension=1, tiled=True)
+    owned = lax.psum_scatter(partial_grad, "tm", scatter_dimension=1, tiled=True)
+    kernel_grad = lax.psum_scatter(owned, "rows", scatter_dimension=0, tiled=True)
     return (activated, input_grad, kernel_grad)
 
 

time: 398 us -> 389 us (0.977)
  waiting for transfers between devices: 340 us -> 328 us
    unnamed x4, waiting for transfers between devices: 328 us -> 319 us
  transfers between devices with their start and end apart: 8 -> 8, of which waited for: 6 -> 6; matrix products, arithmetic and copies ran while one was open for 2% -> 3% of each run, Pallas kernels for 0% -> 0%
where the time goes in v1:
time: 389 us; the launch traced here: 386 us
  waiting for transfers between devices  328 us (84%)
  starting transfers between devices  14.8 us (4%)
  matrix products  14.7 us (4%)
  between operations  14.4 us (4%)
  local copies, waits for them, and re-layouts  13.2 us (3%)
    unnamed x4, waiting for transfers between devices  319 us
    unnamed x12, local copies, waits for them, and re-layouts  11 us
    dot_general x9, matrix products, local(): lax.dot_general(pre_grad, piece, (((0,), (0,)), ((), ())), preferred_elem...  8.56 us
  transfers between devices with their start and end apart: 8, of which 6 were waited for; matrix products, arithmetic and copies ran while one was open for 3% of the time, Pallas kernels for 0%

profile of v1, /device:TPU:56, one launch (start us, length us, event | category | flops | bytes accessed | tf_op | source)
XLA Modules:
  0.0 386.3 jit_solution(9722810967203220438)
XLA Ops:
  7.2 1.7 collective-permute-start
  9.0 1.2 collective-permute-done
  10.1 0.9 constant_dynamic-update-slice_fusion
  11.1 3.5 collective-permute-start.1
  14.6 2.4 collective-permute-start.2
  17.0 2.0 copy.7
  19.1 1.3 dynamic-slice
  20.4 3.2 collective-permute-done.2
  23.7 0.5 fusion.26
  24.5 0.9 copy-done
  25.4 0.3 fusion.23
  25.8 0.3 convolution_add_fusion.15
  26.1 0.3 convolution_add_fusion.14
  26.5 0.3 convolution_add_fusion.13
  26.7 0.3 convolution_add_fusion.12
  27.4 0.3 convolution_add_fusion.11
  27.6 0.3 convolution_add_fusion.10
  27.9 0.3 convolution_add_fusion.9
  28.3 1.0 fusion.15
  29.3 1.0 convolution_dynamic-update-slice_fusion.8
  30.2 1.0 convolution_dynamic-update-slice_fusion.7
  31.2 0.9 convolution_dynamic-update-slice_fusion.6
  32.2 0.9 convolution_dynamic-update-slice_fusion.5
  33.1 0.9 convolution_dynamic-update-slice_fusion.4
  34.0 1.0 convolution_dynamic-update-slice_fusion.3
  35.0 0.9 convolution_dynamic-update-slice_fusion.2
  35.9 1.3 collective-permute-start.3
  37.2 0.9 convolution_dynamic-update-slice_fusion.1
  38.2 1.9 collective-permute-done.3
  40.1 3.3 collective-permute-start.4
  43.4 2.5 collective-permute-start.5
  46.0 1.0 convolution_dynamic-update-slice_fusion
  46.9 2.7 copy.8
  49.7 2.6 collective-permute-done.5
  52.7 0.5 fusion.25
  53.7 0.3 fusion.22
  54.0 0.3 convolution_add_fusion.7
  54.3 0.3 convolution_add_fusion.6
  54.6 0.3 convolution_add_fusion.5
  54.8 0.3 convolution_add_fusion.4
  55.1 0.3 convolution_add_fusion.3
  55.4 0.3 convolution_add_fusion.2
  55.6 0.3 convolution_add_fusion.1
  55.9 48.3 %reduce-scatter.4.cloned.1.call-done = f32[432,128]{1,0:T(8,128)} async-done(((f32[3456,128]{1,0:T(8,128)}), f32[432,128]{1,0:T(8,128)}) %reduce-scatter.4.cloned.1.call-update) | async-done | bytes 221200
  104.2 1.8 copy.9
  106.0 0.9 fusion
  107.0 270.6 %all-reduce.5.cloned.1.call-done = f32[128,432]{1,0:T(8,128)} async-done(((f32[128,432]{1,0:T(8,128)}), f32[128,432]{1,0:T(8,128)}) %all-reduce.5.cloned.1.call-update) | async-done | bytes 221200
  377.5 1.9 constant_dynamic-slice_fusion
  (32 shorter events, 2.0 us)
Async XLA Ops:
  7.2 97.1 %reduce-scatter.4.cloned.1.call-start = ((), (), s32[]{:S(2)}) async-start(), calls=%async_computation.1 | async-start | bytes 1990656
  7.2 2.9 collective-permute-start
  11.1 9.3 %collective-permute-start.1 = (bf16[4,1,128,128]{3,2,1,0:T(8,128)(2,1)S(1)}, bf16[4,1,128,128]{3,2,1,0:T(8,128)(2,1)S(1)}, u32[]{:S(2)}, u32[]{:S(2)}) collective-permute-start(bf16[4,1,128,128]{3,2,1,0:T(8,128)(2,1)S(1)} %get-tuple-element.60), channel_id=1, source_target_pairs={{0,1},{1,2},{2,3},{3,4},{4,5},{5,6},{6,7},{7,8},{8,9},{9,10},{10,1... | collective-permute-start | bytes 393224 | tf_op jit(solution)/shard_map/ppermute | solution.py:18
  14.6 9.0 %collective-permute-start.2 = (bf16[4,1,128,128]{3,2,1,0:T(8,128)(2,1)S(1)}, bf16[4,1,128,128]{3,2,1,0:T(8,128)(2,1)S(1)}, u32[]{:S(2)}, u32[]{:S(2)}) collective-permute-start(bf16[4,1,128,128]{3,2,1,0:T(8,128)(2,1)S(1)} %get-tuple-element.61), channel_id=1, source_target_pairs={{1,0},{2,1},{3,2},{4,3},{5,4},{6,5},{7,6},{8,7},{9,8},{10,9},{11,1... | collective-permute-start | bytes 393224 | tf_op jit(solution)/shard_map/ppermute | solution.py:21
  24.3 1.2 copy-start
  26.3 0.9 copy-start.1
  27.4 0.9 copy-start.2
  35.9 4.1 %collective-permute-start.3 = (bf16[2,2,128,128]{3,2,1,0:T(8,128)(2,1)S(1)}, bf16[2,2,128,128]{3,2,1,0:T(8,128)(2,1)S(1)}, u32[]{:S(2)}, u32[]{:S(2)}) collective-permute-start(bf16[2,2,128,128]{3,2,1,0:T(8,128)(2,1)S(1)} %bitcast.123), channel_id=1, source_target_pairs={{128,0},{256,128},{384,256},{512,384},{640,512},{768,640},{896,768... | collective-permute-start | bytes 393224 | tf_op jit(solution)/shard_map/ppermute | solution.py:10
  40.1 9.6 %collective-permute-start.4 = (bf16[4,1,128,128]{3,2,1,0:T(8,128)(2,1)S(1)}, bf16[4,1,128,128]{3,2,1,0:T(8,128)(2,1)S(1)}, u32[]{:S(2)}, u32[]{:S(2)}) collective-permute-start(bf16[4,1,128,128]{3,2,1,0:T(8,128)(2,1)S(1)} %get-tuple-element.51), channel_id=1, source_target_pairs={{0,1},{1,2},{2,3},{3,4},{4,5},{5,6},{6,7},{7,8},{8,9},{9,10},{10,1... | collective-permute-start | bytes 393224 | tf_op jit(solution)/shard_map/ppermute | solution.py:18
  43.4 9.0 %collective-permute-start.5 = (bf16[4,1,128,128]{3,2,1,0:T(8,128)(2,1)S(1)}, bf16[4,1,128,128]{3,2,1,0:T(8,128)(2,1)S(1)}, u32[]{:S(2)}, u32[]{:S(2)}) collective-permute-start(bf16[4,1,128,128]{3,2,1,0:T(8,128)(2,1)S(1)} %get-tuple-element.52), channel_id=1, source_target_pairs={{1,0},{2,1},{3,2},{4,3},{5,4},{6,5},{7,6},{8,7},{9,8},{10,9},{11,1... | collective-permute-start | bytes 393224 | tf_op jit(solution)/shard_map/ppermute | solution.py:21
  49.7 327.8 %all-reduce.5.cloned.1.call-start = ((), (), s32[]{:S(2)}) async-start(), calls=%async_computation.2 | async-start | bytes 524288
Sparse Core Ops, SparseCore 0:
  49.8 54.3 reduce-scatter.3
  107.7 269.7 all-reduce.4

commit v2 on v1

--- a/solution.py
+++ b/solution.py
@@ -77,8 +77,9 @@
         for piece in patches
     ]
     partial_grad = jnp.concatenate(blocks, axis=1)
-    owned = lax.psum_scatter(partial_grad, "tm", scatter_dimension=1, tiled=True)
-    kernel_grad = lax.psum_scatter(owned, "rows", scatter_dimension=0, tiled=True)
+    parts = lax.axis_size("tm")
+    stacked = partial_grad.reshape(partial_grad.shape[0] * parts, partial_grad.shape[1] // parts)
+    kernel_grad = lax.psum_scatter(stacked, ("rows", "tm"), scatter_dimension=0, tiled=True)
     return (activated, input_grad, kernel_grad)
 
 

time: 389 us -> 568 us (1.46)
  waiting for transfers between devices: 328 us -> 508 us
    unnamed x4 -> x2, waiting for transfers between devices: 319 us -> 500 us
  transfers between devices with their start and end apart: 8 -> 7, of which waited for: 6 -> 5; matrix products, arithmetic and copies ran while one was open for 3% -> 2% of each run, Pallas kernels for 0% -> 0%
where the time goes in v2:
time: 568 us; the launch traced here: 566 us
  waiting for transfers between devices  508 us (89%)
  starting transfers between devices  14.8 us (3%)
  matrix products  14.8 us (3%)
  between operations  14.4 us (3%)
  local copies, waits for them, and re-layouts  12.7 us (2%)
    unnamed x2, waiting for transfers between devices  500 us
  transfers between devices with their start and end apart: 7, of which 5 were waited for; matrix products, arithmetic and copies ran while one was open for 2% of the time, Pallas kernels for 0%

profile of v2, /device:TPU:56, one launch (start us, length us, event | category | flops | bytes accessed | tf_op | source)
XLA Modules:
  0.0 565.7 jit_solution(1499380174586881372)
XLA Ops:
  7.2 1.7 collective-permute-start
  9.0 1.2 collective-permute-done
  10.1 0.9 constant_dynamic-update-slice_fusion
  11.1 3.5 collective-permute-start.1
  14.6 2.4 collective-permute-start.2
  17.0 2.0 copy.7
  19.1 1.3 dynamic-slice
  20.4 3.2 collective-permute-done.2
  23.7 0.5 fusion.26
  24.3 0.2 fusion.6
  24.5 0.9 copy-done
  25.4 0.3 fusion.23
  25.8 0.3 convolution_add_fusion.15
  26.1 0.3 convolution_add_fusion.14
  26.5 0.3 convolution_add_fusion.13
  26.7 0.3 convolution_add_fusion.12
  27.0 0.2 copy-done.1
  27.4 0.3 convolution_add_fusion.11
  27.6 0.3 convolution_add_fusion.10
  27.9 0.3 convolution_add_fusion.9
  28.3 1.0 fusion.15
  29.3 1.0 convolution_dynamic-update-slice_fusion.8
  30.3 0.9 convolution_dynamic-update-slice_fusion.7
  31.2 0.9 convolution_dynamic-update-slice_fusion.6
  32.1 0.9 convolution_dynamic-update-slice_fusion.5
  33.1 1.0 convolution_dynamic-update-slice_fusion.4
  34.0 0.9 convolution_dynamic-update-slice_fusion.3
  35.0 1.0 convolution_dynamic-update-slice_fusion.2
  35.9 1.3 collective-permute-start.3
  37.2 1.0 convolution_dynamic-update-slice_fusion.1
  38.2 1.9 collective-permute-done.3
  40.1 3.3 collective-permute-start.4
  43.4 2.6 collective-permute-start.5
  46.0 1.0 convolution_dynamic-update-slice_fusion
  46.9 4.2 reshape.105
  51.2 1.2 collective-permute-done.5
  52.6 0.5 fusion.25
  53.2 0.3 fusion.22
  53.5 0.3 convolution_add_fusion.7
  53.8 0.3 convolution_add_fusion.6
  54.2 0.3 convolution_add_fusion.5
  54.5 0.3 convolution_add_fusion.4
  54.9 0.3 convolution_add_fusion.3
  55.3 0.3 convolution_add_fusion.2
  55.5 0.3 convolution_add_fusion.1
  55.8 0.9 fusion
  56.7 500.2 %all-reduce.5.cloned.1.call-done = f32[1024,432]{1,0:T(8,128)} async-done(((f32[1024,432]{1,0:T(8,128)}), f32[1024,432]{1,0:T(8,128)}) %all-reduce.5.cloned.1.call-update) | async-done | bytes 1769488
  557.0 1.9 constant_dynamic-slice_fusion
  (28 shorter events, 1.6 us)
Async XLA Ops:
  7.2 549.8 %all-reduce.5.cloned.1.call-start = ((), (), s32[]{:S(2)}) async-start(), calls=%async_computation | async-start | bytes 4194304
  7.2 2.9 collective-permute-start
  11.1 9.2 %collective-permute-start.1 = (bf16[4,1,128,128]{3,2,1,0:T(8,128)(2,1)S(1)}, bf16[4,1,128,128]{3,2,1,0:T(8,128)(2,1)S(1)}, u32[]{:S(2)}, u32[]{:S(2)}) collective-permute-start(bf16[4,1,128,128]{3,2,1,0:T(8,128)(2,1)S(1)} %get-tuple-element.60), channel_id=1, source_target_pairs={{0,1},{1,2},{2,3},{3,4},{4,5},{5,6},{6,7},{7,8},{8,9},{9,10},{10,1... | collective-permute-start | bytes 393224 | tf_op jit(solution)/shard_map/ppermute | solution.py:18
  14.6 9.0 %collective-permute-start.2 = (bf16[4,1,128,128]{3,2,1,0:T(8,128)(2,1)S(1)}, bf16[4,1,128,128]{3,2,1,0:T(8,128)(2,1)S(1)}, u32[]{:S(2)}, u32[]{:S(2)}) collective-permute-start(bf16[4,1,128,128]{3,2,1,0:T(8,128)(2,1)S(1)} %get-tuple-element.61), channel_id=1, source_target_pairs={{1,0},{2,1},{3,2},{4,3},{5,4},{6,5},{7,6},{8,7},{9,8},{10,9},{11,1... | collective-permute-start | bytes 393224 | tf_op jit(solution)/shard_map/ppermute | solution.py:21
  24.3 1.2 copy-start
  26.3 0.9 copy-start.1
  27.4 0.9 copy-start.2
  35.9 4.1 collective-permute-start.3
  40.1 11.1 %collective-permute-start.4 = (bf16[4,1,128,128]{3,2,1,0:T(8,128)(2,1)S(1)}, bf16[4,1,128,128]{3,2,1,0:T(8,128)(2,1)S(1)}, u32[]{:S(2)}, u32[]{:S(2)}) collective-permute-start(bf16[4,1,128,128]{3,2,1,0:T(8,128)(2,1)S(1)} %get-tuple-element.51), channel_id=1, source_target_pairs={{0,1},{1,2},{2,3},{3,4},{4,5},{5,6},{6,7},{7,8},{8,9},{9,10},{10,1... | collective-permute-start | bytes 393224 | tf_op jit(solution)/shard_map/ppermute | solution.py:18
  43.4 9.0 %collective-permute-start.5 = (bf16[4,1,128,128]{3,2,1,0:T(8,128)(2,1)S(1)}, bf16[4,1,128,128]{3,2,1,0:T(8,128)(2,1)S(1)}, u32[]{:S(2)}, u32[]{:S(2)}) collective-permute-start(bf16[4,1,128,128]{3,2,1,0:T(8,128)(2,1)S(1)} %get-tuple-element.52), channel_id=1, source_target_pairs={{1,0},{2,1},{3,2},{4,3},{5,4},{6,5},{7,6},{8,7},{9,8},{10,9},{11,1... | collective-permute-start | bytes 393224 | tf_op jit(solution)/shard_map/ppermute | solution.py:21
Sparse Core Ops, SparseCore 0:
  51.3 505.6 all-reduce.4

commit v3 on v1

--- a/solution.py
+++ b/solution.py
@@ -48,6 +48,36 @@
     return total
 
 
+def exchanged_half(x, axis, bit, dim):
+    mine = (lax.axis_index(axis) // (1 << bit)) % 2
+    pairs = [(i, i ^ (1 << bit)) for i in range(lax.axis_size(axis))]
+    keep = lax.dynamic_index_in_dim(x, mine, axis=dim, keepdims=True)
+    send = lax.dynamic_index_in_dim(x, 1 - mine, axis=dim, keepdims=True)
+    return keep + lax.ppermute(send, axis, pairs)
+
+
+def halving_scatter(partial_grad):
+    outs, cols = partial_grad.shape
+    tm_bits = lax.axis_size("tm").bit_length() - 1
+    row_bits = lax.axis_size("rows").bit_length() - 1
+    block = cols >> tm_bits
+    x = partial_grad.reshape((outs,) + (2,) * tm_bits + (block,))
+    for bit in range(tm_bits):
+        x = exchanged_half(x, "tm", bit, tm_bits - bit)
+    x = x.reshape((2,) * row_bits + (block,))
+    y_bits = min(3, row_bits)
+    order = []
+    ys, zs = list(range(y_bits)), list(range(y_bits, row_bits))
+    while ys or zs:
+        if ys:
+            order.append(ys.pop(0))
+        if zs:
+            order.append(zs.pop(0))
+    for bit in order:
+        x = exchanged_half(x, "rows", bit, row_bits - 1 - bit)
+    return x.reshape(1, block)
+
+
 def local(video, kernel, cotangent):
     frames, height, width, chans = video.shape
     forward_mat = kernel.reshape(3, 3, 3 * chans, chans)
@@ -77,8 +107,7 @@
         for piece in patches
     ]
     partial_grad = jnp.concatenate(blocks, axis=1)
-    owned = lax.psum_scatter(partial_grad, "tm", scatter_dimension=1, tiled=True)
-    kernel_grad = lax.psum_scatter(owned, "rows", scatter_dimension=0, tiled=True)
+    kernel_grad = halving_scatter(partial_grad)
     return (activated, input_grad, kernel_grad)
 
 

time: 389 us -> 149 us (0.38)
  waiting for transfers between devices: 328 us -> 44.3 us
  starting transfers between devices: 14.8 us -> 75.8 us
  between operations: 14.4 us -> 1.78 us
    unnamed x4 -> x0, waiting for transfers between devices: 319 us -> none
    ppermute x0 -> x10, starting transfers between devices: none -> 61 us  [exchanged_half(): return keep + lax.ppermute(send, axis, pairs)]
    ppermute x0 -> x10, waiting for transfers between devices: none -> 38.4 us  [exchanged_half(): return keep + lax.ppermute(send, axis, pairs)]
    unnamed x12 -> x26, local copies, waits for them, and re-layouts: 11 us -> 2.71 us
  transfers between devices with their start and end apart: 8 -> 16, of which waited for: 6 -> 11; matrix products, arithmetic and copies ran while one was open for 3% -> 7% of each run, Pallas kernels for 0% -> 0%
where the time goes in v3:
time: 149 us
  starting transfers between devices  75.8 us (51%)
  waiting for transfers between devices  44.3 us (30%)
  matrix products  14.8 us (10%)
  local copies, waits for them, and re-layouts  9.6 us (6%)
  other arithmetic  2.51 us (2%)
  between operations  1.78 us (1%)
    ppermute x10, starting transfers between devices, exchanged_half(): return keep + lax.ppermute(send, axis, pairs)  61 us
    ppermute x10, waiting for transfers between devices, exchanged_half(): return keep + lax.ppermute(send, axis, pairs)  38.4 us
    dot_general x9, matrix products, local(): lax.dot_general(pre_grad, piece, (((0,), (0,)), ((), ())), preferred_elem...  8.64 us
    ppermute x2, starting transfers between devices, padded(): lax.ppermute(lax.slice_in_dim(block, 0, width, axis=dim), axis, backward)  6.28 us
    dot_general x16, matrix products, apply_taps(): jnp.dot(patches[index], kmat[index // 3, index % 3], preferred_element_ty...  5.61 us
    ppermute x2, starting transfers between devices, padded(): lax.ppermute(lax.slice_in_dim(block, block.shape[dim] - width, None, axis...  5.41 us
    ppermute x2, waiting for transfers between devices, padded(): lax.ppermute(lax.slice_in_dim(block, 0, width, axis=dim), axis, backward)  4.68 us
    ppermute x2, starting transfers between devices, passed_along(): return lax.ppermute(x, axis, pairs)  3.16 us
  transfers between devices with their start and end apart: 16, of which 11 were waited for; matrix products, arithmetic and copies ran while one was open for 7% of the time, Pallas kernels for 0%

profile of v3, /device:TPU:56, one launch (start us, length us, event | category | flops | bytes accessed | tf_op | source)
XLA Modules:
  0.0 148.7 jit_solution(9564341883273546488)
XLA Ops:
  0.6 1.9 %collective-permute-start = (bf16[2,2,128,128]{3,2,1,0:T(8,128)(2,1)}, bf16[2,2,128,128]{3,2,1,0:T(8,128)(2,1)S(1)}, u32[]{:S(2)}, u32[]{:S(2)}) collective-permute-start(bf16[2,2,128,128]{3,2,1,0:T(8,128)(2,1)} %param.3), channel_id=1, source_target_pairs={{0,128},{128,256},{256,384},{384,512},{512,640},{640,768},{768,896... | collective-permute-start | bytes 393224 | tf_op jit(solution)/shard_map/ppermute | solution.py:10
  2.5 1.2 collective-permute-done
  3.7 0.9 constant_dynamic-update-slice_fusion
  4.7 3.5 %collective-permute-start.1 = (bf16[4,1,128,128]{3,2,1,0:T(8,128)(2,1)S(1)}, bf16[4,1,128,128]{3,2,1,0:T(8,128)(2,1)S(1)}, u32[]{:S(2)}, u32[]{:S(2)}) collective-permute-start(bf16[4,1,128,128]{3,2,1,0:T(8,128)(2,1)S(1)} %get-tuple-element.60), channel_id=1, source_target_pairs={{0,1},{1,2},{2,3},{3,4},{4,5},{5,6},{6,7},{7,8},{8,9},{9,10},{10,1... | collective-permute-start | bytes 393224 | tf_op jit(solution)/shard_map/ppermute | solution.py:18
  8.2 2.4 %collective-permute-start.2 = (bf16[4,1,128,128]{3,2,1,0:T(8,128)(2,1)S(1)}, bf16[4,1,128,128]{3,2,1,0:T(8,128)(2,1)S(1)}, u32[]{:S(2)}, u32[]{:S(2)}) collective-permute-start(bf16[4,1,128,128]{3,2,1,0:T(8,128)(2,1)S(1)} %get-tuple-element.61), channel_id=1, source_target_pairs={{1,0},{2,1},{3,2},{4,3},{5,4},{6,5},{7,6},{8,7},{9,8},{10,9},{11,1... | collective-permute-start | bytes 393224 | tf_op jit(solution)/shard_map/ppermute | solution.py:21
  10.8 1.4 copy.6
  12.5 4.7 %collective-permute-done.2 = bf16[4,1,128,128]{3,2,1,0:T(8,128)(2,1)S(1)} collective-permute-done((bf16[4,1,128,128]{3,2,1,0:T(8,128)(2,1)S(1)}, bf16[4,1,128,128]{3,2,1,0:T(8,128)(2,1)S(1)}, u32[]{:S(2)}, u32[]{:S(2)}) %collective-permute-start.2) | collective-permute-done | bytes 131104 | tf_op jit(solution)/shard_map/ppermute | solution.py:21
  17.3 0.5 fusion.29
  18.0 0.9 copy-done.1
  21.8 1.0 fusion.15
  22.8 0.9 convolution_dynamic-update-slice_fusion.8
  23.7 1.0 convolution_dynamic-update-slice_fusion.7
  24.7 1.0 convolution_dynamic-update-slice_fusion.6
  25.7 1.0 convolution_dynamic-update-slice_fusion.5
  26.7 0.9 convolution_dynamic-update-slice_fusion.4
  27.6 0.9 convolution_dynamic-update-slice_fusion.3
  28.6 0.9 convolution_dynamic-update-slice_fusion.2
  29.5 1.0 convolution_dynamic-update-slice_fusion.1
  30.5 1.3 collective-permute-start.3
  31.8 1.0 convolution_dynamic-update-slice_fusion
  32.7 2.2 %copy.7 = f32[128,3456]{0,1:T(8,128)S(1)} copy(f32[128,3456]{1,0:T(8,128)} %convolution_dynamic-update-slice_fusion) | data formatting | bytes 3538944 | tf_op jit(solution)/shard_map/concatenate | solution.py:109
  35.0 1.9 %collective-permute-start.4 = (bf16[4,1,128,128]{3,2,1,0:T(8,128)(2,1)S(1)}, bf16[4,1,128,128]{3,2,1,0:T(8,128)(2,1)S(1)}, u32[]{:S(2)}, u32[]{:S(2)}) collective-permute-start(bf16[4,1,128,128]{3,2,1,0:T(8,128)(2,1)S(1)} %get-tuple-element.51), channel_id=1, source_target_pairs={{0,1},{1,2},{2,3},{3,4},{4,5},{5,6},{6,7},{7,8},{8,9},{9,10},{10,1... | collective-permute-start | bytes 393224 | tf_op jit(solution)/shard_map/ppermute | solution.py:18
  36.9 3.9 %collective-permute-start.5 = (bf16[4,1,128,128]{3,2,1,0:T(8,128)(2,1)S(1)}, bf16[4,1,128,128]{3,2,1,0:T(8,128)(2,1)S(1)}, u32[]{:S(2)}, u32[]{:S(2)}) collective-permute-start(bf16[4,1,128,128]{3,2,1,0:T(8,128)(2,1)S(1)} %get-tuple-element.52), channel_id=1, source_target_pairs={{1,0},{2,1},{3,2},{4,3},{5,4},{6,5},{7,6},{8,7},{9,8},{10,9},{11,1... | collective-permute-start | bytes 393224 | tf_op jit(solution)/shard_map/ppermute | solution.py:21
  40.9 6.6 %collective-permute-start.6 = (f32[128,2,2,1,432]{0,4,3,2,1:T(8,128)S(1)}, f32[128,2,2,1,432]{0,4,3,2,1:T(8,128)S(1)}, u32[]{:S(2)}, u32[]{:S(2)}) collective-permute-start(f32[128,2,2,1,432]{0,4,3,2,1:T(8,128)S(1)} %constant_dynamic-slice_fusion.11), channel_id=1, source_target_pairs={{0,128},{128,0},{256,384},{384,256},{512,640},{640,512},{768,896},... | collective-permute-start | bytes 2654216 | tf_op jit(solution)/shard_map/ppermute | solution.py:56
  47.6 0.8 fusion.30
  48.5 1.1 fusion.28
  49.7 0.7 fusion.31
  51.4 7.2 %collective-permute-start.7 = (f32[128,2,1,1,432]{0,4,3,2,1:T(8,128)S(1)}, f32[128,2,1,1,432]{0,4,3,2,1:T(8,128)S(1)}, u32[]{:S(2)}, u32[]{:S(2)}) collective-permute-start(f32[128,2,1,1,432]{0,4,3,2,1:T(8,128)S(1)} %constant_dynamic-slice_fusion.10), channel_id=1, source_target_pairs={{0,256},{128,384},{256,0},{384,128},{512,768},{640,896},{768,512},... | collective-permute-start | bytes 1327112 | tf_op jit(solution)/shard_map/ppermute | solution.py:56
  59.1 9.9 %collective-permute-done.7 = f32[128,2,1,1,432]{0,4,3,2,1:T(8,128)S(1)} collective-permute-done((f32[128,2,1,1,432]{0,4,3,2,1:T(8,128)S(1)}, f32[128,2,1,1,432]{0,4,3,2,1:T(8,128)S(1)}, u32[]{:S(2)}, u32[]{:S(2)}) %collective-permute-start.7) | collective-permute-done | bytes 442400 | tf_op jit(solution)/shard_map/ppermute | solution.py:56
  69.1 5.0 %collective-permute-start.8 = (f32[128,1,1,1,432]{0,4,3,2,1:T(8,128)S(1)}, f32[128,1,1,1,432]{0,4,3,2,1:T(8,128)S(1)}, u32[]{:S(2)}, u32[]{:S(2)}) collective-permute-start(f32[128,1,1,1,432]{0,4,3,2,1:T(8,128)S(1)} %constant_dynamic-slice_fusion.9), channel_id=1, source_target_pairs={{0,512},{128,640},{256,768},{384,896},{512,0},{640,128},{768,256},... | collective-permute-start | bytes 663560 | tf_op jit(solution)/shard_map/ppermute | solution.py:56
  74.4 5.1 %collective-permute-done.8 = f32[128,1,1,1,432]{0,4,3,2,1:T(8,128)S(1)} collective-permute-done((f32[128,1,1,1,432]{0,4,3,2,1:T(8,128)S(1)}, f32[128,1,1,1,432]{0,4,3,2,1:T(8,128)S(1)}, u32[]{:S(2)}, u32[]{:S(2)}) %collective-permute-start.8) | collective-permute-done | bytes 221216 | tf_op jit(solution)/shard_map/ppermute | solution.py:56
  80.1 1.9 %collective-permute-start.9 = (f32[2,2,2,2,2,2,1,432]{7,6,5,4,3,2,1,0:T(1,128)S(1)}, f32[2,2,2,2,2,2,1,432]{7,6,5,4,3,2,1,0:T(1,128)S(1)}, u32[]{:S(2)}, u32[]{:S(2)}) collective-permute-start(f32[2,2,2,2,2,2,1,432]{7,6,5,4,3,2,1,0:T(1,128)S(1)} %constant_dynamic-slice_fusion.8), channel_id=1, source_target_pairs={{0,1},{1,0},{2,3},{3,2},{4,5},{5,4},{6,7},{7,6},{8,9},{9,8},{10,11... | collective-permute-start | bytes 331784 | tf_op jit(solution)/shard_map/ppermute | solution.py:56
  82.1 4.8 %collective-permute-done.9 = f32[2,2,2,2,2,2,1,432]{7,6,5,4,3,2,1,0:T(1,128)S(1)} collective-permute-done((f32[2,2,2,2,2,2,1,432]{7,6,5,4,3,2,1,0:T(1,128)S(1)}, f32[2,2,2,2,2,2,1,432]{7,6,5,4,3,2,1,0:T(1,128)S(1)}, u32[]{:S(2)}, u32[]{:S(2)}) %collective-permute-start.9) | collective-permute-done | bytes 110624 | tf_op jit(solution)/shard_map/ppermute | solution.py:56
  87.1 4.3 %collective-permute-start.10 = (f32[2,2,2,1,2,2,1,432]{7,6,5,4,3,2,1,0:T(1,128)S(1)}, f32[2,2,2,1,2,2,1,432]{7,6,5,4,3,2,1,0:T(1,128)S(1)}, u32[]{:S(2)}, u32[]{:S(2)}) collective-permute-start(f32[2,2,2,1,2,2,1,432]{7,6,5,4,3,2,1,0:T(1,128)S(1)} %constant_dynamic-slice_fusion.7), channel_id=1, source_target_pairs={{0,8},{1,9},{2,10},{3,11},{4,12},{5,13},{6,14},{7,15},{8,0},{9,1},... | collective-permute-start | bytes 165896 | tf_op jit(solution)/shard_map/ppermute | solution.py:56
  91.4 0.3 convolution_add_fusion.3
  91.7 1.9 %collective-permute-done.10 = f32[2,2,2,1,2,2,1,432]{7,6,5,4,3,2,1,0:T(1,128)S(1)} collective-permute-done((f32[2,2,2,1,2,2,1,432]{7,6,5,4,3,2,1,0:T(1,128)S(1)}, f32[2,2,2,1,2,2,1,432]{7,6,5,4,3,2,1,0:T(1,128)S(1)}, u32[]{:S(2)}, u32[]{:S(2)}) %collective-permute-start.10) | collective-permute-done | bytes 55328 | tf_op jit(solution)/shard_map/ppermute | solution.py:56
  93.7 1.9 %collective-permute-start.11 = (f32[2,2,2,1,2,1,1,432]{7,6,5,4,3,2,1,0:T(1,128)S(1)}, f32[2,2,2,1,2,1,1,432]{7,6,5,4,3,2,1,0:T(1,128)S(1)}, u32[]{:S(2)}, u32[]{:S(2)}) collective-permute-start(f32[2,2,2,1,2,1,1,432]{7,6,5,4,3,2,1,0:T(1,128)S(1)} %constant_dynamic-slice_fusion.6), channel_id=1, source_target_pairs={{0,2},{1,3},{2,0},{3,1},{4,6},{5,7},{6,4},{7,5},{8,10},{9,11},{10,... | collective-permute-start | bytes 82952 | tf_op jit(solution)/shard_map/ppermute | solution.py:56
  95.8 4.7 %collective-permute-done.11 = f32[2,2,2,1,2,1,1,432]{7,6,5,4,3,2,1,0:T(1,128)S(1)} collective-permute-done((f32[2,2,2,1,2,1,1,432]{7,6,5,4,3,2,1,0:T(1,128)S(1)}, f32[2,2,2,1,2,1,1,432]{7,6,5,4,3,2,1,0:T(1,128)S(1)}, u32[]{:S(2)}, u32[]{:S(2)}) %collective-permute-start.11) | collective-permute-done | bytes 27680 | tf_op jit(solution)/shard_map/ppermute | solution.py:56
  100.5 9.7 %collective-permute-start.12 = (f32[2,2,1,1,2,1,1,432]{7,6,5,4,3,2,1,0:T(1,128)S(1)}, f32[2,2,1,1,2,1,1,432]{7,6,5,4,3,2,1,0:T(1,128)S(1)}, u32[]{:S(2)}, u32[]{:S(2)}) collective-permute-start(f32[2,2,1,1,2,1,1,432]{7,6,5,4,3,2,1,0:T(1,128)S(1)} %constant_dynamic-slice_fusion.5), channel_id=1, source_target_pairs={{0,16},{1,17},{2,18},{3,19},{4,20},{5,21},{6,22},{7,23},{8,24},{9,... | collective-permute-start | bytes 41480 | tf_op jit(solution)/shard_map/ppermute | solution.py:56
  110.5 1.4 collective-permute-done.12
  112.0 1.9 %collective-permute-start.13 = (f32[2,2,1,1,1,1,1,432]{7,6,5,4,3,2,1,0:T(1,128)S(1)}, f32[2,2,1,1,1,1,1,432]{7,6,5,4,3,2,1,0:T(1,128)S(1)}, u32[]{:S(2)}, u32[]{:S(2)}) collective-permute-start(f32[2,2,1,1,1,1,1,432]{7,6,5,4,3,2,1,0:T(1,128)S(1)} %constant_dynamic-slice_fusion.4), channel_id=1, source_target_pairs={{0,4},{1,5},{2,6},{3,7},{4,0},{5,1},{6,2},{7,3},{8,12},{9,13},{10,... | collective-permute-start | bytes 20744 | tf_op jit(solution)/shard_map/ppermute | solution.py:56
  114.2 7.3 %collective-permute-done.13 = f32[2,2,1,1,1,1,1,432]{7,6,5,4,3,2,1,0:T(1,128)S(1)} collective-permute-done((f32[2,2,1,1,1,1,1,432]{7,6,5,4,3,2,1,0:T(1,128)S(1)}, f32[2,2,1,1,1,1,1,432]{7,6,5,4,3,2,1,0:T(1,128)S(1)}, u32[]{:S(2)}, u32[]{:S(2)}) %collective-permute-start.13) | collective-permute-done | bytes 6944 | tf_op jit(solution)/shard_map/ppermute | solution.py:56
  121.5 10.9 %collective-permute-start.14 = (f32[2,1,1,1,1,1,1,432]{7,6,5,4,3,2,1,0:T(1,128)S(1)}, f32[2,1,1,1,1,1,1,432]{7,6,5,4,3,2,1,0:T(1,128)S(1)}, u32[]{:S(2)}, u32[]{:S(2)}) collective-permute-start(f32[2,1,1,1,1,1,1,432]{7,6,5,4,3,2,1,0:T(1,128)S(1)} %constant_dynamic-slice_fusion.2), channel_id=1, source_target_pairs={{0,32},{1,33},{2,34},{3,35},{4,36},{5,37},{6,38},{7,39},{8,40},{9,... | collective-permute-start | bytes 10376 | tf_op jit(solution)/shard_map/ppermute | solution.py:56
  132.5 1.5 collective-permute-done.14
  134.0 11.5 %collective-permute-start.15 = (f32[1,1,1,1,1,1,1,432]{7,6,5,4,3,2,1,0:T(1,128)S(1)}, f32[1,1,1,1,1,1,1,432]{7,6,5,4,3,2,1,0:T(1,128)S(1)}, u32[]{:S(2)}, u32[]{:S(2)}) collective-permute-start(f32[1,1,1,1,1,1,1,432]{7,6,5,4,3,2,1,0:T(1,128)S(1)} %constant_dynamic-slice_fusion), channel_id=1, source_target_pairs={{0,64},{1,65},{2,66},{3,67},{4,68},{5,69},{6,70},{7,71},{8,72},{9,... | collective-permute-start | bytes 5192 | tf_op jit(solution)/shard_map/ppermute | solution.py:56
  145.4 0.9 fusion
  146.4 1.8 %collective-permute-done.15 = f32[1,1,1,1,1,1,1,432]{7,6,5,4,3,2,1,0:T(1,128)S(1)} collective-permute-done((f32[1,1,1,1,1,1,1,432]{7,6,5,4,3,2,1,0:T(1,128)S(1)}, f32[1,1,1,1,1,1,1,432]{7,6,5,4,3,2,1,0:T(1,128)S(1)}, u32[]{:S(2)}, u32[]{:S(2)}) %collective-permute-start.15) | collective-permute-done | bytes 1760 | tf_op jit(solution)/shard_map/ppermute | solution.py:56
  148.2 0.6 fusion.26
  (83 shorter events, 7.0 us)
Async XLA Ops:
  0.6 10.2 %copy-start = (bf16[3,3,3,128,128]{4,3,2,1,0:T(8,128)(2,1)S(1)}, bf16[3,3,3,128,128]{4,3,2,1,0:T(8,128)(2,1)}, u32[]{:S(2)}) copy-start(bf16[3,3,3,128,128]{4,3,2,1,0:T(8,128)(2,1)} %param.4) | copy-start | bytes 2654212
  0.6 3.1 %collective-permute-start = (bf16[2,2,128,128]{3,2,1,0:T(8,128)(2,1)}, bf16[2,2,128,128]{3,2,1,0:T(8,128)(2,1)S(1)}, u32[]{:S(2)}, u32[]{:S(2)}) collective-permute-start(bf16[2,2,128,128]{3,2,1,0:T(8,128)(2,1)} %param.3), channel_id=1, source_target_pairs={{0,128},{128,256},{256,384},{384,512},{512,640},{640,768},{768,896... | collective-permute-start | bytes 393224 | tf_op jit(solution)/shard_map/ppermute | solution.py:10
  4.7 7.8 %collective-permute-start.1 = (bf16[4,1,128,128]{3,2,1,0:T(8,128)(2,1)S(1)}, bf16[4,1,128,128]{3,2,1,0:T(8,128)(2,1)S(1)}, u32[]{:S(2)}, u32[]{:S(2)}) collective-permute-start(bf16[4,1,128,128]{3,2,1,0:T(8,128)(2,1)S(1)} %get-tuple-element.60), channel_id=1, source_target_pairs={{0,1},{1,2},{2,3},{3,4},{4,5},{5,6},{6,7},{7,8},{8,9},{9,10},{10,1... | collective-permute-start | bytes 393224 | tf_op jit(solution)/shard_map/ppermute | solution.py:18
  8.2 9.0 %collective-permute-start.2 = (bf16[4,1,128,128]{3,2,1,0:T(8,128)(2,1)S(1)}, bf16[4,1,128,128]{3,2,1,0:T(8,128)(2,1)S(1)}, u32[]{:S(2)}, u32[]{:S(2)}) collective-permute-start(bf16[4,1,128,128]{3,2,1,0:T(8,128)(2,1)S(1)} %get-tuple-element.61), channel_id=1, source_target_pairs={{1,0},{2,1},{3,2},{4,3},{5,4},{6,5},{7,6},{8,7},{9,8},{10,9},{11,1... | collective-permute-start | bytes 393224 | tf_op jit(solution)/shard_map/ppermute | solution.py:21
  17.8 1.2 copy-start.1
  19.9 0.9 copy-start.2
  20.9 0.9 copy-start.11
  30.5 4.4 %collective-permute-start.3 = (bf16[2,2,128,128]{3,2,1,0:T(8,128)(2,1)S(1)}, bf16[2,2,128,128]{3,2,1,0:T(8,128)(2,1)S(1)}, u32[]{:S(2)}, u32[]{:S(2)}) collective-permute-start(bf16[2,2,128,128]{3,2,1,0:T(8,128)(2,1)S(1)} %bitcast.127), channel_id=1, source_target_pairs={{128,0},{256,128},{384,256},{512,384},{640,512},{768,640},{896,768... | collective-permute-start | bytes 393224 | tf_op jit(solution)/shard_map/ppermute | solution.py:10
  35.0 12.6 %collective-permute-start.4 = (bf16[4,1,128,128]{3,2,1,0:T(8,128)(2,1)S(1)}, bf16[4,1,128,128]{3,2,1,0:T(8,128)(2,1)S(1)}, u32[]{:S(2)}, u32[]{:S(2)}) collective-permute-start(bf16[4,1,128,128]{3,2,1,0:T(8,128)(2,1)S(1)} %get-tuple-element.51), channel_id=1, source_target_pairs={{0,1},{1,2},{2,3},{3,4},{4,5},{5,6},{6,7},{7,8},{8,9},{9,10},{10,1... | collective-permute-start | bytes 393224 | tf_op jit(solution)/shard_map/ppermute | solution.py:18
  36.9 10.7 %collective-permute-start.5 = (bf16[4,1,128,128]{3,2,1,0:T(8,128)(2,1)S(1)}, bf16[4,1,128,128]{3,2,1,0:T(8,128)(2,1)S(1)}, u32[]{:S(2)}, u32[]{:S(2)}) collective-permute-start(bf16[4,1,128,128]{3,2,1,0:T(8,128)(2,1)S(1)} %get-tuple-element.52), channel_id=1, source_target_pairs={{1,0},{2,1},{3,2},{4,3},{5,4},{6,5},{7,6},{8,7},{9,8},{10,9},{11,1... | collective-permute-start | bytes 393224 | tf_op jit(solution)/shard_map/ppermute | solution.py:21
  40.9 10.3 %collective-permute-start.6 = (f32[128,2,2,1,432]{0,4,3,2,1:T(8,128)S(1)}, f32[128,2,2,1,432]{0,4,3,2,1:T(8,128)S(1)}, u32[]{:S(2)}, u32[]{:S(2)}) collective-permute-start(f32[128,2,2,1,432]{0,4,3,2,1:T(8,128)S(1)} %constant_dynamic-slice_fusion.11), channel_id=1, source_target_pairs={{0,128},{128,0},{256,384},{384,256},{512,640},{640,512},{768,896},... | collective-permute-start | bytes 2654216 | tf_op jit(solution)/shard_map/ppermute | solution.py:56
  51.4 17.6 %collective-permute-start.7 = (f32[128,2,1,1,432]{0,4,3,2,1:T(8,128)S(1)}, f32[128,2,1,1,432]{0,4,3,2,1:T(8,128)S(1)}, u32[]{:S(2)}, u32[]{:S(2)}) collective-permute-start(f32[128,2,1,1,432]{0,4,3,2,1:T(8,128)S(1)} %constant_dynamic-slice_fusion.10), channel_id=1, source_target_pairs={{0,256},{128,384},{256,0},{384,128},{512,768},{640,896},{768,512},... | collective-permute-start | bytes 1327112 | tf_op jit(solution)/shard_map/ppermute | solution.py:56
  69.1 12.9 %copy-start.6 = (bf16[2,2,128,128]{3,2,1,0:T(8,128)(2,1)S(1)}, bf16[2,2,128,128]{3,2,1,0:T(8,128)(2,1)}, u32[]{:S(2)}) copy-start(bf16[2,2,128,128]{3,2,1,0:T(8,128)(2,1)} %get-tuple-element.8) | copy-start | bytes 393220
  69.1 12.9 %copy-start.7 = (bf16[2,2,128,128]{3,2,1,0:T(8,128)(2,1)S(1)}, bf16[2,2,128,128]{3,2,1,0:T(8,128)(2,1)}, u32[]{:S(2)}) copy-start(bf16[2,2,128,128]{3,2,1,0:T(8,128)(2,1)} %get-tuple-element.9) | copy-start | bytes 393220
  69.1 12.9 %copy-start.10 = (bf16[2,2,128,128]{3,2,1,0:T(8,128)(2,1)S(1)}, bf16[2,2,128,128]{3,2,1,0:T(8,128)(2,1)}, u32[]{:S(2)}) copy-start(bf16[2,2,128,128]{3,2,1,0:T(8,128)(2,1)} %get-tuple-element.40) | copy-start | bytes 393220
  69.1 10.4 %collective-permute-start.8 = (f32[128,1,1,1,432]{0,4,3,2,1:T(8,128)S(1)}, f32[128,1,1,1,432]{0,4,3,2,1:T(8,128)S(1)}, u32[]{:S(2)}, u32[]{:S(2)}) collective-permute-start(f32[128,1,1,1,432]{0,4,3,2,1:T(8,128)S(1)} %constant_dynamic-slice_fusion.9), channel_id=1, source_target_pairs={{0,512},{128,640},{256,768},{384,896},{512,0},{640,128},{768,256},... | collective-permute-start | bytes 663560 | tf_op jit(solution)/shard_map/ppermute | solution.py:56
  79.7 16.0 %copy-start.4 = (bf16[2,2,128,128]{3,2,1,0:T(8,128)(2,1)S(1)}, bf16[2,2,128,128]{3,2,1,0:T(8,128)(2,1)}, u32[]{:S(2)}) copy-start(bf16[2,2,128,128]{3,2,1,0:T(8,128)(2,1)} %get-tuple-element.6) | copy-start | bytes 393220
  79.7 16.0 %copy-start.5 = (bf16[2,2,128,128]{3,2,1,0:T(8,128)(2,1)S(1)}, bf16[2,2,128,128]{3,2,1,0:T(8,128)(2,1)}, u32[]{:S(2)}) copy-start(bf16[2,2,128,128]{3,2,1,0:T(8,128)(2,1)} %get-tuple-element.7) | copy-start | bytes 393220
  79.7 16.0 %copy-start.9 = (bf16[2,2,128,128]{3,2,1,0:T(8,128)(2,1)S(1)}, bf16[2,2,128,128]{3,2,1,0:T(8,128)(2,1)}, u32[]{:S(2)}) copy-start(bf16[2,2,128,128]{3,2,1,0:T(8,128)(2,1)} %get-tuple-element.42) | copy-start | bytes 393220
  80.1 6.9 %collective-permute-start.9 = (f32[2,2,2,2,2,2,1,432]{7,6,5,4,3,2,1,0:T(1,128)S(1)}, f32[2,2,2,2,2,2,1,432]{7,6,5,4,3,2,1,0:T(1,128)S(1)}, u32[]{:S(2)}, u32[]{:S(2)}) collective-permute-start(f32[2,2,2,2,2,2,1,432]{7,6,5,4,3,2,1,0:T(1,128)S(1)} %constant_dynamic-slice_fusion.8), channel_id=1, source_target_pairs={{0,1},{1,0},{2,3},{3,2},{4,5},{5,4},{6,7},{7,6},{8,9},{9,8},{10,11... | collective-permute-start | bytes 331784 | tf_op jit(solution)/shard_map/ppermute | solution.py:56
  87.1 6.5 %collective-permute-start.10 = (f32[2,2,2,1,2,2,1,432]{7,6,5,4,3,2,1,0:T(1,128)S(1)}, f32[2,2,2,1,2,2,1,432]{7,6,5,4,3,2,1,0:T(1,128)S(1)}, u32[]{:S(2)}, u32[]{:S(2)}) collective-permute-start(f32[2,2,2,1,2,2,1,432]{7,6,5,4,3,2,1,0:T(1,128)S(1)} %constant_dynamic-slice_fusion.7), channel_id=1, source_target_pairs={{0,8},{1,9},{2,10},{3,11},{4,12},{5,13},{6,14},{7,15},{8,0},{9,1},... | collective-permute-start | bytes 165896 | tf_op jit(solution)/shard_map/ppermute | solution.py:56
  91.7 40.7 %copy-start.3 = (bf16[2,2,128,128]{3,2,1,0:T(8,128)(2,1)S(1)}, bf16[2,2,128,128]{3,2,1,0:T(8,128)(2,1)}, u32[]{:S(2)}) copy-start(bf16[2,2,128,128]{3,2,1,0:T(8,128)(2,1)} %get-tuple-element.20) | copy-start | bytes 393220
  91.7 40.7 %copy-start.8 = (bf16[2,2,128,128]{3,2,1,0:T(8,128)(2,1)S(1)}, bf16[2,2,128,128]{3,2,1,0:T(8,128)(2,1)}, u32[]{:S(2)}) copy-start(bf16[2,2,128,128]{3,2,1,0:T(8,128)(2,1)} %get-tuple-element.39) | copy-start | bytes 393220
  93.7 6.7 %collective-permute-start.11 = (f32[2,2,2,1,2,1,1,432]{7,6,5,4,3,2,1,0:T(1,128)S(1)}, f32[2,2,2,1,2,1,1,432]{7,6,5,4,3,2,1,0:T(1,128)S(1)}, u32[]{:S(2)}, u32[]{:S(2)}) collective-permute-start(f32[2,2,2,1,2,1,1,432]{7,6,5,4,3,2,1,0:T(1,128)S(1)} %constant_dynamic-slice_fusion.6), channel_id=1, source_target_pairs={{0,2},{1,3},{2,0},{3,1},{4,6},{5,7},{6,4},{7,5},{8,10},{9,11},{10,... | collective-permute-start | bytes 82952 | tf_op jit(solution)/shard_map/ppermute | solution.py:56
  100.5 11.4 %collective-permute-start.12 = (f32[2,2,1,1,2,1,1,432]{7,6,5,4,3,2,1,0:T(1,128)S(1)}, f32[2,2,1,1,2,1,1,432]{7,6,5,4,3,2,1,0:T(1,128)S(1)}, u32[]{:S(2)}, u32[]{:S(2)}) collective-permute-start(f32[2,2,1,1,2,1,1,432]{7,6,5,4,3,2,1,0:T(1,128)S(1)} %constant_dynamic-slice_fusion.5), channel_id=1, source_target_pairs={{0,16},{1,17},{2,18},{3,19},{4,20},{5,21},{6,22},{7,23},{8,24},{9,... | collective-permute-start | bytes 41480 | tf_op jit(solution)/shard_map/ppermute | solution.py:56
  112.0 9.5 %collective-permute-start.13 = (f32[2,2,1,1,1,1,1,432]{7,6,5,4,3,2,1,0:T(1,128)S(1)}, f32[2,2,1,1,1,1,1,432]{7,6,5,4,3,2,1,0:T(1,128)S(1)}, u32[]{:S(2)}, u32[]{:S(2)}) collective-permute-start(f32[2,2,1,1,1,1,1,432]{7,6,5,4,3,2,1,0:T(1,128)S(1)} %constant_dynamic-slice_fusion.4), channel_id=1, source_target_pairs={{0,4},{1,5},{2,6},{3,7},{4,0},{5,1},{6,2},{7,3},{8,12},{9,13},{10,... | collective-permute-start | bytes 20744 | tf_op jit(solution)/shard_map/ppermute | solution.py:56
  121.5 12.5 %collective-permute-start.14 = (f32[2,1,1,1,1,1,1,432]{7,6,5,4,3,2,1,0:T(1,128)S(1)}, f32[2,1,1,1,1,1,1,432]{7,6,5,4,3,2,1,0:T(1,128)S(1)}, u32[]{:S(2)}, u32[]{:S(2)}) collective-permute-start(f32[2,1,1,1,1,1,1,432]{7,6,5,4,3,2,1,0:T(1,128)S(1)} %constant_dynamic-slice_fusion.2), channel_id=1, source_target_pairs={{0,32},{1,33},{2,34},{3,35},{4,36},{5,37},{6,38},{7,39},{8,40},{9,... | collective-permute-start | bytes 10376 | tf_op jit(solution)/shard_map/ppermute | solution.py:56
  134.0 14.2 %collective-permute-start.15 = (f32[1,1,1,1,1,1,1,432]{7,6,5,4,3,2,1,0:T(1,128)S(1)}, f32[1,1,1,1,1,1,1,432]{7,6,5,4,3,2,1,0:T(1,128)S(1)}, u32[]{:S(2)}, u32[]{:S(2)}) collective-permute-start(f32[1,1,1,1,1,1,1,432]{7,6,5,4,3,2,1,0:T(1,128)S(1)} %constant_dynamic-slice_fusion), channel_id=1, source_target_pairs={{0,64},{1,65},{2,66},{3,67},{4,68},{5,69},{6,70},{7,71},{8,72},{9,... | collective-permute-start | bytes 5192 | tf_op jit(solution)/shard_map/ppermute | solution.py:56

commit v4 on v3

--- a/solution.py
+++ b/solution.py
@@ -78,6 +78,15 @@
     return x.reshape(1, block)
 
 
+def exchanged_scatter(partial_grad):
+    outs, cols = partial_grad.shape
+    parts = lax.axis_size("tm")
+    x = partial_grad.reshape(outs, parts, cols // parts)
+    x = lax.all_to_all(x, "tm", 1, 1).sum(axis=1)
+    x = lax.all_to_all(x, "rows", 0, 0).sum(axis=0)
+    return x.reshape(1, -1)
+
+
 def local(video, kernel, cotangent):
     frames, height, width, chans = video.shape
     forward_mat = kernel.reshape(3, 3, 3 * chans, chans)
@@ -107,7 +116,7 @@
         for piece in patches
     ]
     partial_grad = jnp.concatenate(blocks, axis=1)
-    kernel_grad = halving_scatter(partial_grad)
+    kernel_grad = exchanged_scatter(partial_grad)
     return (activated, input_grad, kernel_grad)
 
 

time: 149 us -> 119 us (0.80)
  starting transfers between devices: 75.8 us -> 47.5 us
  matrix products: 14.8 us -> 9.12 us
  waiting for transfers between devices: 44.3 us -> 46.1 us
  other arithmetic: 2.51 us -> 4.29 us
    ppermute x10 -> x0, starting transfers between devices: 61 us -> none  [exchanged_half(): return keep + lax.ppermute(send, axis, pairs)]
    ppermute x10 -> x0, waiting for transfers between devices: 38.4 us -> none  [exchanged_half(): return keep + lax.ppermute(send, axis, pairs)]
    all_to_all x0 -> x2, waiting for transfers between devices: none -> 37.8 us  [the longest x1 19.6 us: exchanged_scatter(): x = lax.all_to_all(x, 'rows', 0, 0).sum(axis=0)]
    all_to_all x0 -> x2, starting transfers between devices: none -> 32.8 us  [the longest x1 24.2 us: exchanged_scatter(): x = lax.all_to_all(x, 'rows', 0, 0).sum(axis=0)]
    dot_general x9, matrix products: 8.64 us -> 2.27 us  [local(): lax.dot_general(pre_grad, piece, (((0,), (0,)), ((), ())), preferred_elem...]
    ppermute x2, waiting for transfers between devices: 1.17 us -> 3.76 us  [passed_along(): return lax.ppermute(x, axis, pairs)]
    concatenate x11, other arithmetic: 0.93 us -> 2.93 us  [make_patches(): jnp.concatenate(parts, axis=-1).reshape(frames * height * width, 3 * chans)]
    unnamed x26 -> x12, local copies, waits for them, and re-layouts: 2.71 us -> 3.29 us
  transfers between devices with their start and end apart: 16 -> 8, of which waited for: 11 -> 5; matrix products, arithmetic and copies ran while one was open for 7% -> 11% of each run, Pallas kernels for 0% -> 0%
where the time goes in v4:
time: 119 us; the launch traced here: 118 us
  starting transfers between devices  47.5 us (40%)
  waiting for transfers between devices  46.1 us (39%)
  local copies, waits for them, and re-layouts  9.9 us (8%)
  matrix products  9.12 us (8%)
  other arithmetic  4.29 us (4%)
    all_to_all x1, starting transfers between devices, exchanged_scatter(): x = lax.all_to_all(x, 'rows', 0, 0).sum(axis=0)  24.2 us
    all_to_all x1, waiting for transfers between devices, exchanged_scatter(): x = lax.all_to_all(x, 'rows', 0, 0).sum(axis=0)  19.6 us
    all_to_all x1, waiting for transfers between devices, exchanged_scatter(): x = lax.all_to_all(x, 'tm', 1, 1).sum(axis=1)  18.2 us
    all_to_all x1, starting transfers between devices, exchanged_scatter(): x = lax.all_to_all(x, 'tm', 1, 1).sum(axis=1)  8.63 us
    dot_general x16, matrix products, apply_taps(): jnp.dot(patches[index], kmat[index // 3, index % 3], preferred_element_ty...  6.33 us
    ppermute x2, starting transfers between devices, padded(): lax.ppermute(lax.slice_in_dim(block, 0, width, axis=dim), axis, backward)  6.22 us
    ppermute x2, starting transfers between devices, padded(): lax.ppermute(lax.slice_in_dim(block, block.shape[dim] - width, None, axis...  5.47 us
    ppermute x2, waiting for transfers between devices, padded(): lax.ppermute(lax.slice_in_dim(block, 0, width, axis=dim), axis, backward)  4.5 us
  transfers between devices with their start and end apart: 8, of which 5 were waited for; matrix products, arithmetic and copies ran while one was open for 11% of the time, Pallas kernels for 0%

profile of v4, /device:TPU:56, one launch (start us, length us, event | category | flops | bytes accessed | tf_op | source)
XLA Modules:
  0.0 118.0 jit_solution(6261687056100136320)
XLA Ops:
  0.6 1.7 %collective-permute-start = (bf16[2,2,128,128]{3,2,1,0:T(8,128)(2,1)}, bf16[2,2,128,128]{3,2,1,0:T(8,128)(2,1)S(1)}, u32[]{:S(2)}, u32[]{:S(2)}) collective-permute-start(bf16[2,2,128,128]{3,2,1,0:T(8,128)(2,1)} %param.3), channel_id=1, source_target_pairs={{0,128},{128,256},{256,384},{384,512},{512,640},{640,768},{768,896... | collective-permute-start | bytes 393224 | tf_op jit(solution)/shard_map/ppermute | solution.py:10
  2.4 1.2 collective-permute-done
  3.6 0.9 constant_dynamic-update-slice_fusion
  4.5 3.5 %collective-permute-start.1 = (bf16[4,1,128,128]{3,2,1,0:T(8,128)(2,1)S(1)}, bf16[4,1,128,128]{3,2,1,0:T(8,128)(2,1)S(1)}, u32[]{:S(2)}, u32[]{:S(2)}) collective-permute-start(bf16[4,1,128,128]{3,2,1,0:T(8,128)(2,1)S(1)} %get-tuple-element.60), channel_id=1, source_target_pairs={{0,1},{1,2},{2,3},{3,4},{4,5},{5,6},{6,7},{7,8},{8,9},{9,10},{10,1... | collective-permute-start | bytes 393224 | tf_op jit(solution)/shard_map/ppermute | solution.py:18
  8.0 2.4 %collective-permute-start.2 = (bf16[4,1,128,128]{3,2,1,0:T(8,128)(2,1)S(1)}, bf16[4,1,128,128]{3,2,1,0:T(8,128)(2,1)S(1)}, u32[]{:S(2)}, u32[]{:S(2)}) collective-permute-start(bf16[4,1,128,128]{3,2,1,0:T(8,128)(2,1)S(1)} %get-tuple-element.61), channel_id=1, source_target_pairs={{1,0},{2,1},{3,2},{4,3},{5,4},{6,5},{7,6},{8,7},{9,8},{10,9},{11,1... | collective-permute-start | bytes 393224 | tf_op jit(solution)/shard_map/ppermute | solution.py:21
  10.4 2.0 %copy.8 = bf16[3,3,3,128,128]{3,4,2,1,0:T(8,128)(2,1)S(1)} copy(bf16[3,3,3,128,128]{4,3,2,1,0:T(8,128)(2,1)} %param.4) | data formatting | bytes 1769472 | tf_op args[1]
  12.5 4.5 %collective-permute-done.2 = bf16[4,1,128,128]{3,2,1,0:T(8,128)(2,1)S(1)} collective-permute-done((bf16[4,1,128,128]{3,2,1,0:T(8,128)(2,1)S(1)}, bf16[4,1,128,128]{3,2,1,0:T(8,128)(2,1)S(1)}, u32[]{:S(2)}, u32[]{:S(2)}) %collective-permute-start.2) | collective-permute-done | bytes 131104 | tf_op jit(solution)/shard_map/ppermute | solution.py:21
  17.2 0.5 fusion.26
  17.9 0.9 copy-done
  18.8 0.3 fusion.23
  19.2 0.3 convolution_add_fusion.15
  19.5 0.3 convolution_add_fusion.14
  19.8 0.3 convolution_add_fusion.13
  20.1 0.3 convolution_add_fusion.12
  20.7 0.3 convolution_add_fusion.11
  21.0 0.3 convolution_add_fusion.10
  21.3 0.3 convolution_add_fusion.9
  21.6 1.0 fusion.15
  22.9 0.3 convolution_dynamic-update-slice_fusion.7
  23.2 0.3 convolution_dynamic-update-slice_fusion.6
  23.4 0.3 convolution_dynamic-update-slice_fusion.5
  23.7 0.3 convolution_dynamic-update-slice_fusion.4
  23.9 0.3 convolution_dynamic-update-slice_fusion.3
  24.4 1.3 %collective-permute-start.3 = (bf16[2,2,128,128]{3,2,1,0:T(8,128)(2,1)S(1)}, bf16[2,2,128,128]{3,2,1,0:T(8,128)(2,1)S(1)}, u32[]{:S(2)}, u32[]{:S(2)}) collective-permute-start(bf16[2,2,128,128]{3,2,1,0:T(8,128)(2,1)S(1)} %bitcast.123), channel_id=1, source_target_pairs={{128,0},{256,128},{384,256},{512,384},{640,512},{768,640},{896,768... | collective-permute-start | bytes 393224 | tf_op jit(solution)/shard_map/ppermute | solution.py:10
  26.0 2.6 %collective-permute-done.3 = bf16[2,2,128,128]{3,2,1,0:T(8,128)(2,1)S(1)} collective-permute-done((bf16[2,2,128,128]{3,2,1,0:T(8,128)(2,1)S(1)}, bf16[2,2,128,128]{3,2,1,0:T(8,128)(2,1)S(1)}, u32[]{:S(2)}, u32[]{:S(2)}) %collective-permute-start.3) | collective-permute-done | bytes 131104 | tf_op jit(solution)/shard_map/ppermute | solution.py:10
  28.6 2.0 %collective-permute-start.4 = (bf16[4,1,128,128]{3,2,1,0:T(8,128)(2,1)S(1)}, bf16[4,1,128,128]{3,2,1,0:T(8,128)(2,1)S(1)}, u32[]{:S(2)}, u32[]{:S(2)}) collective-permute-start(bf16[4,1,128,128]{3,2,1,0:T(8,128)(2,1)S(1)} %get-tuple-element.51), channel_id=1, source_target_pairs={{0,1},{1,2},{2,3},{3,4},{4,5},{5,6},{6,7},{7,8},{8,9},{9,10},{10,1... | collective-permute-start | bytes 393224 | tf_op jit(solution)/shard_map/ppermute | solution.py:18
  30.6 3.9 %collective-permute-start.5 = (bf16[4,1,128,128]{3,2,1,0:T(8,128)(2,1)S(1)}, bf16[4,1,128,128]{3,2,1,0:T(8,128)(2,1)S(1)}, u32[]{:S(2)}, u32[]{:S(2)}) collective-permute-start(bf16[4,1,128,128]{3,2,1,0:T(8,128)(2,1)S(1)} %get-tuple-element.52), channel_id=1, source_target_pairs={{1,0},{2,1},{3,2},{4,3},{5,4},{6,5},{7,6},{8,7},{9,8},{10,9},{11,1... | collective-permute-start | bytes 393224 | tf_op jit(solution)/shard_map/ppermute | solution.py:21
  34.7 1.7 %copy.9 = f32[128,3456]{0,1:T(8,128)} copy(f32[128,3456]{1,0:T(8,128)S(1)} %convolution_dynamic-update-slice_fusion) | data formatting | bytes 3538944 | tf_op jit(solution)/shard_map/concatenate | solution.py:118
  36.5 8.6 %all-to-all-start = ((f32[128,8,432]{0,2,1:T(8,128)}), f32[128,8,432]{0,2,1:T(8,128)S(1)}, u32[]{:S(2)}, u32[]{:S(2)}) async-start(f32[128,8,432]{0,2,1:T(8,128)} %bitcast.128), calls=%async_computation | async-start | bytes 3538944 | tf_op jit(solution)/shard_map/all_to_all | solution.py:85
  45.2 0.7 fusion.27
  46.1 1.1 fusion.25
  47.2 0.7 fusion.28
  48.3 0.3 fusion.22
  48.5 0.3 convolution_add_fusion.7
  48.8 0.3 convolution_add_fusion.6
  49.1 0.3 convolution_add_fusion.5
  49.3 0.3 convolution_add_fusion.4
  49.6 1.0 convolution_add_fusion.3
  50.6 18.2 %all-to-all-done = f32[128,8,432]{0,2,1:T(8,128)S(1)} async-done(((f32[128,8,432]{0,2,1:T(8,128)}), f32[128,8,432]{0,2,1:T(8,128)S(1)}, u32[]{:S(2)}, u32[]{:S(2)}) %all-to-all-start) | async-done | bytes 1769504 | tf_op jit(solution)/shard_map/all_to_all | solution.py:85
  68.9 0.8 copy.10
  69.7 24.2 %all-to-all-start.1 = ((f32[128,1,432]{2,1,0:T(1,128)}), f32[128,1,432]{2,1,0:T(1,128)S(1)}, u32[]{:S(2)}, u32[]{:S(2)}) async-start(f32[128,1,432]{2,1,0:T(1,128)} %copy.10), calls=%async_computation.1 | async-start | bytes 524288 | tf_op jit(solution)/shard_map/all_to_all | solution.py:86
  93.9 1.1 pad_maximum_fusion.17
  95.0 1.0 pad_maximum_fusion.15
  96.0 0.3 convolution_add_fusion.2
  96.3 0.3 convolution_add_fusion.1
  96.6 0.9 fusion
  97.5 19.6 %all-to-all-done.1 = f32[128,1,432]{2,1,0:T(1,128)S(1)} async-done(((f32[128,1,432]{2,1,0:T(1,128)}), f32[128,1,432]{2,1,0:T(1,128)S(1)}, u32[]{:S(2)}, u32[]{:S(2)}) %all-to-all-start.1) | async-done | bytes 221216 | tf_op jit(solution)/shard_map/all_to_all | solution.py:86
  117.2 0.8 reduce_sum.19
  (34 shorter events, 2.8 us)
Async XLA Ops:
  0.6 2.9 %collective-permute-start = (bf16[2,2,128,128]{3,2,1,0:T(8,128)(2,1)}, bf16[2,2,128,128]{3,2,1,0:T(8,128)(2,1)S(1)}, u32[]{:S(2)}, u32[]{:S(2)}) collective-permute-start(bf16[2,2,128,128]{3,2,1,0:T(8,128)(2,1)} %param.3), channel_id=1, source_target_pairs={{0,128},{128,256},{256,384},{384,512},{512,640},{640,768},{768,896... | collective-permute-start | bytes 393224 | tf_op jit(solution)/shard_map/ppermute | solution.py:10
  4.5 8.0 %collective-permute-start.1 = (bf16[4,1,128,128]{3,2,1,0:T(8,128)(2,1)S(1)}, bf16[4,1,128,128]{3,2,1,0:T(8,128)(2,1)S(1)}, u32[]{:S(2)}, u32[]{:S(2)}) collective-permute-start(bf16[4,1,128,128]{3,2,1,0:T(8,128)(2,1)S(1)} %get-tuple-element.60), channel_id=1, source_target_pairs={{0,1},{1,2},{2,3},{3,4},{4,5},{5,6},{6,7},{7,8},{8,9},{9,10},{10,1... | collective-permute-start | bytes 393224 | tf_op jit(solution)/shard_map/ppermute | solution.py:18
  8.0 9.0 %collective-permute-start.2 = (bf16[4,1,128,128]{3,2,1,0:T(8,128)(2,1)S(1)}, bf16[4,1,128,128]{3,2,1,0:T(8,128)(2,1)S(1)}, u32[]{:S(2)}, u32[]{:S(2)}) collective-permute-start(bf16[4,1,128,128]{3,2,1,0:T(8,128)(2,1)S(1)} %get-tuple-element.61), channel_id=1, source_target_pairs={{1,0},{2,1},{3,2},{4,3},{5,4},{6,5},{7,6},{8,7},{9,8},{10,9},{11,1... | collective-permute-start | bytes 393224 | tf_op jit(solution)/shard_map/ppermute | solution.py:21
  17.6 1.2 copy-start
  19.7 0.9 copy-start.2
  20.7 0.9 copy-start.4
  24.4 4.1 %collective-permute-start.3 = (bf16[2,2,128,128]{3,2,1,0:T(8,128)(2,1)S(1)}, bf16[2,2,128,128]{3,2,1,0:T(8,128)(2,1)S(1)}, u32[]{:S(2)}, u32[]{:S(2)}) collective-permute-start(bf16[2,2,128,128]{3,2,1,0:T(8,128)(2,1)S(1)} %bitcast.123), channel_id=1, source_target_pairs={{128,0},{256,128},{384,256},{512,384},{640,512},{768,640},{896,768... | collective-permute-start | bytes 393224 | tf_op jit(solution)/shard_map/ppermute | solution.py:10
  28.6 16.5 %collective-permute-start.4 = (bf16[4,1,128,128]{3,2,1,0:T(8,128)(2,1)S(1)}, bf16[4,1,128,128]{3,2,1,0:T(8,128)(2,1)S(1)}, u32[]{:S(2)}, u32[]{:S(2)}) collective-permute-start(bf16[4,1,128,128]{3,2,1,0:T(8,128)(2,1)S(1)} %get-tuple-element.51), channel_id=1, source_target_pairs={{0,1},{1,2},{2,3},{3,4},{4,5},{5,6},{6,7},{7,8},{8,9},{9,10},{10,1... | collective-permute-start | bytes 393224 | tf_op jit(solution)/shard_map/ppermute | solution.py:18
  30.6 14.5 %collective-permute-start.5 = (bf16[4,1,128,128]{3,2,1,0:T(8,128)(2,1)S(1)}, bf16[4,1,128,128]{3,2,1,0:T(8,128)(2,1)S(1)}, u32[]{:S(2)}, u32[]{:S(2)}) collective-permute-start(bf16[4,1,128,128]{3,2,1,0:T(8,128)(2,1)S(1)} %get-tuple-element.52), channel_id=1, source_target_pairs={{1,0},{2,1},{3,2},{4,3},{5,4},{6,5},{7,6},{8,7},{9,8},{10,9},{11,1... | collective-permute-start | bytes 393224 | tf_op jit(solution)/shard_map/ppermute | solution.py:21
  36.5 32.3 %all-to-all-start = ((f32[128,8,432]{0,2,1:T(8,128)}), f32[128,8,432]{0,2,1:T(8,128)S(1)}, u32[]{:S(2)}, u32[]{:S(2)}) async-start(f32[128,8,432]{0,2,1:T(8,128)} %bitcast.128), calls=%async_computation | async-start | bytes 3538944 | tf_op jit(solution)/shard_map/all_to_all | solution.py:85
  50.6 44.4 %copy-start.3 = (bf16[2,2,128,128]{3,2,1,0:T(8,128)(2,1)S(1)}, bf16[2,2,128,128]{3,2,1,0:T(8,128)(2,1)}, u32[]{:S(2)}) copy-start(bf16[2,2,128,128]{3,2,1,0:T(8,128)(2,1)} %get-tuple-element.6) | copy-start | bytes 393220
  68.9 27.1 %copy-start.1 = (f32[512,128]{1,0:T(8,128)S(1)}, f32[512,128]{1,0:T(8,128)}, u32[]{:S(2)}) copy-start(f32[512,128]{1,0:T(8,128)} %convolution_add_fusion.3) | copy-start | bytes 786436
  69.7 47.4 %all-to-all-start.1 = ((f32[128,1,432]{2,1,0:T(1,128)}), f32[128,1,432]{2,1,0:T(1,128)S(1)}, u32[]{:S(2)}, u32[]{:S(2)}) async-start(f32[128,1,432]{2,1,0:T(1,128)} %copy.10), calls=%async_computation.1 | async-start | bytes 524288 | tf_op jit(solution)/shard_map/all_to_all | solution.py:86

commit v5 on v4

--- a/solution.py
+++ b/solution.py
@@ -1,7 +1,9 @@
 import jax
 import jax.numpy as jnp
 from jax import lax
-from jax.sharding import PartitionSpec as P
+from jax.sharding import Mesh, PartitionSpec as P
+
+ROWS = ("rz", "ry")
 
 
 def passed_along(x, axis, by):
@@ -81,9 +83,12 @@
 def exchanged_scatter(partial_grad):
     outs, cols = partial_grad.shape
     parts = lax.axis_size("tm")
+    inner = lax.axis_size("ry")
     x = partial_grad.reshape(outs, parts, cols // parts)
     x = lax.all_to_all(x, "tm", 1, 1).sum(axis=1)
-    x = lax.all_to_all(x, "rows", 0, 0).sum(axis=0)
+    x = x.reshape(outs // inner, inner, -1)
+    x = lax.all_to_all(x, "ry", 1, 1).sum(axis=1)
+    x = lax.all_to_all(x, "rz", 0, 0).sum(axis=0)
     return x.reshape(1, -1)
 
 
@@ -91,7 +96,7 @@
     frames, height, width, chans = video.shape
     forward_mat = kernel.reshape(3, 3, 3 * chans, chans)
     earlier = passed_along(video, "tm", 1)
-    extended = padded(jnp.concatenate([earlier, video], axis=0), (("rows", 1),), 1)
+    extended = padded(jnp.concatenate([earlier, video], axis=0), ((ROWS, 1),), 1)
     patches = make_patches(extended)
     pre = apply_taps(patches, forward_mat)
     sig = 1.0 / (1.0 + jnp.exp(-pre))
@@ -100,7 +105,7 @@
     pre_grad = (grad_flat * sig * (1.0 + pre * (1.0 - sig))).astype(jnp.bfloat16)
     pre_grid = pre_grad.reshape(frames, height, width, chans)
     later = passed_along(pre_grid, "tm", -1)
-    grad_ext = padded(jnp.concatenate([pre_grid, later], axis=0), (("rows", 1),), 1)
+    grad_ext = padded(jnp.concatenate([pre_grid, later], axis=0), ((ROWS, 1),), 1)
     flipped = jnp.transpose(kernel[::-1, ::-1, ::-1], (0, 1, 2, 4, 3)).reshape(
         3, 3, 3 * chans, chans
     )
@@ -121,6 +126,9 @@
 
 
 def solution(mesh):
-    in_specs = (P("tm", "rows", None, None), P(), P("tm", "rows", None, None))
-    out_specs = (P("tm", "rows", None, None), P("tm", "rows", None, None), P("rows", "tm"))
-    return jax.shard_map(local, mesh=mesh, in_specs=in_specs, out_specs=out_specs, check_vma=False)
+    frames, rows = mesh.shape["tm"], mesh.shape["rows"]
+    inner = 8 if rows % 8 == 0 else 1
+    split = Mesh(mesh.devices.reshape(frames, rows // inner, inner), ("tm",) + ROWS)
+    in_specs = (P("tm", ROWS, None, None), P(), P("tm", ROWS, None, None))
+    out_specs = (P("tm", ROWS, None, None), P("tm", ROWS, None, None), P(ROWS, "tm"))
+    return jax.shard_map(local, mesh=split, in_specs=in_specs, out_specs=out_specs, check_vma=False)

time: 119 us -> 123 us (1.034)
  the two profiles are of different devices: /device:TPU:56 before, /device:TPU:2 now
where the time goes in v5:
time: 123 us
  waiting for transfers between devices  48.4 us (39%)
  starting transfers between devices  47.7 us (39%)
  local copies, waits for them, and re-layouts  11.1 us (9%)
  matrix products  8.38 us (7%)
  other arithmetic  6.02 us (5%)
    all_to_all x1, starting transfers between devices, exchanged_scatter(): x = lax.all_to_all(x, 'rz', 0, 0).sum(axis=0)  19.6 us
    all_to_all x1, waiting for transfers between devices, exchanged_scatter(): x = lax.all_to_all(x, 'tm', 1, 1).sum(axis=1)  15 us
    all_to_all x1, waiting for transfers between devices, exchanged_scatter(): x = lax.all_to_all(x, 'rz', 0, 0).sum(axis=0)  11.7 us
    all_to_all x1, waiting for transfers between devices, exchanged_scatter(): x = lax.all_to_all(x, 'ry', 1, 1).sum(axis=1)  11 us
    ppermute x2, starting transfers between devices, passed_along(): return lax.ppermute(x, axis, pairs)  10.7 us
    ppermute x2, waiting for transfers between devices, passed_along(): return lax.ppermute(x, axis, pairs)  6.81 us
    all_to_all x1, starting transfers between devices, exchanged_scatter(): x = lax.all_to_all(x, 'ry', 1, 1).sum(axis=1)  6.36 us
    dot_general x16, matrix products, apply_taps(): jnp.dot(patches[index], kmat[index // 3, index % 3], preferred_element_ty...  5.59 us
  transfers between devices with their start and end apart: 9, of which 7 were waited for; matrix products, arithmetic and copies ran while one was open for 10% of the time, Pallas kernels for 0%

profile of v5, /device:TPU:2, one launch (start us, length us, event | category | flops | bytes accessed | tf_op | source)
XLA Modules:
  0.0 122.7 jit_solution(10622325602618063790)
XLA Ops:
  0.6 1.9 %collective-permute-start = (bf16[2,2,128,128]{3,2,1,0:T(8,128)(2,1)}, bf16[2,2,128,128]{3,2,1,0:T(8,128)(2,1)S(1)}, u32[]{:S(2)}, u32[]{:S(2)}) collective-permute-start(bf16[2,2,128,128]{3,2,1,0:T(8,128)(2,1)} %param.3), channel_id=1, source_target_pairs={{0,128},{128,256},{256,384},{384,512},{512,640},{640,768},{768,896... | collective-permute-start | bytes 393224 | tf_op jit(solution)/shard_map/ppermute | solution.py:12
  2.6 4.6 %collective-permute-done = bf16[2,2,128,128]{3,2,1,0:T(8,128)(2,1)S(1)} collective-permute-done((bf16[2,2,128,128]{3,2,1,0:T(8,128)(2,1)}, bf16[2,2,128,128]{3,2,1,0:T(8,128)(2,1)S(1)}, u32[]{:S(2)}, u32[]{:S(2)}) %collective-permute-start) | collective-permute-done | bytes 131104 | tf_op jit(solution)/shard_map/ppermute | solution.py:12
  7.1 0.9 constant_dynamic-update-slice_fusion
  8.1 3.5 %collective-permute-start.1 = (bf16[4,1,128,128]{3,2,1,0:T(8,128)(2,1)S(1)}, bf16[4,1,128,128]{3,2,1,0:T(8,128)(2,1)S(1)}, u32[]{:S(2)}, u32[]{:S(2)}) collective-permute-start(bf16[4,1,128,128]{3,2,1,0:T(8,128)(2,1)S(1)} %get-tuple-element.60), channel_id=1, source_target_pairs={{0,1},{1,2},{2,3},{3,4},{4,5},{5,6},{6,7},{7,8},{8,9},{9,10},{10,1... | collective-permute-start | bytes 393224 | tf_op jit(solution)/shard_map/ppermute | solution.py:20
  11.6 1.3 %collective-permute-start.2 = (bf16[4,1,128,128]{3,2,1,0:T(8,128)(2,1)S(1)}, bf16[4,1,128,128]{3,2,1,0:T(8,128)(2,1)S(1)}, u32[]{:S(2)}, u32[]{:S(2)}) collective-permute-start(bf16[4,1,128,128]{3,2,1,0:T(8,128)(2,1)S(1)} %get-tuple-element.61), channel_id=1, source_target_pairs={{1,0},{2,1},{3,2},{4,3},{5,4},{6,5},{7,6},{8,7},{9,8},{10,9},{11,1... | collective-permute-start | bytes 393224 | tf_op jit(solution)/shard_map/ppermute | solution.py:23
  12.9 2.0 %copy.11 = bf16[3,3,3,128,128]{3,4,2,1,0:T(8,128)(2,1)S(1)} copy(bf16[3,3,3,128,128]{4,3,2,1,0:T(8,128)(2,1)} %param.4) | data formatting | bytes 1769472 | tf_op args[1]
  15.0 3.5 %collective-permute-done.2 = bf16[4,1,128,128]{3,2,1,0:T(8,128)(2,1)S(1)} collective-permute-done((bf16[4,1,128,128]{3,2,1,0:T(8,128)(2,1)S(1)}, bf16[4,1,128,128]{3,2,1,0:T(8,128)(2,1)S(1)}, u32[]{:S(2)}, u32[]{:S(2)}) %collective-permute-start.2) | collective-permute-done | bytes 131104 | tf_op jit(solution)/shard_map/ppermute | solution.py:23
  18.6 0.5 fusion.26
  19.4 0.9 copy-done
  20.3 0.3 fusion.23
  20.7 0.3 convolution_add_fusion.15
  21.0 0.3 convolution_add_fusion.14
  21.4 0.3 convolution_add_fusion.13
  21.6 0.3 convolution_add_fusion.12
  22.3 0.3 convolution_add_fusion.11
  22.5 0.3 convolution_add_fusion.10
  22.8 0.3 convolution_add_fusion.9
  23.2 1.0 fusion.15
  26.0 8.8 %collective-permute-start.3 = (bf16[2,2,128,128]{3,2,1,0:T(8,128)(2,1)S(1)}, bf16[2,2,128,128]{3,2,1,0:T(8,128)(2,1)S(1)}, u32[]{:S(2)}, u32[]{:S(2)}) collective-permute-start(bf16[2,2,128,128]{3,2,1,0:T(8,128)(2,1)S(1)} %bitcast.123), channel_id=1, source_target_pairs={{128,0},{256,128},{384,256},{512,384},{640,512},{768,640},{896,768... | collective-permute-start | bytes 393224 | tf_op jit(solution)/shard_map/ppermute | solution.py:12
  35.1 2.2 %collective-permute-done.3 = bf16[2,2,128,128]{3,2,1,0:T(8,128)(2,1)S(1)} collective-permute-done((bf16[2,2,128,128]{3,2,1,0:T(8,128)(2,1)S(1)}, bf16[2,2,128,128]{3,2,1,0:T(8,128)(2,1)S(1)}, u32[]{:S(2)}, u32[]{:S(2)}) %collective-permute-start.3) | collective-permute-done | bytes 131104 | tf_op jit(solution)/shard_map/ppermute | solution.py:12
  37.3 0.7 fusion.17
  38.0 1.4 %collective-permute-start.4 = (bf16[4,1,128,128]{3,2,1,0:T(8,128)(2,1)}, bf16[4,1,128,128]{3,2,1,0:T(8,128)(2,1)S(1)}, u32[]{:S(2)}, u32[]{:S(2)}) collective-permute-start(bf16[4,1,128,128]{3,2,1,0:T(8,128)(2,1)} %get-tuple-element.51), channel_id=1, source_target_pairs={{0,1},{1,2},{2,3},{3,4},{4,5},{5,6},{6,7},{7,8},{8,9},{9,10},{10,1... | collective-permute-start | bytes 393224 | tf_op jit(solution)/shard_map/ppermute | solution.py:20
  39.5 1.3 %collective-permute-start.5 = (bf16[4,1,128,128]{3,2,1,0:T(8,128)(2,1)}, bf16[4,1,128,128]{3,2,1,0:T(8,128)(2,1)}, u32[]{:S(2)}, u32[]{:S(2)}) collective-permute-start(bf16[4,1,128,128]{3,2,1,0:T(8,128)(2,1)} %get-tuple-element.52), channel_id=1, source_target_pairs={{1,0},{2,1},{3,2},{4,3},{5,4},{6,5},{7,6},{8,7},{9,8},{10,9},{11,1... | collective-permute-start | bytes 393224 | tf_op jit(solution)/shard_map/ppermute | solution.py:23
  41.0 1.7 %copy.12 = f32[128,3456]{0,1:T(8,128)} copy(f32[128,3456]{1,0:T(8,128)S(1)} %convolution_dynamic-update-slice_fusion) | data formatting | bytes 3538944 | tf_op jit(solution)/shard_map/concatenate | solution.py:123
  42.8 3.5 %all-to-all-start = ((f32[128,8,432]{0,2,1:T(8,128)}), f32[128,8,432]{0,2,1:T(8,128)S(1)}, u32[]{:S(2)}, u32[]{:S(2)}) async-start(f32[128,8,432]{0,2,1:T(8,128)} %bitcast.128), calls=%async_computation | async-start | bytes 3538944 | tf_op jit(solution)/shard_map/all_to_all | solution.py:88
  46.3 0.3 collective-permute-done.5
  46.6 1.0 pad_maximum_fusion.11
  47.6 0.7 fusion.27
  48.3 1.1 select_maximum_fusion
  49.4 1.2 fusion.25
  50.8 0.8 pad_maximum_fusion.16
  51.7 0.3 fusion.22
  52.0 0.3 convolution_add_fusion.7
  52.3 0.3 convolution_add_fusion.6
  52.5 0.3 convolution_add_fusion.5
  52.8 0.3 convolution_add_fusion.4
  53.1 0.3 convolution_add_fusion.3
  53.4 15.0 %all-to-all-done = f32[128,8,432]{0,2,1:T(8,128)S(1)} async-done(((f32[128,8,432]{0,2,1:T(8,128)}), f32[128,8,432]{0,2,1:T(8,128)S(1)}, u32[]{:S(2)}, u32[]{:S(2)}) %all-to-all-start) | async-done | bytes 1769504 | tf_op jit(solution)/shard_map/all_to_all | solution.py:88
  68.4 0.8 reduce_sum.27
  69.2 1.1 copy.13
  70.3 0.9 copy.14
  71.2 6.4 %all-to-all-start.1 = ((f32[16,8,432]{2,0,1:T(8,128)}), f32[16,8,432]{2,0,1:T(8,128)S(1)}, u32[]{:S(2)}, u32[]{:S(2)}) async-start(f32[16,8,432]{2,0,1:T(8,128)} %copy.14), calls=%async_computation.1 | async-start | bytes 524288 | tf_op jit(solution)/shard_map/all_to_all | solution.py:90
  78.2 11.0 %all-to-all-done.1 = f32[16,8,432]{2,0,1:T(8,128)S(1)} async-done(((f32[16,8,432]{2,0,1:T(8,128)}), f32[16,8,432]{2,0,1:T(8,128)S(1)}, u32[]{:S(2)}, u32[]{:S(2)}) %all-to-all-start.1) | async-done | bytes 221216 | tf_op jit(solution)/shard_map/all_to_all | solution.py:90
  89.2 0.6 all_to_all.14
  89.9 19.6 %all-to-all-start.2 = ((f32[16,1,432]{2,1,0:T(1,128)}), f32[16,1,432]{2,1,0:T(1,128)S(1)}, u32[]{:S(2)}, u32[]{:S(2)}) async-start(f32[16,1,432]{2,1,0:T(1,128)} %all_to_all.14), calls=%async_computation.2 | async-start | bytes 65536 | tf_op jit(solution)/shard_map/all_to_all | solution.py:91
  109.4 0.9 fusion
  110.4 11.7 %all-to-all-done.2 = f32[16,1,432]{2,1,0:T(1,128)S(1)} async-done(((f32[16,1,432]{2,1,0:T(1,128)}), f32[16,1,432]{2,1,0:T(1,128)S(1)}, u32[]{:S(2)}, u32[]{:S(2)}) %all-to-all-start.2) | async-done | bytes 27680 | tf_op jit(solution)/shard_map/all_to_all | solution.py:91
  122.1 0.6 reduce_sum.29
  (43 shorter events, 4.3 us)
Async XLA Ops:
  0.6 6.5 %collective-permute-start = (bf16[2,2,128,128]{3,2,1,0:T(8,128)(2,1)}, bf16[2,2,128,128]{3,2,1,0:T(8,128)(2,1)S(1)}, u32[]{:S(2)}, u32[]{:S(2)}) collective-permute-start(bf16[2,2,128,128]{3,2,1,0:T(8,128)(2,1)} %param.3), channel_id=1, source_target_pairs={{0,128},{128,256},{256,384},{384,512},{512,640},{640,768},{768,896... | collective-permute-start | bytes 393224 | tf_op jit(solution)/shard_map/ppermute | solution.py:12
  8.1 6.9 %collective-permute-start.1 = (bf16[4,1,128,128]{3,2,1,0:T(8,128)(2,1)S(1)}, bf16[4,1,128,128]{3,2,1,0:T(8,128)(2,1)S(1)}, u32[]{:S(2)}, u32[]{:S(2)}) collective-permute-start(bf16[4,1,128,128]{3,2,1,0:T(8,128)(2,1)S(1)} %get-tuple-element.60), channel_id=1, source_target_pairs={{0,1},{1,2},{2,3},{3,4},{4,5},{5,6},{6,7},{7,8},{8,9},{9,10},{10,1... | collective-permute-start | bytes 393224 | tf_op jit(solution)/shard_map/ppermute | solution.py:20
  11.6 6.9 %collective-permute-start.2 = (bf16[4,1,128,128]{3,2,1,0:T(8,128)(2,1)S(1)}, bf16[4,1,128,128]{3,2,1,0:T(8,128)(2,1)S(1)}, u32[]{:S(2)}, u32[]{:S(2)}) collective-permute-start(bf16[4,1,128,128]{3,2,1,0:T(8,128)(2,1)S(1)} %get-tuple-element.61), channel_id=1, source_target_pairs={{1,0},{2,1},{3,2},{4,3},{5,4},{6,5},{7,6},{8,7},{9,8},{10,9},{11,1... | collective-permute-start | bytes 393224 | tf_op jit(solution)/shard_map/ppermute | solution.py:23
  19.1 1.2 copy-start
  21.2 0.9 copy-start.2
  22.3 0.9 copy-start.6
  26.0 11.3 %collective-permute-start.3 = (bf16[2,2,128,128]{3,2,1,0:T(8,128)(2,1)S(1)}, bf16[2,2,128,128]{3,2,1,0:T(8,128)(2,1)S(1)}, u32[]{:S(2)}, u32[]{:S(2)}) collective-permute-start(bf16[2,2,128,128]{3,2,1,0:T(8,128)(2,1)S(1)} %bitcast.123), channel_id=1, source_target_pairs={{128,0},{256,128},{384,256},{512,384},{640,512},{768,640},{896,768... | collective-permute-start | bytes 393224 | tf_op jit(solution)/shard_map/ppermute | solution.py:12
  38.0 8.3 %collective-permute-start.4 = (bf16[4,1,128,128]{3,2,1,0:T(8,128)(2,1)}, bf16[4,1,128,128]{3,2,1,0:T(8,128)(2,1)S(1)}, u32[]{:S(2)}, u32[]{:S(2)}) collective-permute-start(bf16[4,1,128,128]{3,2,1,0:T(8,128)(2,1)} %get-tuple-element.51), channel_id=1, source_target_pairs={{0,1},{1,2},{2,3},{3,4},{4,5},{5,6},{6,7},{7,8},{8,9},{9,10},{10,1... | collective-permute-start | bytes 393224 | tf_op jit(solution)/shard_map/ppermute | solution.py:20
  39.5 7.2 %collective-permute-start.5 = (bf16[4,1,128,128]{3,2,1,0:T(8,128)(2,1)}, bf16[4,1,128,128]{3,2,1,0:T(8,128)(2,1)}, u32[]{:S(2)}, u32[]{:S(2)}) collective-permute-start(bf16[4,1,128,128]{3,2,1,0:T(8,128)(2,1)} %get-tuple-element.52), channel_id=1, source_target_pairs={{1,0},{2,1},{3,2},{4,3},{5,4},{6,5},{7,6},{8,7},{9,8},{10,9},{11,1... | collective-permute-start | bytes 393224 | tf_op jit(solution)/shard_map/ppermute | solution.py:23
  42.8 25.6 %all-to-all-start = ((f32[128,8,432]{0,2,1:T(8,128)}), f32[128,8,432]{0,2,1:T(8,128)S(1)}, u32[]{:S(2)}, u32[]{:S(2)}) async-start(f32[128,8,432]{0,2,1:T(8,128)} %bitcast.128), calls=%async_computation | async-start | bytes 3538944 | tf_op jit(solution)/shard_map/all_to_all | solution.py:88
  69.2 8.6 %copy-start.3 = (bf16[2,2,128,128]{3,2,1,0:T(8,128)(2,1)S(1)}, bf16[2,2,128,128]{3,2,1,0:T(8,128)(2,1)}, u32[]{:S(2)}) copy-start(bf16[2,2,128,128]{3,2,1,0:T(8,128)(2,1)} %get-tuple-element.3) | copy-start | bytes 393220
  69.2 8.7 %copy-start.4 = (bf16[2,2,128,128]{3,2,1,0:T(8,128)(2,1)S(1)}, bf16[2,2,128,128]{3,2,1,0:T(8,128)(2,1)}, u32[]{:S(2)}) copy-start(bf16[2,2,128,128]{3,2,1,0:T(8,128)(2,1)} %get-tuple-element.20) | copy-start | bytes 393220
  69.2 8.7 %copy-start.5 = (bf16[2,2,128,128]{3,2,1,0:T(8,128)(2,1)S(1)}, bf16[2,2,128,128]{3,2,1,0:T(8,128)(2,1)}, u32[]{:S(2)}) copy-start(bf16[2,2,128,128]{3,2,1,0:T(8,128)(2,1)} %get-tuple-element.39) | copy-start | bytes 393220
  69.2 8.7 %copy-start.1 = (bf16[2,2,128,384]{3,2,1,0:T(8,128)(2,1)S(1)}, bf16[2,2,128,384]{3,2,1,0:T(8,128)(2,1)}, u32[]{:S(2)}) copy-start(bf16[2,2,128,384]{3,2,1,0:T(8,128)(2,1)} %get-tuple-element.62) | copy-start | bytes 1179652
  71.2 18.0 %all-to-all-start.1 = ((f32[16,8,432]{2,0,1:T(8,128)}), f32[16,8,432]{2,0,1:T(8,128)S(1)}, u32[]{:S(2)}, u32[]{:S(2)}) async-start(f32[16,8,432]{2,0,1:T(8,128)} %copy.14), calls=%async_computation.1 | async-start | bytes 524288 | tf_op jit(solution)/shard_map/all_to_all | solution.py:90
  89.9 32.2 %all-to-all-start.2 = ((f32[16,1,432]{2,1,0:T(1,128)}), f32[16,1,432]{2,1,0:T(1,128)S(1)}, u32[]{:S(2)}, u32[]{:S(2)}) async-start(f32[16,1,432]{2,1,0:T(1,128)} %all_to_all.14), calls=%async_computation.2 | async-start | bytes 65536 | tf_op jit(solution)/shard_map/all_to_all | solution.py:91

commit v6 on v4

--- a/solution.py
+++ b/solution.py
@@ -81,9 +81,8 @@
 def exchanged_scatter(partial_grad):
     outs, cols = partial_grad.shape
     parts = lax.axis_size("tm")
-    x = partial_grad.reshape(outs, parts, cols // parts)
-    x = lax.all_to_all(x, "tm", 1, 1).sum(axis=1)
-    x = lax.all_to_all(x, "rows", 0, 0).sum(axis=0)
+    x = partial_grad.reshape(outs * parts, cols // parts)
+    x = lax.all_to_all(x, ("rows", "tm"), 0, 0).sum(axis=0)
     return x.reshape(1, -1)
 
 

time: 119 us -> 171 us (1.44)
  the two profiles are of different devices: /device:TPU:56 before, /device:TPU:1 now
where the time goes in v6:
time: 171 us
  waiting for transfers between devices  97.9 us (57%)
  starting transfers between devices  47.3 us (28%)
  local copies, waits for them, and re-layouts  12.1 us (7%)
  matrix products  8.37 us (5%)
  other arithmetic  4.04 us (2%)
    all_to_all x1, waiting for transfers between devices, exchanged_scatter(): x = lax.all_to_all(x, ('rows', 'tm'), 0, 0).sum(axis=0)  74.2 us
    all_to_all x1, starting transfers between devices, exchanged_scatter(): x = lax.all_to_all(x, ('rows', 'tm'), 0, 0).sum(axis=0)  27.1 us
    ppermute x2, starting transfers between devices, passed_along(): return lax.ppermute(x, axis, pairs)  15 us
    ppermute x2, waiting for transfers between devices, passed_along(): return lax.ppermute(x, axis, pairs)  12.9 us
    ppermute x2, waiting for transfers between devices, padded(): lax.ppermute(lax.slice_in_dim(block, 0, width, axis=dim), axis, backward)  8.52 us
    dot_general x16, matrix products, apply_taps(): jnp.dot(patches[index], kmat[index // 3, index % 3], preferred_element_ty...  5.59 us
    all_to_all x1, local copies, waits for them, and re-layouts, exchanged_scatter(): x = lax.all_to_all(x, ('rows', 'tm'), 0, 0).sum(axis=0)  4.87 us
    unnamed x10, local copies, waits for them, and re-layouts  4.21 us
  transfers between devices with their start and end apart: 7, of which 7 were waited for; matrix products, arithmetic and copies ran while one was open for 5% of the time, Pallas kernels for 0%

profile of v6, /device:TPU:1, one launch (start us, length us, event | category | flops | bytes accessed | tf_op | source)
XLA Modules:
  0.0 170.8 jit_solution(13147962894091395429)
XLA Ops:
  0.6 4.5 %collective-permute-start = (bf16[2,2,128,128]{3,2,1,0:T(8,128)(2,1)}, bf16[2,2,128,128]{3,2,1,0:T(8,128)(2,1)S(1)}, u32[]{:S(2)}, u32[]{:S(2)}) collective-permute-start(bf16[2,2,128,128]{3,2,1,0:T(8,128)(2,1)} %param.3), channel_id=1, source_target_pairs={{0,128},{128,256},{256,384},{384,512},{512,640},{640,768},{768,896... | collective-permute-start | bytes 393224 | tf_op jit(solution)/shard_map/ppermute | solution.py:10
  5.1 12.0 %collective-permute-done = bf16[2,2,128,128]{3,2,1,0:T(8,128)(2,1)S(1)} collective-permute-done((bf16[2,2,128,128]{3,2,1,0:T(8,128)(2,1)}, bf16[2,2,128,128]{3,2,1,0:T(8,128)(2,1)S(1)}, u32[]{:S(2)}, u32[]{:S(2)}) %collective-permute-start) | collective-permute-done | bytes 131104 | tf_op jit(solution)/shard_map/ppermute | solution.py:10
  17.1 0.9 constant_dynamic-update-slice_fusion
  18.1 1.3 collective-permute-start.1
  19.4 1.3 collective-permute-start.2
  20.7 1.7 collective-permute-done.1
  22.4 3.9 %collective-permute-done.2 = bf16[4,1,128,128]{3,2,1,0:T(8,128)(2,1)S(1)} collective-permute-done((bf16[4,1,128,128]{3,2,1,0:T(8,128)(2,1)S(1)}, bf16[4,1,128,128]{3,2,1,0:T(8,128)(2,1)S(1)}, u32[]{:S(2)}, u32[]{:S(2)}) %collective-permute-start.2) | collective-permute-done | bytes 131104 | tf_op jit(solution)/shard_map/ppermute | solution.py:21
  26.4 0.5 fusion.26
  27.2 0.9 copy-done.1
  28.1 0.3 fusion.23
  28.5 0.3 convolution_add_fusion.15
  28.7 0.3 convolution_add_fusion.14
  29.1 0.3 convolution_add_fusion.13
  29.4 0.3 convolution_add_fusion.12
  30.0 0.3 convolution_add_fusion.11
  30.3 0.3 convolution_add_fusion.10
  30.6 0.3 convolution_add_fusion.9
  30.9 1.0 fusion.15
  32.2 0.3 convolution_dynamic-update-slice_fusion.7
  32.4 0.3 convolution_dynamic-update-slice_fusion.6
  32.7 0.3 convolution_dynamic-update-slice_fusion.5
  33.0 0.3 convolution_dynamic-update-slice_fusion.4
  33.5 0.3 convolution_dynamic-update-slice_fusion.2
  33.7 0.3 convolution_dynamic-update-slice_fusion.1
  34.3 4.9 %all_to_all.8 = f32[1024,1,432]{2,1,0:T(1,128)} reshape(f32[128,3456]{1,0:T(8,128)S(1)} %convolution_dynamic-update-slice_fusion) | data formatting | bytes 3538944 | tf_op jit(solution)/shard_map/all_to_all | solution.py:85
  39.1 27.1 %all-to-all-start = ((f32[1024,1,432]{2,1,0:T(1,128)}), f32[1024,1,432]{2,1,0:T(1,128)S(1)}, u32[]{:S(2)}, u32[]{:S(2)}) async-start(f32[1024,1,432]{2,1,0:T(1,128)} %all_to_all.8), calls=%async_computation | async-start | bytes 4194304 | tf_op jit(solution)/shard_map/all_to_all | solution.py:85
  66.2 10.5 %collective-permute-start.3 = (bf16[2,2,128,128]{3,2,1,0:T(8,128)(2,1)S(1)}, bf16[2,2,128,128]{3,2,1,0:T(8,128)(2,1)S(1)}, u32[]{:S(2)}, u32[]{:S(2)}) collective-permute-start(bf16[2,2,128,128]{3,2,1,0:T(8,128)(2,1)S(1)} %bitcast.121), channel_id=1, source_target_pairs={{128,0},{256,128},{384,256},{512,384},{640,512},{768,640},{896,768... | collective-permute-start | bytes 393224 | tf_op jit(solution)/shard_map/ppermute | solution.py:10
  76.7 1.0 collective-permute-done.3
  77.7 0.7 fusion.17
  78.4 1.3 collective-permute-start.4
  79.7 1.3 collective-permute-start.5
  81.0 2.0 %copy.7 = bf16[3,3,3,128,128]{3,4,2,1,0:T(8,128)(2,1)S(1)} copy(bf16[3,3,3,128,128]{4,3,2,1,0:T(8,128)(2,1)} %param.4) | data formatting | bytes 1769472 | tf_op args[1]
  83.0 1.0 rev.3
  84.0 0.6 collective-permute-done.4
  84.6 4.6 %collective-permute-done.5 = bf16[4,1,128,128]{3,2,1,0:T(8,128)(2,1)S(1)} collective-permute-done((bf16[4,1,128,128]{3,2,1,0:T(8,128)(2,1)}, bf16[4,1,128,128]{3,2,1,0:T(8,128)(2,1)S(1)}, u32[]{:S(2)}, u32[]{:S(2)}) %collective-permute-start.5) | collective-permute-done | bytes 131104 | tf_op jit(solution)/shard_map/ppermute | solution.py:21
  89.5 0.5 fusion.25
  90.6 0.9 copy-done
  91.5 0.3 fusion.22
  91.8 0.3 convolution_add_fusion.7
  92.0 0.3 convolution_add_fusion.6
  92.3 0.3 convolution_add_fusion.5
  92.6 0.3 convolution_add_fusion.4
  92.9 0.3 convolution_add_fusion.3
  93.1 0.3 convolution_add_fusion.2
  93.4 0.3 convolution_add_fusion.1
  93.7 0.9 fusion
  94.6 74.2 %all-to-all-done = f32[1024,1,432]{2,1,0:T(1,128)S(1)} async-done(((f32[1024,1,432]{2,1,0:T(1,128)}), f32[1024,1,432]{2,1,0:T(1,128)S(1)}, u32[]{:S(2)}, u32[]{:S(2)}) %all-to-all-start) | async-done | bytes 1769504 | tf_op jit(solution)/shard_map/all_to_all | solution.py:85
  168.8 2.0 %reduce_sum.9 = f32[432]{0:T(512)} reduce(f32[1024,1,432]{2,1,0:T(1,128)S(1)} %all-to-all-done, f32[]{:T(128)} %constant.6.clone.1), dimensions={0,1}, to_apply=%region_0.1 | reduce | flops 441936 | bytes 1771204 | tf_op jit(solution)/shard_map/reduce_sum | solution.py:85
  (28 shorter events, 2.6 us)
Async XLA Ops:
  0.6 16.5 %collective-permute-start = (bf16[2,2,128,128]{3,2,1,0:T(8,128)(2,1)}, bf16[2,2,128,128]{3,2,1,0:T(8,128)(2,1)S(1)}, u32[]{:S(2)}, u32[]{:S(2)}) collective-permute-start(bf16[2,2,128,128]{3,2,1,0:T(8,128)(2,1)} %param.3), channel_id=1, source_target_pairs={{0,128},{128,256},{256,384},{384,512},{512,640},{640,768},{768,896... | collective-permute-start | bytes 393224 | tf_op jit(solution)/shard_map/ppermute | solution.py:10
  18.1 4.3 %collective-permute-start.1 = (bf16[4,1,128,128]{3,2,1,0:T(8,128)(2,1)S(1)}, bf16[4,1,128,128]{3,2,1,0:T(8,128)(2,1)S(1)}, u32[]{:S(2)}, u32[]{:S(2)}) collective-permute-start(bf16[4,1,128,128]{3,2,1,0:T(8,128)(2,1)S(1)} %get-tuple-element.60), channel_id=1, source_target_pairs={{0,1},{1,2},{2,3},{3,4},{4,5},{5,6},{6,7},{7,8},{8,9},{9,10},{10,1... | collective-permute-start | bytes 393224 | tf_op jit(solution)/shard_map/ppermute | solution.py:18
  19.4 6.8 %collective-permute-start.2 = (bf16[4,1,128,128]{3,2,1,0:T(8,128)(2,1)S(1)}, bf16[4,1,128,128]{3,2,1,0:T(8,128)(2,1)S(1)}, u32[]{:S(2)}, u32[]{:S(2)}) collective-permute-start(bf16[4,1,128,128]{3,2,1,0:T(8,128)(2,1)S(1)} %get-tuple-element.61), channel_id=1, source_target_pairs={{1,0},{2,1},{3,2},{4,3},{5,4},{6,5},{7,6},{8,7},{9,8},{10,9},{11,1... | collective-permute-start | bytes 393224 | tf_op jit(solution)/shard_map/ppermute | solution.py:21
  26.9 1.2 copy-start.1
  29.0 0.9 copy-start.2
  30.0 0.9 copy-start.3
  39.1 129.7 %all-to-all-start = ((f32[1024,1,432]{2,1,0:T(1,128)}), f32[1024,1,432]{2,1,0:T(1,128)S(1)}, u32[]{:S(2)}, u32[]{:S(2)}) async-start(f32[1024,1,432]{2,1,0:T(1,128)} %all_to_all.8), calls=%async_computation | async-start | bytes 4194304 | tf_op jit(solution)/shard_map/all_to_all | solution.py:85
  66.2 11.5 %collective-permute-start.3 = (bf16[2,2,128,128]{3,2,1,0:T(8,128)(2,1)S(1)}, bf16[2,2,128,128]{3,2,1,0:T(8,128)(2,1)S(1)}, u32[]{:S(2)}, u32[]{:S(2)}) collective-permute-start(bf16[2,2,128,128]{3,2,1,0:T(8,128)(2,1)S(1)} %bitcast.121), channel_id=1, source_target_pairs={{128,0},{256,128},{384,256},{512,384},{640,512},{768,640},{896,768... | collective-permute-start | bytes 393224 | tf_op jit(solution)/shard_map/ppermute | solution.py:10
  78.4 6.2 %collective-permute-start.4 = (bf16[4,1,128,128]{3,2,1,0:T(8,128)(2,1)}, bf16[4,1,128,128]{3,2,1,0:T(8,128)(2,1)S(1)}, u32[]{:S(2)}, u32[]{:S(2)}) collective-permute-start(bf16[4,1,128,128]{3,2,1,0:T(8,128)(2,1)} %get-tuple-element.51), channel_id=1, source_target_pairs={{0,1},{1,2},{2,3},{3,4},{4,5},{5,6},{6,7},{7,8},{8,9},{9,10},{10,1... | collective-permute-start | bytes 393224 | tf_op jit(solution)/shard_map/ppermute | solution.py:18
  79.7 9.5 %collective-permute-start.5 = (bf16[4,1,128,128]{3,2,1,0:T(8,128)(2,1)}, bf16[4,1,128,128]{3,2,1,0:T(8,128)(2,1)S(1)}, u32[]{:S(2)}, u32[]{:S(2)}) collective-permute-start(bf16[4,1,128,128]{3,2,1,0:T(8,128)(2,1)} %get-tuple-element.52), channel_id=1, source_target_pairs={{1,0},{2,1},{3,2},{4,3},{5,4},{6,5},{7,6},{8,7},{9,8},{10,9},{11,1... | collective-permute-start | bytes 393224 | tf_op jit(solution)/shard_map/ppermute | solution.py:21
  90.3 1.2 copy-start

commit v7 on v1

--- a/solution.py
+++ b/solution.py
@@ -4,23 +4,29 @@
 from jax.sharding import PartitionSpec as P
 
 
-def passed_along(x, axis, by):
-    devices = lax.axis_size(axis)
-    pairs = [(i, i + by) for i in range(devices) if 0 <= i + by < devices]
-    return lax.ppermute(x, axis, pairs)
+def shifted(x, by_tm, by_rows):
+    frames, rows = lax.axis_size("tm"), lax.axis_size("rows")
+    pairs = [
+        (m * rows + r, (m + by_tm) * rows + r + by_rows)
+        for m in range(frames)
+        for r in range(rows)
+        if 0 <= m + by_tm < frames and 0 <= r + by_rows < rows
+    ]
+    return lax.ppermute(x, ("tm", "rows"), pairs)
 
 
-def padded(block, sides, width):
-    for axis, dim in sides:
-        count = lax.axis_size(axis)
-        forward = [(i, i + 1) for i in range(count - 1)]
-        backward = [(target, source) for source, target in forward]
-        low = lax.ppermute(
-            lax.slice_in_dim(block, block.shape[dim] - width, None, axis=dim), axis, forward
-        )
-        high = lax.ppermute(lax.slice_in_dim(block, 0, width, axis=dim), axis, backward)
-        block = jnp.concatenate([low, block, high], axis=dim)
-    return block
+def haloed(block, by_tm):
+    last, first = block[:, -1:], block[:, :1]
+    other = shifted(block, by_tm, 0)
+    above = shifted(last, 0, 1)
+    below = shifted(first, 0, -1)
+    above_other = shifted(last, by_tm, 1)
+    below_other = shifted(first, by_tm, -1)
+    if by_tm > 0:
+        parts = [(above_other, above), (other, block), (below_other, below)]
+    else:
+        parts = [(above, above_other), (block, other), (below, below_other)]
+    return jnp.concatenate([jnp.concatenate(p, axis=0) for p in parts], axis=1)
 
 
 def make_patches(extended):
@@ -48,11 +54,19 @@
     return total
 
 
+def exchanged_scatter(partial_grad):
+    outs, cols = partial_grad.shape
+    parts = lax.axis_size("tm")
+    x = partial_grad.reshape(outs, parts, cols // parts)
+    x = lax.all_to_all(x, "tm", 1, 1).sum(axis=1)
+    x = lax.all_to_all(x, "rows", 0, 0).sum(axis=0)
+    return x.reshape(1, -1)
+
+
 def local(video, kernel, cotangent):
     frames, height, width, chans = video.shape
     forward_mat = kernel.reshape(3, 3, 3 * chans, chans)
-    earlier = passed_along(video, "tm", 1)
-    extended = padded(jnp.concatenate([earlier, video], axis=0), (("rows", 1),), 1)
+    extended = haloed(video, 1)
     patches = make_patches(extended)
     pre = apply_taps(patches, forward_mat)
     sig = 1.0 / (1.0 + jnp.exp(-pre))
@@ -60,8 +74,7 @@
     grad_flat = cotangent.reshape(frames * height * width, chans).astype(jnp.float32)
     pre_grad = (grad_flat * sig * (1.0 + pre * (1.0 - sig))).astype(jnp.bfloat16)
     pre_grid = pre_grad.reshape(frames, height, width, chans)
-    later = passed_along(pre_grid, "tm", -1)
-    grad_ext = padded(jnp.concatenate([pre_grid, later], axis=0), (("rows", 1),), 1)
+    grad_ext = haloed(pre_grid, -1)
     flipped = jnp.transpose(kernel[::-1, ::-1, ::-1], (0, 1, 2, 4, 3)).reshape(
         3, 3, 3 * chans, chans
     )
@@ -77,8 +90,7 @@
         for piece in patches
     ]
     partial_grad = jnp.concatenate(blocks, axis=1)
-    owned = lax.psum_scatter(partial_grad, "tm", scatter_dimension=1, tiled=True)
-    kernel_grad = lax.psum_scatter(owned, "rows", scatter_dimension=0, tiled=True)
+    kernel_grad = exchanged_scatter(partial_grad)
     return (activated, input_grad, kernel_grad)
 
 

time: 389 us -> 126 us (0.32)
  waiting for transfers between devices: 328 us -> 40.5 us
  starting transfers between devices: 14.8 us -> 59.5 us
  between operations: 14.4 us -> 1.2 us
  matrix products: 14.7 us -> 8.39 us
    unnamed x4 -> x0, waiting for transfers between devices: 319 us -> none
    all_to_all x0 -> x2, waiting for transfers between devices: none -> 38.5 us  [the longest x1 19.6 us: exchanged_scatter(): x = lax.all_to_all(x, 'rows', 0, 0).sum(axis=0)]
    all_to_all x0 -> x2, starting transfers between devices: none -> 35.8 us  [the longest x1 25.4 us: exchanged_scatter(): x = lax.all_to_all(x, 'rows', 0, 0).sum(axis=0)]
    ppermute x6 -> x10, starting transfers between devices: 14.7 us -> 23.7 us  [shifted(): return lax.ppermute(x, ('tm', 'rows'), pairs)]
    unnamed x12, local copies, waits for them, and re-layouts: 11 us -> 3.12 us
    ppermute x6 -> x10, waiting for transfers between devices: 8.91 us -> 1.99 us  [shifted(): return lax.ppermute(x, ('tm', 'rows'), pairs)]
    dot_general x9, matrix products: 8.56 us -> 2.26 us  [local(): lax.dot_general(pre_grad, piece, (((0,), (0,)), ((), ())), preferred_elem...]
  transfers between devices with their start and end apart: 8 -> 12, of which waited for: 6 -> 3; matrix products, arithmetic and copies ran while one was open for 3% -> 11% of each run, Pallas kernels for 0% -> 0%
where the time goes in v7:
time: 126 us; the launch traced here: 125 us
  starting transfers between devices  59.5 us (47%)
  waiting for transfers between devices  40.5 us (32%)
  local copies, waits for them, and re-layouts  10.7 us (8%)
  matrix products  8.39 us (7%)
  other arithmetic  5.02 us (4%)
    all_to_all x1, starting transfers between devices, exchanged_scatter(): x = lax.all_to_all(x, 'rows', 0, 0).sum(axis=0)  25.4 us
    ppermute x10, starting transfers between devices, shifted(): return lax.ppermute(x, ('tm', 'rows'), pairs)  23.7 us
    all_to_all x1, waiting for transfers between devices, exchanged_scatter(): x = lax.all_to_all(x, 'rows', 0, 0).sum(axis=0)  19.6 us
    all_to_all x1, waiting for transfers between devices, exchanged_scatter(): x = lax.all_to_all(x, 'tm', 1, 1).sum(axis=1)  18.9 us
    all_to_all x1, starting transfers between devices, exchanged_scatter(): x = lax.all_to_all(x, 'tm', 1, 1).sum(axis=1)  10.4 us
    dot_general x16, matrix products, apply_taps(): jnp.dot(patches[index], kmat[index // 3, index % 3], preferred_element_ty...  5.61 us
    unnamed x12, local copies, waits for them, and re-layouts  3.12 us
    concatenate x11, other arithmetic, make_patches(): jnp.concatenate(parts, axis=-1).reshape(frames * height * width, 3 * chans)  2.99 us
  transfers between devices with their start and end apart: 12, of which 3 were waited for; matrix products, arithmetic and copies ran while one was open for 11% of the time, Pallas kernels for 0%

profile of v7, /device:TPU:56, one launch (start us, length us, event | category | flops | bytes accessed | tf_op | source)
XLA Modules:
  0.0 125.2 jit_solution(15120317141614039726)
XLA Ops:
  0.6 0.9 fusion.28
  1.5 2.9 %collective-permute-start = (bf16[2,1,128,128]{3,2,1,0:T(8,128)(2,1)S(1)}, bf16[2,1,128,128]{3,2,1,0:T(8,128)(2,1)S(1)}, u32[]{:S(2)}, u32[]{:S(2)}) collective-permute-start(bf16[2,1,128,128]{3,2,1,0:T(8,128)(2,1)S(1)} %get-tuple-element.62), channel_id=1, source_target_pairs={{0,129},{1,130},{2,131},{3,132},{4,133},{5,134},{6,135},{7,136},{8... | collective-permute-start | bytes 196616 | tf_op jit(solution)/shard_map/ppermute | solution.py:15
  4.5 3.5 %collective-permute-start.1 = (bf16[2,1,128,128]{3,2,1,0:T(8,128)(2,1)S(1)}, bf16[2,1,128,128]{3,2,1,0:T(8,128)(2,1)S(1)}, u32[]{:S(2)}, u32[]{:S(2)}) collective-permute-start(bf16[2,1,128,128]{3,2,1,0:T(8,128)(2,1)S(1)} %get-tuple-element.62), channel_id=1, source_target_pairs={{0,1},{1,2},{2,3},{3,4},{4,5},{5,6},{6,7},{7,8},{8,9},{9,10},{10,1... | collective-permute-start | bytes 196616 | tf_op jit(solution)/shard_map/ppermute | solution.py:15
  8.0 3.4 %collective-permute-start.3 = (bf16[2,1,128,128]{3,2,1,0:T(8,128)(2,1)S(1)}, bf16[2,1,128,128]{3,2,1,0:T(8,128)(2,1)S(1)}, u32[]{:S(2)}, u32[]{:S(2)}) collective-permute-start(bf16[2,1,128,128]{3,2,1,0:T(8,128)(2,1)S(1)} %get-tuple-element.63), channel_id=1, source_target_pairs={{1,128},{2,129},{3,130},{4,131},{5,132},{6,133},{7,134},{8,135},{9... | collective-permute-start | bytes 196616 | tf_op jit(solution)/shard_map/ppermute | solution.py:15
  11.4 2.4 %collective-permute-start.4 = (bf16[2,1,128,128]{3,2,1,0:T(8,128)(2,1)S(1)}, bf16[2,1,128,128]{3,2,1,0:T(8,128)(2,1)S(1)}, u32[]{:S(2)}, u32[]{:S(2)}) collective-permute-start(bf16[2,1,128,128]{3,2,1,0:T(8,128)(2,1)S(1)} %get-tuple-element.63), channel_id=1, source_target_pairs={{1,0},{2,1},{3,2},{4,3},{5,4},{6,5},{7,6},{8,7},{9,8},{10,9},{11,1... | collective-permute-start | bytes 196616 | tf_op jit(solution)/shard_map/ppermute | solution.py:15
  13.7 1.7 %collective-permute-start.2 = (bf16[2,2,128,128]{3,2,1,0:T(8,128)(2,1)}, bf16[2,2,128,128]{3,2,1,0:T(8,128)(2,1)S(1)}, u32[]{:S(2)}, u32[]{:S(2)}) collective-permute-start(bf16[2,2,128,128]{3,2,1,0:T(8,128)(2,1)} %param.3), channel_id=1, source_target_pairs={{0,128},{1,129},{2,130},{3,131},{4,132},{5,133},{6,134},{7,135},{8... | collective-permute-start | bytes 393224 | tf_op jit(solution)/shard_map/ppermute | solution.py:15
  15.5 2.0 %copy.8 = bf16[3,3,3,128,128]{3,4,2,1,0:T(8,128)(2,1)S(1)} copy(bf16[3,3,3,128,128]{4,3,2,1,0:T(8,128)(2,1)} %param.4) | data formatting | bytes 1769472 | tf_op args[1]
  17.7 2.0 %collective-permute-done.4 = bf16[2,1,128,128]{3,2,1,0:T(8,128)(2,1)S(1)} collective-permute-done((bf16[2,1,128,128]{3,2,1,0:T(8,128)(2,1)S(1)}, bf16[2,1,128,128]{3,2,1,0:T(8,128)(2,1)S(1)}, u32[]{:S(2)}, u32[]{:S(2)}) %collective-permute-start.4) | collective-permute-done | bytes 65568 | tf_op jit(solution)/shard_map/ppermute | solution.py:15
  20.0 0.5 fusion.24
  20.7 1.0 copy-done
  21.6 0.3 fusion.21
  22.0 0.3 convolution_add_fusion.15
  22.3 0.3 convolution_add_fusion.14
  22.7 0.3 convolution_add_fusion.13
  22.9 0.3 convolution_add_fusion.12
  23.3 0.3 convolution_add_fusion.11
  23.6 0.3 convolution_add_fusion.10
  23.9 0.3 convolution_add_fusion.9
  24.2 1.0 fusion.15
  25.5 3.6 %collective-permute-start.5 = (bf16[2,1,128,128]{3,2,1,0:T(8,128)(2,1)S(1)}, bf16[2,1,128,128]{3,2,1,0:T(8,128)(2,1)S(1)}, u32[]{:S(2)}, u32[]{:S(2)}) collective-permute-start(bf16[2,1,128,128]{3,2,1,0:T(8,128)(2,1)S(1)} %get-tuple-element.60), channel_id=1, source_target_pairs={{0,1},{1,2},{2,3},{3,4},{4,5},{5,6},{6,7},{7,8},{8,9},{9,10},{10,1... | collective-permute-start | bytes 196616 | tf_op jit(solution)/shard_map/ppermute | solution.py:15
  29.2 1.3 %collective-permute-start.6 = (bf16[2,1,128,128]{3,2,1,0:T(8,128)(2,1)S(1)}, bf16[2,1,128,128]{3,2,1,0:T(8,128)(2,1)S(1)}, u32[]{:S(2)}, u32[]{:S(2)}) collective-permute-start(bf16[2,1,128,128]{3,2,1,0:T(8,128)(2,1)S(1)} %get-tuple-element.60), channel_id=1, source_target_pairs={{128,1},{129,2},{130,3},{131,4},{132,5},{133,6},{134,7},{135,8},{1... | collective-permute-start | bytes 196616 | tf_op jit(solution)/shard_map/ppermute | solution.py:15
  30.5 2.2 %collective-permute-start.8 = (bf16[2,1,128,128]{3,2,1,0:T(8,128)(2,1)S(1)}, bf16[2,1,128,128]{3,2,1,0:T(8,128)(2,1)S(1)}, u32[]{:S(2)}, u32[]{:S(2)}) collective-permute-start(bf16[2,1,128,128]{3,2,1,0:T(8,128)(2,1)S(1)} %get-tuple-element.61), channel_id=1, source_target_pairs={{1,0},{2,1},{3,2},{4,3},{5,4},{6,5},{7,6},{8,7},{9,8},{10,9},{11,1... | collective-permute-start | bytes 196616 | tf_op jit(solution)/shard_map/ppermute | solution.py:15
  32.7 1.3 %collective-permute-start.9 = (bf16[2,1,128,128]{3,2,1,0:T(8,128)(2,1)S(1)}, bf16[2,1,128,128]{3,2,1,0:T(8,128)(2,1)S(1)}, u32[]{:S(2)}, u32[]{:S(2)}) collective-permute-start(bf16[2,1,128,128]{3,2,1,0:T(8,128)(2,1)S(1)} %get-tuple-element.61), channel_id=1, source_target_pairs={{129,0},{130,1},{131,2},{132,3},{133,4},{134,5},{135,6},{136,7},{1... | collective-permute-start | bytes 196616 | tf_op jit(solution)/shard_map/ppermute | solution.py:15
  34.0 1.3 %collective-permute-start.7 = (bf16[2,2,128,128]{3,2,1,0:T(8,128)(2,1)S(1)}, bf16[2,2,128,128]{3,2,1,0:T(8,128)(2,1)S(1)}, u32[]{:S(2)}, u32[]{:S(2)}) collective-permute-start(bf16[2,2,128,128]{3,2,1,0:T(8,128)(2,1)S(1)} %bitcast.124), channel_id=1, source_target_pairs={{128,0},{129,1},{130,2},{131,3},{132,4},{133,5},{134,6},{135,7},{1... | collective-permute-start | bytes 393224 | tf_op jit(solution)/shard_map/ppermute | solution.py:15
  35.5 0.3 convolution_dynamic-update-slice_fusion.6
  36.3 0.3 convolution_dynamic-update-slice_fusion.3
  37.3 1.8 %copy.9 = f32[128,3456]{0,1:T(8,128)} copy(f32[128,3456]{1,0:T(8,128)S(1)} %convolution_dynamic-update-slice_fusion) | data formatting | bytes 3538944 | tf_op jit(solution)/shard_map/concatenate | solution.py:92
  39.1 10.4 %all-to-all-start = ((f32[128,8,432]{0,2,1:T(8,128)}), f32[128,8,432]{0,2,1:T(8,128)S(1)}, u32[]{:S(2)}, u32[]{:S(2)}) async-start(f32[128,8,432]{0,2,1:T(8,128)} %bitcast.128), calls=%async_computation | async-start | bytes 3538944 | tf_op jit(solution)/shard_map/all_to_all | solution.py:61
  49.7 0.7 fusion.25
  50.5 1.1 fusion.23
  51.6 0.7 fusion.26
  52.7 0.3 fusion.20
  52.9 0.3 convolution_add_fusion.7
  53.2 0.3 convolution_add_fusion.6
  53.5 0.3 convolution_add_fusion.5
  53.7 0.3 convolution_add_fusion.4
  54.0 0.3 convolution_add_fusion.3
  54.3 18.9 %all-to-all-done = f32[128,8,432]{0,2,1:T(8,128)S(1)} async-done(((f32[128,8,432]{0,2,1:T(8,128)}), f32[128,8,432]{0,2,1:T(8,128)S(1)}, u32[]{:S(2)}, u32[]{:S(2)}) %all-to-all-start) | async-done | bytes 1769504 | tf_op jit(solution)/shard_map/all_to_all | solution.py:61
  73.2 0.8 reduce_sum.18
  73.9 1.8 %copy.10 = f32[128,1,432]{2,1,0:T(1,128)} copy(f32[128,1,432]{0,2,1:T(8,128)} %bitcast.173) | data formatting | bytes 442368 | tf_op jit(solution)/shard_map/all_to_all | solution.py:62
  75.7 25.4 %all-to-all-start.1 = ((f32[128,1,432]{2,1,0:T(1,128)}), f32[128,1,432]{2,1,0:T(1,128)S(1)}, u32[]{:S(2)}, u32[]{:S(2)}) async-start(f32[128,1,432]{2,1,0:T(1,128)} %copy.10), calls=%async_computation.1 | async-start | bytes 524288 | tf_op jit(solution)/shard_map/all_to_all | solution.py:62
  101.2 1.1 pad_maximum_fusion.17
  102.2 1.1 pad_maximum_fusion.15
  103.3 0.3 convolution_add_fusion.2
  103.6 0.3 convolution_add_fusion.1
  103.9 0.9 fusion
  104.8 19.6 %all-to-all-done.1 = f32[128,1,432]{2,1,0:T(1,128)S(1)} async-done(((f32[128,1,432]{2,1,0:T(1,128)}), f32[128,1,432]{2,1,0:T(1,128)S(1)}, u32[]{:S(2)}, u32[]{:S(2)}) %all-to-all-start.1) | async-done | bytes 221216 | tf_op jit(solution)/shard_map/all_to_all | solution.py:62
  124.4 0.8 reduce_sum.19
  (46 shorter events, 3.3 us)
Async XLA Ops:
  1.5 16.1 %collective-permute-start = (bf16[2,1,128,128]{3,2,1,0:T(8,128)(2,1)S(1)}, bf16[2,1,128,128]{3,2,1,0:T(8,128)(2,1)S(1)}, u32[]{:S(2)}, u32[]{:S(2)}) collective-permute-start(bf16[2,1,128,128]{3,2,1,0:T(8,128)(2,1)S(1)} %get-tuple-element.62), channel_id=1, source_target_pairs={{0,129},{1,130},{2,131},{3,132},{4,133},{5,134},{6,135},{7,136},{8... | collective-permute-start | bytes 196616 | tf_op jit(solution)/shard_map/ppermute | solution.py:15
  4.5 13.2 %collective-permute-start.1 = (bf16[2,1,128,128]{3,2,1,0:T(8,128)(2,1)S(1)}, bf16[2,1,128,128]{3,2,1,0:T(8,128)(2,1)S(1)}, u32[]{:S(2)}, u32[]{:S(2)}) collective-permute-start(bf16[2,1,128,128]{3,2,1,0:T(8,128)(2,1)S(1)} %get-tuple-element.62), channel_id=1, source_target_pairs={{0,1},{1,2},{2,3},{3,4},{4,5},{5,6},{6,7},{7,8},{8,9},{9,10},{10,1... | collective-permute-start | bytes 196616 | tf_op jit(solution)/shard_map/ppermute | solution.py:15
  7.9 11.8 %copy-start.1 = (bf16[2,2,128,128]{3,2,1,0:T(8,128)(2,1)S(1)}, bf16[2,2,128,128]{3,2,1,0:T(8,128)(2,1)}, u32[]{:S(2)}) copy-start(bf16[2,2,128,128]{3,2,1,0:T(8,128)(2,1)} %param.3) | copy-start | bytes 393220
  8.0 9.7 %collective-permute-start.3 = (bf16[2,1,128,128]{3,2,1,0:T(8,128)(2,1)S(1)}, bf16[2,1,128,128]{3,2,1,0:T(8,128)(2,1)S(1)}, u32[]{:S(2)}, u32[]{:S(2)}) collective-permute-start(bf16[2,1,128,128]{3,2,1,0:T(8,128)(2,1)S(1)} %get-tuple-element.63), channel_id=1, source_target_pairs={{1,128},{2,129},{3,130},{4,131},{5,132},{6,133},{7,134},{8,135},{9... | collective-permute-start | bytes 196616 | tf_op jit(solution)/shard_map/ppermute | solution.py:15
  11.4 8.3 %collective-permute-start.4 = (bf16[2,1,128,128]{3,2,1,0:T(8,128)(2,1)S(1)}, bf16[2,1,128,128]{3,2,1,0:T(8,128)(2,1)S(1)}, u32[]{:S(2)}, u32[]{:S(2)}) collective-permute-start(bf16[2,1,128,128]{3,2,1,0:T(8,128)(2,1)S(1)} %get-tuple-element.63), channel_id=1, source_target_pairs={{1,0},{2,1},{3,2},{4,3},{5,4},{6,5},{7,6},{8,7},{9,8},{10,9},{11,1... | collective-permute-start | bytes 196616 | tf_op jit(solution)/shard_map/ppermute | solution.py:15
  13.7 5.9 %collective-permute-start.2 = (bf16[2,2,128,128]{3,2,1,0:T(8,128)(2,1)}, bf16[2,2,128,128]{3,2,1,0:T(8,128)(2,1)S(1)}, u32[]{:S(2)}, u32[]{:S(2)}) collective-permute-start(bf16[2,2,128,128]{3,2,1,0:T(8,128)(2,1)} %param.3), channel_id=1, source_target_pairs={{0,128},{1,129},{2,130},{3,131},{4,132},{5,133},{6,134},{7,135},{8... | collective-permute-start | bytes 393224 | tf_op jit(solution)/shard_map/ppermute | solution.py:15
  20.5 1.2 copy-start
  23.3 0.9 copy-start.2
  25.5 24.0 %collective-permute-start.5 = (bf16[2,1,128,128]{3,2,1,0:T(8,128)(2,1)S(1)}, bf16[2,1,128,128]{3,2,1,0:T(8,128)(2,1)S(1)}, u32[]{:S(2)}, u32[]{:S(2)}) collective-permute-start(bf16[2,1,128,128]{3,2,1,0:T(8,128)(2,1)S(1)} %get-tuple-element.60), channel_id=1, source_target_pairs={{0,1},{1,2},{2,3},{3,4},{4,5},{5,6},{6,7},{7,8},{8,9},{9,10},{10,1... | collective-permute-start | bytes 196616 | tf_op jit(solution)/shard_map/ppermute | solution.py:15
  29.2 20.4 %collective-permute-start.6 = (bf16[2,1,128,128]{3,2,1,0:T(8,128)(2,1)S(1)}, bf16[2,1,128,128]{3,2,1,0:T(8,128)(2,1)S(1)}, u32[]{:S(2)}, u32[]{:S(2)}) collective-permute-start(bf16[2,1,128,128]{3,2,1,0:T(8,128)(2,1)S(1)} %get-tuple-element.60), channel_id=1, source_target_pairs={{128,1},{129,2},{130,3},{131,4},{132,5},{133,6},{134,7},{135,8},{1... | collective-permute-start | bytes 196616 | tf_op jit(solution)/shard_map/ppermute | solution.py:15
  30.5 19.0 %collective-permute-start.8 = (bf16[2,1,128,128]{3,2,1,0:T(8,128)(2,1)S(1)}, bf16[2,1,128,128]{3,2,1,0:T(8,128)(2,1)S(1)}, u32[]{:S(2)}, u32[]{:S(2)}) collective-permute-start(bf16[2,1,128,128]{3,2,1,0:T(8,128)(2,1)S(1)} %get-tuple-element.61), channel_id=1, source_target_pairs={{1,0},{2,1},{3,2},{4,3},{5,4},{6,5},{7,6},{8,7},{9,8},{10,9},{11,1... | collective-permute-start | bytes 196616 | tf_op jit(solution)/shard_map/ppermute | solution.py:15
  32.7 16.9 %collective-permute-start.9 = (bf16[2,1,128,128]{3,2,1,0:T(8,128)(2,1)S(1)}, bf16[2,1,128,128]{3,2,1,0:T(8,128)(2,1)S(1)}, u32[]{:S(2)}, u32[]{:S(2)}) collective-permute-start(bf16[2,1,128,128]{3,2,1,0:T(8,128)(2,1)S(1)} %get-tuple-element.61), channel_id=1, source_target_pairs={{129,0},{130,1},{131,2},{132,3},{133,4},{134,5},{135,6},{136,7},{1... | collective-permute-start | bytes 196616 | tf_op jit(solution)/shard_map/ppermute | solution.py:15
  34.0 15.6 %collective-permute-start.7 = (bf16[2,2,128,128]{3,2,1,0:T(8,128)(2,1)S(1)}, bf16[2,2,128,128]{3,2,1,0:T(8,128)(2,1)S(1)}, u32[]{:S(2)}, u32[]{:S(2)}) collective-permute-start(bf16[2,2,128,128]{3,2,1,0:T(8,128)(2,1)S(1)} %bitcast.124), channel_id=1, source_target_pairs={{128,0},{129,1},{130,2},{131,3},{132,4},{133,5},{134,6},{135,7},{1... | collective-permute-start | bytes 393224 | tf_op jit(solution)/shard_map/ppermute | solution.py:15
  39.1 34.1 %all-to-all-start = ((f32[128,8,432]{0,2,1:T(8,128)}), f32[128,8,432]{0,2,1:T(8,128)S(1)}, u32[]{:S(2)}, u32[]{:S(2)}) async-start(f32[128,8,432]{0,2,1:T(8,128)} %bitcast.128), calls=%async_computation | async-start | bytes 3538944 | tf_op jit(solution)/shard_map/all_to_all | solution.py:61
  75.7 48.7 %all-to-all-start.1 = ((f32[128,1,432]{2,1,0:T(1,128)}), f32[128,1,432]{2,1,0:T(1,128)S(1)}, u32[]{:S(2)}, u32[]{:S(2)}) async-start(f32[128,1,432]{2,1,0:T(1,128)} %copy.10), calls=%async_computation.1 | async-start | bytes 524288 | tf_op jit(solution)/shard_map/all_to_all | solution.py:62

commit v8 on v7

--- a/solution.py
+++ b/solution.py
@@ -65,16 +65,32 @@
 
 def local(video, kernel, cotangent):
     frames, height, width, chans = video.shape
+    both = jnp.concatenate([video, cotangent], axis=-1)
+    later = shifted(both, -1, 0)
+    col_video = jnp.concatenate([shifted(video, 1, 0), video, later[..., :chans]], axis=0)
+    col_grad = jnp.concatenate([cotangent, later[..., chans:]], axis=0)
+    flat_video = col_video.reshape(-1, width, chans)
+    cut = flat_video.shape[0]
+
+    def payload(edge):
+        return jnp.concatenate([flat_video, edge.reshape(-1, width, chans)], axis=0)
+
+    def unpacked(got):
+        return got[:cut].reshape(col_video.shape), got[cut:].reshape(2 * frames, 1, width, chans)
+
+    above_video, above_grad = unpacked(shifted(payload(col_grad[:, -1:]), 0, 1))
+    below_video, below_grad = unpacked(shifted(payload(col_grad[:, :1]), 0, -1))
+    footage = jnp.concatenate([above_video, col_video, below_video], axis=1)
+    grad_in = jnp.concatenate([above_grad, col_grad, below_grad], axis=1)
     forward_mat = kernel.reshape(3, 3, 3 * chans, chans)
-    extended = haloed(video, 1)
-    patches = make_patches(extended)
-    pre = apply_taps(patches, forward_mat)
+    pre = apply_taps(make_patches(footage), forward_mat)
     sig = 1.0 / (1.0 + jnp.exp(-pre))
-    activated = (pre * sig).astype(jnp.bfloat16).reshape(frames, height, width, chans)
-    grad_flat = cotangent.reshape(frames * height * width, chans).astype(jnp.float32)
+    wide_frames, wide_rows = 2 * frames, height + 2
+    grid = (wide_frames, wide_rows, width, chans)
+    activated = (pre * sig).astype(jnp.bfloat16).reshape(grid)[:frames, 1 : height + 1]
+    grad_flat = grad_in.reshape(-1, chans).astype(jnp.float32)
     pre_grad = (grad_flat * sig * (1.0 + pre * (1.0 - sig))).astype(jnp.bfloat16)
-    pre_grid = pre_grad.reshape(frames, height, width, chans)
-    grad_ext = haloed(pre_grid, -1)
+    grad_ext = pre_grad.reshape(grid)
     flipped = jnp.transpose(kernel[::-1, ::-1, ::-1], (0, 1, 2, 4, 3)).reshape(
         3, 3, 3 * chans, chans
     )
@@ -83,11 +99,13 @@
         .astype(jnp.bfloat16)
         .reshape(frames, height, width, chans)
     )
+    own_grad = grad_ext[:frames, 1 : height + 1].reshape(frames * height * width, chans)
+    own_patches = make_patches(footage[: frames + 2, height - 1 : 2 * height + 1])
     blocks = [
         lax.dot_general(
-            pre_grad, piece, (((0,), (0,)), ((), ())), preferred_element_type=jnp.float32
+            own_grad, piece, (((0,), (0,)), ((), ())), preferred_element_type=jnp.float32
         )
-        for piece in patches
+        for piece in own_patches
     ]
     partial_grad = jnp.concatenate(blocks, axis=1)
     kernel_grad = exchanged_scatter(partial_grad)

time: 126 us -> 150 us (1.19)
  local copies, waits for them, and re-layouts: 10.7 us -> 31.3 us
  starting transfers between devices: 59.5 us -> 45.9 us
  matrix products: 8.39 us -> 17 us
  other arithmetic: 5.02 us -> 11.3 us
  waiting for transfers between devices: 40.5 us -> 42.2 us
    ppermute x10 -> x4, starting transfers between devices: 23.7 us -> 12.3 us  [shifted(): return lax.ppermute(x, ('tm', 'rows'), pairs)]
    concatenate x5 -> x9, local copies, waits for them, and re-layouts: 0.08 us -> 8.21 us  [make_patches(): jnp.concatenate(parts, axis=-1).reshape(frames * height * width, 3 * chans)]
    slice x4 -> x10, local copies, waits for them, and re-layouts: 2.98 us -> 9.79 us  [make_patches(): parts = [wide[a:a + frames, b:b + height, c:c + width] for c in range(3)]]
    ppermute x10 -> x4, waiting for transfers between devices: 1.99 us -> 8.16 us  [shifted(): return lax.ppermute(x, ('tm', 'rows'), pairs)]
    dot_general x16, matrix products: 5.61 us -> 11.5 us  [apply_taps(): jnp.dot(patches[index], kmat[index // 3, index % 3], preferred_element_ty...]
    all_to_all x1, waiting for transfers between devices: 18.9 us -> 13.5 us  [exchanged_scatter(): x = lax.all_to_all(x, 'tm', 1, 1).sum(axis=1)]
    concatenate x11 -> x14, other arithmetic: 2.99 us -> 6.27 us  [make_patches(): jnp.concatenate(parts, axis=-1).reshape(frames * height * width, 3 * chans)]
    reshape x0 -> x3, local copies, waits for them, and re-layouts: none -> 3.15 us  [the longest x2 1.83 us: unpacked(): got[cut:].reshape(2 * frames, 1, width, chans)]
  transfers between devices with their start and end apart: 12 -> 6, of which waited for: 3 -> 5; matrix products, arithmetic and copies ran while one was open for 11% -> 11% of each run, Pallas kernels for 0% -> 0%
where the time goes in v8:
time: 150 us; the launch traced here: 149 us
  starting transfers between devices  45.9 us (31%)
  waiting for transfers between devices  42.2 us (28%)
  local copies, waits for them, and re-layouts  31.3 us (21%)
  matrix products  17 us (11%)
  other arithmetic  11.3 us (8%)
  between operations  1.62 us (1%)
    all_to_all x1, starting transfers between devices, exchanged_scatter(): x = lax.all_to_all(x, 'rows', 0, 0).sum(axis=0)  25.1 us
    all_to_all x1, waiting for transfers between devices, exchanged_scatter(): x = lax.all_to_all(x, 'rows', 0, 0).sum(axis=0)  20.5 us
    all_to_all x1, waiting for transfers between devices, exchanged_scatter(): x = lax.all_to_all(x, 'tm', 1, 1).sum(axis=1)  13.5 us
    ppermute x4, starting transfers between devices, shifted(): return lax.ppermute(x, ('tm', 'rows'), pairs)  12.3 us
    dot_general x16, matrix products, apply_taps(): jnp.dot(patches[index], kmat[index // 3, index % 3], preferred_element_ty...  11.5 us
    slice x10, local copies, waits for them, and re-layouts, make_patches(): parts = [wide[a:a + frames, b:b + height, c:c + width] for c in range(3)]  9.79 us
    all_to_all x1, starting transfers between devices, exchanged_scatter(): x = lax.all_to_all(x, 'tm', 1, 1).sum(axis=1)  8.48 us
    concatenate x9, local copies, waits for them, and re-layouts, make_patches(): jnp.concatenate(parts, axis=-1).reshape(frames * height * width, 3 * chans)  8.21 us
  transfers between devices with their start and end apart: 6, of which 5 were waited for; matrix products, arithmetic and copies ran while one was open for 11% of the time, Pallas kernels for 0%

profile of v8, /device:TPU:56, one launch (start us, length us, event | category | flops | bytes accessed | tf_op | source)
XLA Modules:
  0.0 149.3 jit_solution(12563414642589527808)
XLA Ops:
  0.6 1.0 pad_maximum_fusion.25
  1.7 1.3 collective-permute-start.1
  3.0 3.0 %collective-permute-start = (bf16[2,2,128,128]{3,2,1,0:T(8,128)(2,1)}, bf16[2,2,128,128]{3,2,1,0:T(8,128)(2,1)S(1)}, u32[]{:S(2)}, u32[]{:S(2)}) collective-permute-start(bf16[2,2,128,128]{3,2,1,0:T(8,128)(2,1)} %param.3), channel_id=1, source_target_pairs={{0,128},{1,129},{2,130},{3,131},{4,132},{5,133},{6,134},{7,135},{8... | collective-permute-start | bytes 393224 | tf_op jit(solution)/shard_map/ppermute | solution.py:15
  6.1 1.0 fusion.59
  7.3 1.1 pad_maximum_fusion.12
  8.3 3.2 %collective-permute-start.3 = (bf16[16,128,128]{2,1,0:T(8,128)(2,1)}, bf16[16,128,128]{2,1,0:T(8,128)(2,1)}, u32[]{:S(2)}, u32[]{:S(2)}) collective-permute-start(bf16[16,128,128]{2,1,0:T(8,128)(2,1)} %get-tuple-element.85), channel_id=1, source_target_pairs={{1,0},{2,1},{3,2},{4,3},{5,4},{6,5},{7,6},{8,7},{9,8},{10,9},{11,1... | collective-permute-start | bytes 1572872 | tf_op jit(solution)/shard_map/ppermute | solution.py:15
  11.6 4.7 %collective-permute-start.2 = (bf16[16,128,128]{2,1,0:T(8,128)(2,1)}, bf16[16,128,128]{2,1,0:T(8,128)(2,1)}, u32[]{:S(2)}, u32[]{:S(2)}) collective-permute-start(bf16[16,128,128]{2,1,0:T(8,128)(2,1)} %get-tuple-element.84), channel_id=1, source_target_pairs={{0,1},{1,2},{2,3},{3,4},{4,5},{5,6},{6,7},{7,8},{8,9},{9,10},{10,1... | collective-permute-start | bytes 1572872 | tf_op jit(solution)/shard_map/ppermute | solution.py:15
  16.3 1.4 copy.49
  17.8 7.4 %collective-permute-done.3 = bf16[16,128,128]{2,1,0:T(8,128)(2,1)} collective-permute-done((bf16[16,128,128]{2,1,0:T(8,128)(2,1)}, bf16[16,128,128]{2,1,0:T(8,128)(2,1)}, u32[]{:S(2)}, u32[]{:S(2)}) %collective-permute-start.3) | collective-permute-done | bytes 524320 | tf_op jit(solution)/shard_map/ppermute | solution.py:15
  25.2 1.0 slice.485
  26.9 1.0 slice.484
  28.1 1.5 pad_slice_fusion.39
  29.8 1.3 pad_slice_fusion.38
  31.9 0.9 slice_bitcast_fusion
  32.8 0.9 slice_bitcast_fusion.1
  41.4 1.9 %fusion.11 = (bf16[2048,128]{1,0:T(8,128)(2,1)}, bf16[2048,128]{1,0:T(8,128)(2,1)}) fusion(bf16[4,4,128,128]{3,2,1,0:T(8,128)(2,1)S(1)} %pad_maximum_fusion.13, f32[2048,128]{1,0:T(8,128)S(1)} %convolution_add_fusion.1, bf16[2048,384]{1,0:T(8,128)(2,1)S(1)} %bitcast.233, bf16[3,3,384,128]{3,2,1,0:T(8,128)(2,1)S(1)} %bitcast.232), kind=kOutput, calls=%fused_computation.65 | convolution fusion | flops 204734464 | bytes 4292608 | tf_op jit(solution)/shard_map/dot_general | solution.py:51
  43.4 1.3 copy.46
  44.7 2.0 %pad_slice_fusion.1 = (bf16[2,2,128,128]{2,3,1,0:T(8,128)(2,1)}, bf16[2,2,128,128]{2,3,1,0:T(8,128)(2,1)S(1)}, bf16[2,2,128,128]{2,3,1,0:T(8,128)(2,1)}, bf16[2,...) fusion(bf16[4,4,128,128]{2,3,1,0:T(8,128)(2,1)S(1)} %copy.46), kind=kLoop, calls=%fused_computation.1 | loop fusion | bytes 3276800 | tf_op jit(solution)/shard_map/slice | solution.py:41
  46.7 1.0 fusion.76
  47.7 1.2 pad_slice_fusion.21
  48.8 1.0 fusion.72
  49.8 1.1 pad_slice_fusion.20
  50.9 1.6 %slice.504 = bf16[2,2,128,128]{3,2,1,0:T(8,128)(2,1)} slice(bf16[4,4,128,128]{3,2,1,0:T(8,128)(2,1)} %bitcast.256), slice={[0:2], [1:3], [0:128], [0:128]} | slice | bytes 262144 | tf_op jit(solution)/shard_map/slice | solution.py:90
  52.9 0.9 copy.51
  53.9 0.9 copy.53
  54.9 1.1 copy.55
  56.0 0.9 copy.57
  57.0 1.0 copy.59
  58.0 1.4 fusion.9
  59.5 1.4 fusion.8
  63.6 1.7 %copy.66 = f32[128,3456]{0,1:T(8,128)} copy(f32[128,3456]{1,0:T(8,128)S(1)} %fusion.1) | data formatting | bytes 3538944 | tf_op jit(solution)/shard_map/concatenate | solution.py:110
  65.3 8.5 %all-to-all-start = ((f32[128,8,432]{0,2,1:T(8,128)}), f32[128,8,432]{0,2,1:T(8,128)S(1)}, u32[]{:S(2)}, u32[]{:S(2)}) async-start(f32[128,8,432]{0,2,1:T(8,128)} %bitcast.70), calls=%async_computation | async-start | bytes 3538944 | tf_op jit(solution)/shard_map/all_to_all | solution.py:61
  73.8 1.1 pad_maximum_fusion.22
  74.8 0.9 copy.61
  75.8 1.1 pad_maximum_fusion.23
  76.9 0.9 copy.63
  77.8 1.8 %pad_maximum_fusion.24 = bf16[2,2,128,384]{2,3,1,0:T(8,128)(2,1)} fusion(bf16[2,2,128,128]{2,3,1,0:T(8,128)(2,1)} %get-tuple-element.71, bf16[2,2,128,128]{2,3,1,0:T(8,128)(2,1)} %get-tuple-element.72, bf16[2,2,128,128]{2,3,1,0:T(8,128)(2,1)} %get-tuple-element.55), kind=kLoop, calls=%fused_computation.86 | loop fusion | flops 1179648 | bytes 786432 | tf_op jit(solution)/shard_map/concatenate | solution.py:43
  79.6 1.2 copy.65
  81.1 1.3 convolution_add_fusion.15
  83.0 1.0 convolution_add_fusion.12
  84.0 13.5 %all-to-all-done = f32[128,8,432]{0,2,1:T(8,128)S(1)} async-done(((f32[128,8,432]{0,2,1:T(8,128)}), f32[128,8,432]{0,2,1:T(8,128)S(1)}, u32[]{:S(2)}, u32[]{:S(2)}) %all-to-all-start) | async-done | bytes 1769504 | tf_op jit(solution)/shard_map/all_to_all | solution.py:61
  97.5 0.8 reduce_sum.18
  98.3 1.9 %copy.67 = f32[128,1,432]{2,1,0:T(1,128)} copy(f32[128,1,432]{0,2,1:T(8,128)} %bitcast.244) | data formatting | bytes 442368 | tf_op jit(solution)/shard_map/all_to_all | solution.py:62
  100.1 25.1 %all-to-all-start.1 = ((f32[128,1,432]{2,1,0:T(1,128)}), f32[128,1,432]{2,1,0:T(1,128)S(1)}, u32[]{:S(2)}, u32[]{:S(2)}) async-start(f32[128,1,432]{2,1,0:T(1,128)} %copy.67), calls=%async_computation.1 | async-start | bytes 524288 | tf_op jit(solution)/shard_map/all_to_all | solution.py:62
  125.3 1.2 convolution_add_fusion.11
  127.0 0.9 fusion
  128.0 20.5 %all-to-all-done.1 = f32[128,1,432]{2,1,0:T(1,128)S(1)} async-done(((f32[128,1,432]{2,1,0:T(1,128)}), f32[128,1,432]{2,1,0:T(1,128)S(1)}, u32[]{:S(2)}, u32[]{:S(2)}) %all-to-all-start.1) | async-done | bytes 221216 | tf_op jit(solution)/shard_map/all_to_all | solution.py:62
  148.5 0.8 reduce_sum.19
  (152 shorter events, 13.9 us)
Async XLA Ops:
  0.6 6.6 %copy-start.2 = (bf16[2,2,128,128]{3,2,1,0:T(8,128)(2,1)S(1)}, bf16[2,2,128,128]{3,2,1,0:T(8,128)(2,1)}, u32[]{:S(2)}) copy-start(bf16[2,2,128,128]{3,2,1,0:T(8,128)(2,1)} %param.3) | copy-start | bytes 393220
  1.7 4.4 %collective-permute-start.1 = (bf16[2,2,128,256]{3,2,1,0:T(8,128)(2,1)S(1)}, bf16[2,2,128,256]{3,2,1,0:T(8,128)(2,1)S(1)}, u32[]{:S(2)}, u32[]{:S(2)}) collective-permute-start(bf16[2,2,128,256]{3,2,1,0:T(8,128)(2,1)S(1)} %pad_maximum_fusion.25), channel_id=1, source_target_pairs={{128,0},{129,1},{130,2},{131,3},{132,4},{133,5},{134,6},{135,7},{1... | collective-permute-start | bytes 786440 | tf_op jit(solution)/shard_map/ppermute | solution.py:15
  3.0 4.2 %collective-permute-start = (bf16[2,2,128,128]{3,2,1,0:T(8,128)(2,1)}, bf16[2,2,128,128]{3,2,1,0:T(8,128)(2,1)S(1)}, u32[]{:S(2)}, u32[]{:S(2)}) collective-permute-start(bf16[2,2,128,128]{3,2,1,0:T(8,128)(2,1)} %param.3), channel_id=1, source_target_pairs={{0,128},{1,129},{2,130},{3,131},{4,132},{5,133},{6,134},{7,135},{8... | collective-permute-start | bytes 393224 | tf_op jit(solution)/shard_map/ppermute | solution.py:15
  6.1 21.8 %copy-start.5 = (bf16[2,2,128,128]{3,2,1,0:T(8,128)(2,1)}, bf16[2,2,128,128]{3,2,1,0:T(8,128)(2,1)S(1)}, u32[]{:S(2)}) copy-start(bf16[2,2,128,128]{3,2,1,0:T(8,128)(2,1)S(1)} %get-tuple-element.89) | copy-start | bytes 393220
  6.1 10.2 %copy-start = (bf16[3,3,3,128,128]{4,3,2,1,0:T(8,128)(2,1)S(1)}, bf16[3,3,3,128,128]{4,3,2,1,0:T(8,128)(2,1)}, u32[]{:S(2)}) copy-start(bf16[3,3,3,128,128]{4,3,2,1,0:T(8,128)(2,1)} %param.4) | copy-start | bytes 2654212
  7.2 20.9 %copy-start.16 = (bf16[2,2,128,128]{3,2,1,0:T(8,128)(2,1)}, bf16[2,2,128,128]{3,2,1,0:T(8,128)(2,1)S(1)}, u32[]{:S(2)}) copy-start(bf16[2,2,128,128]{3,2,1,0:T(8,128)(2,1)S(1)} %collective-permute-done) | copy-start | bytes 393220
  8.3 16.8 %collective-permute-start.3 = (bf16[16,128,128]{2,1,0:T(8,128)(2,1)}, bf16[16,128,128]{2,1,0:T(8,128)(2,1)}, u32[]{:S(2)}, u32[]{:S(2)}) collective-permute-start(bf16[16,128,128]{2,1,0:T(8,128)(2,1)} %get-tuple-element.85), channel_id=1, source_target_pairs={{1,0},{2,1},{3,2},{4,3},{5,4},{6,5},{7,6},{8,7},{9,8},{10,9},{11,1... | collective-permute-start | bytes 1572872 | tf_op jit(solution)/shard_map/ppermute | solution.py:15
  11.6 15.3 %collective-permute-start.2 = (bf16[16,128,128]{2,1,0:T(8,128)(2,1)}, bf16[16,128,128]{2,1,0:T(8,128)(2,1)}, u32[]{:S(2)}, u32[]{:S(2)}) collective-permute-start(bf16[16,128,128]{2,1,0:T(8,128)(2,1)} %get-tuple-element.84), channel_id=1, source_target_pairs={{0,1},{1,2},{2,3},{3,4},{4,5},{5,6},{6,7},{7,8},{8,9},{9,10},{10,1... | collective-permute-start | bytes 1572872 | tf_op jit(solution)/shard_map/ppermute | solution.py:15
  29.7 1.3 copy-start.3
  29.7 1.3 copy-start.6
  29.8 1.3 copy-start.17
  31.5 2.2 %copy-start.13 = (bf16[2,2,128,128]{3,2,1,0:T(8,128)(2,1)S(1)}, bf16[2,2,128,128]{3,2,1,0:T(8,128)(2,1)}, u32[]{:S(2)}) copy-start(bf16[2,2,128,128]{3,2,1,0:T(8,128)(2,1)} %param.5) | copy-start | bytes 393220
  31.6 2.2 %copy-start.15 = (bf16[2,2,128,128]{3,2,1,0:T(8,128)(2,1)S(1)}, bf16[2,2,128,128]{3,2,1,0:T(8,128)(2,1)}, u32[]{:S(2)}) copy-start(bf16[2,2,128,128]{3,2,1,0:T(8,128)(2,1)} %copy-done.14) | copy-start | bytes 393220
  33.8 1.2 copy-start.1
  49.8 3.0 %copy-start.29 = (bf16[2,2,128,128]{2,3,1,0:T(8,128)(2,1)S(1)}, bf16[2,2,128,128]{2,3,1,0:T(8,128)(2,1)}, u32[]{:S(2)}) copy-start(bf16[2,2,128,128]{2,3,1,0:T(8,128)(2,1)} %get-tuple-element.57) | copy-start | bytes 393220
  49.8 3.0 %copy-start.30 = (bf16[2,2,128,128]{2,3,1,0:T(8,128)(2,1)S(1)}, bf16[2,2,128,128]{2,3,1,0:T(8,128)(2,1)}, u32[]{:S(2)}) copy-start(bf16[2,2,128,128]{2,3,1,0:T(8,128)(2,1)} %get-tuple-element.58) | copy-start | bytes 393220
  49.8 3.0 %copy-start.34 = (bf16[2,2,128,128]{2,3,1,0:T(8,128)(2,1)S(1)}, bf16[2,2,128,128]{2,3,1,0:T(8,128)(2,1)}, u32[]{:S(2)}) copy-start(bf16[2,2,128,128]{2,3,1,0:T(8,128)(2,1)} %get-tuple-element.79) | copy-start | bytes 393220
  52.5 1.3 copy-start.26
  52.5 1.3 copy-start.27
  52.5 1.3 copy-start.33
  52.8 2.0 %copy-start.24 = (bf16[2,2,128,128]{2,3,1,0:T(8,128)(2,1)S(1)}, bf16[2,2,128,128]{2,3,1,0:T(8,128)(2,1)}, u32[]{:S(2)}) copy-start(bf16[2,2,128,128]{2,3,1,0:T(8,128)(2,1)} %get-tuple-element.61) | copy-start | bytes 393220
  52.8 2.0 %copy-start.25 = (bf16[2,2,128,128]{2,3,1,0:T(8,128)(2,1)S(1)}, bf16[2,2,128,128]{2,3,1,0:T(8,128)(2,1)}, u32[]{:S(2)}) copy-start(bf16[2,2,128,128]{2,3,1,0:T(8,128)(2,1)} %get-tuple-element.62) | copy-start | bytes 393220
  52.8 2.0 %copy-start.32 = (bf16[2,2,128,128]{2,3,1,0:T(8,128)(2,1)S(1)}, bf16[2,2,128,128]{2,3,1,0:T(8,128)(2,1)}, u32[]{:S(2)}) copy-start(bf16[2,2,128,128]{2,3,1,0:T(8,128)(2,1)} %get-tuple-element.77) | copy-start | bytes 393220
  53.8 2.2 %copy-start.22 = (bf16[2,2,128,128]{2,3,1,0:T(8,128)(2,1)S(1)}, bf16[2,2,128,128]{2,3,1,0:T(8,128)(2,1)}, u32[]{:S(2)}) copy-start(bf16[2,2,128,128]{2,3,1,0:T(8,128)(2,1)} %get-tuple-element.63) | copy-start | bytes 393220
  53.8 2.2 %copy-start.23 = (bf16[2,2,128,128]{2,3,1,0:T(8,128)(2,1)S(1)}, bf16[2,2,128,128]{2,3,1,0:T(8,128)(2,1)}, u32[]{:S(2)}) copy-start(bf16[2,2,128,128]{2,3,1,0:T(8,128)(2,1)} %get-tuple-element.64) | copy-start | bytes 393220
  53.8 2.2 %copy-start.31 = (bf16[2,2,128,128]{2,3,1,0:T(8,128)(2,1)S(1)}, bf16[2,2,128,128]{2,3,1,0:T(8,128)(2,1)}, u32[]{:S(2)}) copy-start(bf16[2,2,128,128]{2,3,1,0:T(8,128)(2,1)} %get-tuple-element.76) | copy-start | bytes 393220
  54.8 2.2 %copy-start.20 = (bf16[2,2,128,128]{2,3,1,0:T(8,128)(2,1)S(1)}, bf16[2,2,128,128]{2,3,1,0:T(8,128)(2,1)}, u32[]{:S(2)}) copy-start(bf16[2,2,128,128]{2,3,1,0:T(8,128)(2,1)} %get-tuple-element.65) | copy-start | bytes 393220
  54.8 2.2 %copy-start.21 = (bf16[2,2,128,128]{2,3,1,0:T(8,128)(2,1)S(1)}, bf16[2,2,128,128]{2,3,1,0:T(8,128)(2,1)}, u32[]{:S(2)}) copy-start(bf16[2,2,128,128]{2,3,1,0:T(8,128)(2,1)} %get-tuple-element.66) | copy-start | bytes 393220
  54.8 2.2 %copy-start.28 = (bf16[2,2,128,128]{2,3,1,0:T(8,128)(2,1)S(1)}, bf16[2,2,128,128]{2,3,1,0:T(8,128)(2,1)}, u32[]{:S(2)}) copy-start(bf16[2,2,128,128]{2,3,1,0:T(8,128)(2,1)} %get-tuple-element.75) | copy-start | bytes 393220
  58.0 3.0 %copy-start.19 = (bf16[2048,128]{1,0:T(8,128)(2,1)S(1)}, bf16[2048,128]{1,0:T(8,128)(2,1)}, u32[]{:S(2)}) copy-start(bf16[2048,128]{1,0:T(8,128)(2,1)} %get-tuple-element.23) | copy-start | bytes 1572868
  58.0 3.0 %copy-start.39 = (bf16[2,2,128,128]{3,2,1,0:T(8,128)(2,1)S(1)}, bf16[2,2,128,128]{3,2,1,0:T(8,128)(2,1)}, u32[]{:S(2)}) copy-start(bf16[2,2,128,128]{3,2,1,0:T(8,128)(2,1)} %get-tuple-element.27) | copy-start | bytes 393220
  58.0 3.0 %copy-start.49 = (bf16[2,2,128,128]{3,2,1,0:T(8,128)(2,1)S(1)}, bf16[2,2,128,128]{3,2,1,0:T(8,128)(2,1)}, u32[]{:S(2)}) copy-start(bf16[2,2,128,128]{3,2,1,0:T(8,128)(2,1)} %get-tuple-element.41) | copy-start | bytes 393220
  58.0 3.0 %copy-start.50 = (bf16[2,2,128,128]{3,2,1,0:T(8,128)(2,1)S(1)}, bf16[2,2,128,128]{3,2,1,0:T(8,128)(2,1)}, u32[]{:S(2)}) copy-start(bf16[2,2,128,128]{3,2,1,0:T(8,128)(2,1)} %get-tuple-element.42) | copy-start | bytes 393220
  58.0 3.3 %copy-start.38 = (bf16[2,2,128,128]{3,2,1,0:T(8,128)(2,1)S(1)}, bf16[2,2,128,128]{3,2,1,0:T(8,128)(2,1)}, u32[]{:S(2)}) copy-start(bf16[2,2,128,128]{3,2,1,0:T(8,128)(2,1)} %get-tuple-element.97) | copy-start | bytes 393220
  58.0 3.3 %copy-start.43 = (bf16[2,2,128,128]{3,2,1,0:T(8,128)(2,1)S(1)}, bf16[2,2,128,128]{3,2,1,0:T(8,128)(2,1)}, u32[]{:S(2)}) copy-start(bf16[2,2,128,128]{3,2,1,0:T(8,128)(2,1)} %get-tuple-element.43) | copy-start | bytes 393220
  58.0 3.3 %copy-start.44 = (bf16[2,2,128,128]{3,2,1,0:T(8,128)(2,1)S(1)}, bf16[2,2,128,128]{3,2,1,0:T(8,128)(2,1)}, u32[]{:S(2)}) copy-start(bf16[2,2,128,128]{3,2,1,0:T(8,128)(2,1)} %get-tuple-element.44) | copy-start | bytes 393220
  59.5 2.1 %copy-start.4 = (bf16[2,2,128,128]{3,2,1,0:T(8,128)(2,1)S(1)}, bf16[2,2,128,128]{3,2,1,0:T(8,128)(2,1)}, u32[]{:S(2)}) copy-start(bf16[2,2,128,128]{3,2,1,0:T(8,128)(2,1)} %param.3) | copy-start | bytes 393220
  59.5 2.1 %copy-start.18 = (bf16[2,2,128,128]{3,2,1,0:T(8,128)(2,1)S(1)}, bf16[2,2,128,128]{3,2,1,0:T(8,128)(2,1)}, u32[]{:S(2)}) copy-start(bf16[2,2,128,128]{3,2,1,0:T(8,128)(2,1)} %copy-done.16) | copy-start | bytes 393220
  59.5 2.1 %copy-start.42 = (bf16[2,2,128,128]{3,2,1,0:T(8,128)(2,1)S(1)}, bf16[2,2,128,128]{3,2,1,0:T(8,128)(2,1)}, u32[]{:S(2)}) copy-start(bf16[2,2,128,128]{3,2,1,0:T(8,128)(2,1)} %get-tuple-element.45) | copy-start | bytes 393220
  59.5 2.1 %copy-start.53 = (bf16[2,2,128,128]{3,2,1,0:T(8,128)(2,1)S(1)}, bf16[2,2,128,128]{3,2,1,0:T(8,128)(2,1)}, u32[]{:S(2)}) copy-start(bf16[2,2,128,128]{3,2,1,0:T(8,128)(2,1)} %get-tuple-element.47) | copy-start | bytes 393220
  65.3 32.2 %all-to-all-start = ((f32[128,8,432]{0,2,1:T(8,128)}), f32[128,8,432]{0,2,1:T(8,128)S(1)}, u32[]{:S(2)}, u32[]{:S(2)}) async-start(f32[128,8,432]{0,2,1:T(8,128)} %bitcast.70), calls=%async_computation | async-start | bytes 3538944 | tf_op jit(solution)/shard_map/all_to_all | solution.py:61
  80.8 1.6 %copy-start.8 = (bf16[2,2,128,384]{3,2,1,0:T(8,128)(2,1)S(1)}, bf16[2,2,128,384]{3,2,1,0:T(8,128)(2,1)}, u32[]{:S(2)}) copy-start(bf16[2,2,128,384]{3,2,1,0:T(8,128)(2,1)} %copy.53) | copy-start | bytes 1179652
  80.8 1.9 %copy-start.9 = (bf16[2,2,128,384]{3,2,1,0:T(8,128)(2,1)S(1)}, bf16[2,2,128,384]{3,2,1,0:T(8,128)(2,1)}, u32[]{:S(2)}) copy-start(bf16[2,2,128,384]{3,2,1,0:T(8,128)(2,1)} %copy.55) | copy-start | bytes 1179652
  81.1 1.9 %copy-start.10 = (bf16[2,2,128,384]{3,2,1,0:T(8,128)(2,1)S(1)}, bf16[2,2,128,384]{3,2,1,0:T(8,128)(2,1)}, u32[]{:S(2)}) copy-start(bf16[2,2,128,384]{3,2,1,0:T(8,128)(2,1)} %copy.57) | copy-start | bytes 1179652
  84.0 41.3 %copy-start.7 = (bf16[2,2,128,384]{3,2,1,0:T(8,128)(2,1)S(1)}, bf16[2,2,128,384]{3,2,1,0:T(8,128)(2,1)}, u32[]{:S(2)}) copy-start(bf16[2,2,128,384]{3,2,1,0:T(8,128)(2,1)} %copy.59) | copy-start | bytes 1179652
  98.3 28.2 %copy-start.11 = (bf16[2,2,128,384]{3,2,1,0:T(8,128)(2,1)S(1)}, bf16[2,2,128,384]{3,2,1,0:T(8,128)(2,1)}, u32[]{:S(2)}) copy-start(bf16[2,2,128,384]{3,2,1,0:T(8,128)(2,1)} %copy.61) | copy-start | bytes 1179652
  98.3 28.5 %copy-start.12 = (bf16[2,2,128,384]{3,2,1,0:T(8,128)(2,1)S(1)}, bf16[2,2,128,384]{3,2,1,0:T(8,128)(2,1)}, u32[]{:S(2)}) copy-start(bf16[2,2,128,384]{3,2,1,0:T(8,128)(2,1)} %copy.63) | copy-start | bytes 1179652
  100.1 48.4 %all-to-all-start.1 = ((f32[128,1,432]{2,1,0:T(1,128)}), f32[128,1,432]{2,1,0:T(1,128)S(1)}, u32[]{:S(2)}, u32[]{:S(2)}) async-start(f32[128,1,432]{2,1,0:T(1,128)} %copy.67), calls=%async_computation.1 | async-start | bytes 524288 | tf_op jit(solution)/shard_map/all_to_all | solution.py:62
  (12 other events, 12.0 us)

commit v9 on v1

--- a/solution.py
+++ b/solution.py
@@ -48,6 +48,13 @@
     return total
 
 
+def tm_summed(partial_grad):
+    outs, cols = partial_grad.shape
+    parts = lax.axis_size("tm")
+    x = partial_grad.reshape(outs, parts, cols // parts)
+    return lax.all_to_all(x, "tm", 1, 1).sum(axis=1)
+
+
 def local(video, kernel, cotangent):
     frames, height, width, chans = video.shape
     forward_mat = kernel.reshape(3, 3, 3 * chans, chans)
@@ -59,6 +66,15 @@
     activated = (pre * sig).astype(jnp.bfloat16).reshape(frames, height, width, chans)
     grad_flat = cotangent.reshape(frames * height * width, chans).astype(jnp.float32)
     pre_grad = (grad_flat * sig * (1.0 + pre * (1.0 - sig))).astype(jnp.bfloat16)
+    blocks = [
+        lax.dot_general(
+            pre_grad, piece, (((0,), (0,)), ((), ())), preferred_element_type=jnp.float32
+        )
+        for piece in patches
+    ]
+    summed = tm_summed(jnp.concatenate(blocks, axis=1))
+    summed, pre_grad = lax.optimization_barrier((summed, pre_grad))
+    kernel_grad = lax.all_to_all(summed, "rows", 0, 0).sum(axis=0).reshape(1, -1)
     pre_grid = pre_grad.reshape(frames, height, width, chans)
     later = passed_along(pre_grid, "tm", -1)
     grad_ext = padded(jnp.concatenate([pre_grid, later], axis=0), (("rows", 1),), 1)
@@ -70,15 +86,6 @@
         .astype(jnp.bfloat16)
         .reshape(frames, height, width, chans)
     )
-    blocks = [
-        lax.dot_general(
-            pre_grad, piece, (((0,), (0,)), ((), ())), preferred_element_type=jnp.float32
-        )
-        for piece in patches
-    ]
-    partial_grad = jnp.concatenate(blocks, axis=1)
-    owned = lax.psum_scatter(partial_grad, "tm", scatter_dimension=1, tiled=True)
-    kernel_grad = lax.psum_scatter(owned, "rows", scatter_dimension=0, tiled=True)
     return (activated, input_grad, kernel_grad)
 
 

time: 389 us -> 131 us (0.34)
  the two profiles are of different devices: /device:TPU:56 before, /device:TPU:66 now
where the time goes in v9:
time: 131 us
  starting transfers between devices  41.3 us (32%)
  waiting for transfers between devices  34.2 us (26%)
  blocking collectives  27.2 us (21%)
  matrix products  14.7 us (11%)
  local copies, waits for them, and re-layouts  7.62 us (6%)
  other arithmetic  4.43 us (3%)
    all_to_all x1, blocking collectives, tm_summed(): return lax.all_to_all(x, 'tm', 1, 1).sum(axis=1)  27.2 us
    all_to_all x1, starting transfers between devices, local(): lax.all_to_all(summed, 'rows', 0, 0).sum(axis=0).reshape(1, -1)  24.6 us
    all_to_all x1, waiting for transfers between devices, local(): lax.all_to_all(summed, 'rows', 0, 0).sum(axis=0).reshape(1, -1)  20 us
    dot_general x9, matrix products, local(): lax.dot_general(pre_grad, piece, (((0,), (0,)), ((), ())), preferred_elem...  8.61 us
    ppermute x2, waiting for transfers between devices, passed_along(): return lax.ppermute(x, axis, pairs)  7.07 us
    ppermute x2, waiting for transfers between devices, padded(): lax.ppermute(lax.slice_in_dim(block, block.shape[dim] - width, None, axis...  6.47 us
    ppermute x2, starting transfers between devices, padded(): lax.ppermute(lax.slice_in_dim(block, 0, width, axis=dim), axis, backward)  6.38 us
    ppermute x2, starting transfers between devices, padded(): lax.ppermute(lax.slice_in_dim(block, block.shape[dim] - width, None, axis...  5.84 us
  transfers between devices with their start and end apart: 7, of which 5 were waited for; matrix products, arithmetic and copies ran while one was open for 5% of the time, Pallas kernels for 0%

profile of v9, /device:TPU:66, one launch (start us, length us, event | category | flops | bytes accessed | tf_op | source)
XLA Modules:
  0.0 130.5 jit_solution(9453675103442444166)
XLA Ops:
  0.6 1.9 %collective-permute-start = (bf16[2,2,128,128]{3,2,1,0:T(8,128)(2,1)}, bf16[2,2,128,128]{3,2,1,0:T(8,128)(2,1)S(1)}, u32[]{:S(2)}, u32[]{:S(2)}) collective-permute-start(bf16[2,2,128,128]{3,2,1,0:T(8,128)(2,1)} %param.3), channel_id=1, source_target_pairs={{0,128},{128,256},{256,384},{384,512},{512,640},{640,768},{768,896... | collective-permute-start | bytes 393224 | tf_op jit(solution)/shard_map/ppermute | solution.py:10
  2.6 4.6 %collective-permute-done = bf16[2,2,128,128]{3,2,1,0:T(8,128)(2,1)S(1)} collective-permute-done((bf16[2,2,128,128]{3,2,1,0:T(8,128)(2,1)}, bf16[2,2,128,128]{3,2,1,0:T(8,128)(2,1)S(1)}, u32[]{:S(2)}, u32[]{:S(2)}) %collective-permute-start) | collective-permute-done | bytes 131104 | tf_op jit(solution)/shard_map/ppermute | solution.py:10
  7.1 0.9 constant_dynamic-update-slice_fusion
  8.1 4.5 %collective-permute-start.2 = (bf16[4,1,128,128]{3,2,1,0:T(8,128)(2,1)S(1)}, bf16[4,1,128,128]{3,2,1,0:T(8,128)(2,1)S(1)}, u32[]{:S(2)}, u32[]{:S(2)}) collective-permute-start(bf16[4,1,128,128]{3,2,1,0:T(8,128)(2,1)S(1)} %get-tuple-element.65), channel_id=1, source_target_pairs={{1,0},{2,1},{3,2},{4,3},{5,4},{6,5},{7,6},{8,7},{9,8},{10,9},{11,1... | collective-permute-start | bytes 393224 | tf_op jit(solution)/shard_map/ppermute | solution.py:21
  12.6 1.9 %collective-permute-start.1 = (bf16[4,1,128,128]{3,2,1,0:T(8,128)(2,1)S(1)}, bf16[4,1,128,128]{3,2,1,0:T(8,128)(2,1)S(1)}, u32[]{:S(2)}, u32[]{:S(2)}) collective-permute-start(bf16[4,1,128,128]{3,2,1,0:T(8,128)(2,1)S(1)} %get-tuple-element.64), channel_id=1, source_target_pairs={{0,1},{1,2},{2,3},{3,4},{4,5},{5,6},{6,7},{7,8},{8,9},{9,10},{10,1... | collective-permute-start | bytes 393224 | tf_op jit(solution)/shard_map/ppermute | solution.py:18
  14.5 0.6 collective-permute-done.2
  15.1 6.5 %collective-permute-done.1 = bf16[4,1,128,128]{3,2,1,0:T(8,128)(2,1)S(1)} collective-permute-done((bf16[4,1,128,128]{3,2,1,0:T(8,128)(2,1)S(1)}, bf16[4,1,128,128]{3,2,1,0:T(8,128)(2,1)S(1)}, u32[]{:S(2)}, u32[]{:S(2)}) %collective-permute-start.1) | collective-permute-done | bytes 131104 | tf_op jit(solution)/shard_map/ppermute | solution.py:18
  21.7 0.4 fusion.26
  22.4 0.9 copy-done
  23.7 0.3 convolution_add_fusion.15
  23.9 0.3 convolution_add_fusion.14
  24.3 0.3 convolution_add_fusion.13
  24.6 0.3 convolution_add_fusion.12
  25.2 0.3 convolution_add_fusion.11
  25.5 0.3 convolution_add_fusion.10
  25.8 0.3 convolution_add_fusion.9
  26.1 1.0 fusion.15
  27.1 1.0 convolution_dynamic-update-slice_fusion.8
  28.1 0.9 convolution_dynamic-update-slice_fusion.7
  29.0 0.9 convolution_dynamic-update-slice_fusion.6
  30.0 1.0 convolution_dynamic-update-slice_fusion.5
  30.9 0.9 convolution_dynamic-update-slice_fusion.4
  31.9 1.0 convolution_dynamic-update-slice_fusion.3
  32.9 1.0 convolution_dynamic-update-slice_fusion.2
  33.8 1.0 convolution_dynamic-update-slice_fusion.1
  34.8 1.0 convolution_dynamic-update-slice_fusion
  35.7 2.2 %copy.8 = f32[128,3456]{0,1:T(8,128)S(1)} copy(f32[128,3456]{1,0:T(8,128)} %convolution_dynamic-update-slice_fusion) | data formatting | bytes 3538944 | tf_op jit(solution)/shard_map/concatenate | solution.py:75
  37.9 27.2 %all_to_all.14 = f32[128,8,432]{0,2,1:T(8,128)} all-to-all(f32[128,8,432]{0,2,1:T(8,128)S(1)} %bitcast.128), channel_id=1, replica_groups=mesh['tm'=8,'rows'=128] {'tm'}, dimensions={1} | all-to-all | bytes 3538944 | tf_op jit(solution)/shard_map/all_to_all | solution.py:55
  65.2 1.6 %reduce_sum.18 = f32[128,432]{0,1:T(8,128)S(1)} reduce(f32[128,8,432]{0,2,1:T(8,128)} %all_to_all.14, f32[]{:T(128)} %constant.6.clone.1), dimensions={1}, to_apply=%region_0.1 | reduce | flops 387072 | bytes 1990660 | tf_op jit(solution)/shard_map/reduce_sum | solution.py:55
  66.8 2.5 %collective-permute-start.3 = (bf16[2,2,128,128]{3,2,1,0:T(8,128)(2,1)S(1)}, bf16[2,2,128,128]{3,2,1,0:T(8,128)(2,1)S(1)}, u32[]{:S(2)}, u32[]{:S(2)}) collective-permute-start(bf16[2,2,128,128]{3,2,1,0:T(8,128)(2,1)S(1)} %bitcast.123), channel_id=1, source_target_pairs={{128,0},{256,128},{384,256},{512,384},{640,512},{768,640},{896,768... | collective-permute-start | bytes 393224 | tf_op jit(solution)/shard_map/ppermute | solution.py:10
  69.3 2.5 %collective-permute-done.3 = bf16[2,2,128,128]{3,2,1,0:T(8,128)(2,1)S(1)} collective-permute-done((bf16[2,2,128,128]{3,2,1,0:T(8,128)(2,1)S(1)}, bf16[2,2,128,128]{3,2,1,0:T(8,128)(2,1)S(1)}, u32[]{:S(2)}, u32[]{:S(2)}) %collective-permute-start.3) | collective-permute-done | bytes 131104 | tf_op jit(solution)/shard_map/ppermute | solution.py:10
  71.8 0.7 fusion.17
  72.5 1.9 %collective-permute-start.5 = (bf16[4,1,128,128]{3,2,1,0:T(8,128)(2,1)}, bf16[4,1,128,128]{3,2,1,0:T(8,128)(2,1)S(1)}, u32[]{:S(2)}, u32[]{:S(2)}) collective-permute-start(bf16[4,1,128,128]{3,2,1,0:T(8,128)(2,1)} %get-tuple-element.56), channel_id=1, source_target_pairs={{1,0},{2,1},{3,2},{4,3},{5,4},{6,5},{7,6},{8,7},{9,8},{10,9},{11,1... | collective-permute-start | bytes 393224 | tf_op jit(solution)/shard_map/ppermute | solution.py:21
  74.4 3.9 %collective-permute-start.4 = (bf16[4,1,128,128]{3,2,1,0:T(8,128)(2,1)S(1)}, bf16[4,1,128,128]{3,2,1,0:T(8,128)(2,1)S(1)}, u32[]{:S(2)}, u32[]{:S(2)}) collective-permute-start(bf16[4,1,128,128]{3,2,1,0:T(8,128)(2,1)S(1)} %get-tuple-element.55), channel_id=1, source_target_pairs={{0,1},{1,2},{2,3},{3,4},{4,5},{5,6},{6,7},{7,8},{8,9},{9,10},{10,1... | collective-permute-start | bytes 393224 | tf_op jit(solution)/shard_map/ppermute | solution.py:18
  78.3 1.4 %copy.9 = bf16[3,3,3,128,128]{3,4,2,1,0:T(8,128)(2,1)S(1)} copy(bf16[3,3,3,128,128]{4,3,2,1,0:T(8,128)(2,1)S(1)} %copy-done) | data formatting | bytes 1769472 | tf_op args[1]
  79.8 0.8 copy.10
  80.6 24.6 %all-to-all-start.1 = ((f32[128,1,432]{2,1,0:T(1,128)}), f32[128,1,432]{2,1,0:T(1,128)S(1)}, u32[]{:S(2)}, u32[]{:S(2)}) async-start(f32[128,1,432]{2,1,0:T(1,128)} %copy.10), calls=%async_computation.1 | async-start | bytes 524288 | tf_op jit(solution)/shard_map/all_to_all | solution.py:77
  105.5 0.4 fusion.25
  106.1 0.3 fusion.22
  106.4 0.3 convolution_add_fusion.7
  106.8 0.3 convolution_add_fusion.6
  107.1 0.3 convolution_add_fusion.5
  107.5 0.3 convolution_add_fusion.4
  107.8 0.3 convolution_add_fusion.3
  108.2 0.3 convolution_add_fusion.2
  108.7 0.9 fusion
  109.7 20.0 %all-to-all-done.1 = f32[128,1,432]{2,1,0:T(1,128)S(1)} async-done(((f32[128,1,432]{2,1,0:T(1,128)}), f32[128,1,432]{2,1,0:T(1,128)S(1)}, u32[]{:S(2)}, u32[]{:S(2)}) %all-to-all-start.1) | async-done | bytes 221216 | tf_op jit(solution)/shard_map/all_to_all | solution.py:77
  129.7 0.8 reduce_sum.19
  (29 shorter events, 2.4 us)
Async XLA Ops:
  0.6 6.5 %collective-permute-start = (bf16[2,2,128,128]{3,2,1,0:T(8,128)(2,1)}, bf16[2,2,128,128]{3,2,1,0:T(8,128)(2,1)S(1)}, u32[]{:S(2)}, u32[]{:S(2)}) collective-permute-start(bf16[2,2,128,128]{3,2,1,0:T(8,128)(2,1)} %param.3), channel_id=1, source_target_pairs={{0,128},{128,256},{256,384},{384,512},{512,640},{640,768},{768,896... | collective-permute-start | bytes 393224 | tf_op jit(solution)/shard_map/ppermute | solution.py:10
  8.1 7.0 %collective-permute-start.2 = (bf16[4,1,128,128]{3,2,1,0:T(8,128)(2,1)S(1)}, bf16[4,1,128,128]{3,2,1,0:T(8,128)(2,1)S(1)}, u32[]{:S(2)}, u32[]{:S(2)}) collective-permute-start(bf16[4,1,128,128]{3,2,1,0:T(8,128)(2,1)S(1)} %get-tuple-element.65), channel_id=1, source_target_pairs={{1,0},{2,1},{3,2},{4,3},{5,4},{6,5},{7,6},{8,7},{9,8},{10,9},{11,1... | collective-permute-start | bytes 393224 | tf_op jit(solution)/shard_map/ppermute | solution.py:21
  12.6 9.0 %collective-permute-start.1 = (bf16[4,1,128,128]{3,2,1,0:T(8,128)(2,1)S(1)}, bf16[4,1,128,128]{3,2,1,0:T(8,128)(2,1)S(1)}, u32[]{:S(2)}, u32[]{:S(2)}) collective-permute-start(bf16[4,1,128,128]{3,2,1,0:T(8,128)(2,1)S(1)} %get-tuple-element.64), channel_id=1, source_target_pairs={{0,1},{1,2},{2,3},{3,4},{4,5},{5,6},{6,7},{7,8},{8,9},{9,10},{10,1... | collective-permute-start | bytes 393224 | tf_op jit(solution)/shard_map/ppermute | solution.py:18
  22.1 1.2 copy-start
  24.2 0.9 copy-start.1
  25.2 0.9 copy-start.2
  66.8 5.0 %collective-permute-start.3 = (bf16[2,2,128,128]{3,2,1,0:T(8,128)(2,1)S(1)}, bf16[2,2,128,128]{3,2,1,0:T(8,128)(2,1)S(1)}, u32[]{:S(2)}, u32[]{:S(2)}) collective-permute-start(bf16[2,2,128,128]{3,2,1,0:T(8,128)(2,1)S(1)} %bitcast.123), channel_id=1, source_target_pairs={{128,0},{256,128},{384,256},{512,384},{640,512},{768,640},{896,768... | collective-permute-start | bytes 393224 | tf_op jit(solution)/shard_map/ppermute | solution.py:10
  72.5 32.8 %collective-permute-start.5 = (bf16[4,1,128,128]{3,2,1,0:T(8,128)(2,1)}, bf16[4,1,128,128]{3,2,1,0:T(8,128)(2,1)S(1)}, u32[]{:S(2)}, u32[]{:S(2)}) collective-permute-start(bf16[4,1,128,128]{3,2,1,0:T(8,128)(2,1)} %get-tuple-element.56), channel_id=1, source_target_pairs={{1,0},{2,1},{3,2},{4,3},{5,4},{6,5},{7,6},{8,7},{9,8},{10,9},{11,1... | collective-permute-start | bytes 393224 | tf_op jit(solution)/shard_map/ppermute | solution.py:21
  74.4 30.9 %collective-permute-start.4 = (bf16[4,1,128,128]{3,2,1,0:T(8,128)(2,1)S(1)}, bf16[4,1,128,128]{3,2,1,0:T(8,128)(2,1)S(1)}, u32[]{:S(2)}, u32[]{:S(2)}) collective-permute-start(bf16[4,1,128,128]{3,2,1,0:T(8,128)(2,1)S(1)} %get-tuple-element.55), channel_id=1, source_target_pairs={{0,1},{1,2},{2,3},{3,4},{4,5},{5,6},{6,7},{7,8},{8,9},{9,10},{10,1... | collective-permute-start | bytes 393224 | tf_op jit(solution)/shard_map/ppermute | solution.py:18
  80.6 49.1 %all-to-all-start.1 = ((f32[128,1,432]{2,1,0:T(1,128)}), f32[128,1,432]{2,1,0:T(1,128)S(1)}, u32[]{:S(2)}, u32[]{:S(2)}) async-start(f32[128,1,432]{2,1,0:T(1,128)} %copy.10), calls=%async_computation.1 | async-start | bytes 524288 | tf_op jit(solution)/shard_map/all_to_all | solution.py:77

commit v10 on v1

--- a/solution.py
+++ b/solution.py
@@ -48,20 +48,32 @@
     return total
 
 
+def exchanged_scatter(partial_grad):
+    outs, cols = partial_grad.shape
+    parts = lax.axis_size("tm")
+    x = partial_grad.reshape(outs, parts, cols // parts)
+    x = lax.all_to_all(x, "tm", 1, 1).sum(axis=1)
+    x = lax.all_to_all(x, "rows", 0, 0).sum(axis=0)
+    return x.reshape(1, -1)
+
+
 def local(video, kernel, cotangent):
     frames, height, width, chans = video.shape
     forward_mat = kernel.reshape(3, 3, 3 * chans, chans)
     earlier = passed_along(video, "tm", 1)
-    extended = padded(jnp.concatenate([earlier, video], axis=0), (("rows", 1),), 1)
+    later = passed_along(jnp.concatenate([video, cotangent], axis=-1), "tm", -1)
+    column = jnp.concatenate([earlier, video, later[..., :chans]], axis=0)
+    extended = padded(column, (("rows", 1),), 1)
     patches = make_patches(extended)
     pre = apply_taps(patches, forward_mat)
     sig = 1.0 / (1.0 + jnp.exp(-pre))
-    activated = (pre * sig).astype(jnp.bfloat16).reshape(frames, height, width, chans)
-    grad_flat = cotangent.reshape(frames * height * width, chans).astype(jnp.float32)
+    own = frames * height * width
+    activated = (pre[:own] * sig[:own]).astype(jnp.bfloat16).reshape(frames, height, width, chans)
+    grad_in = jnp.concatenate([cotangent, later[..., chans:]], axis=0)
+    grad_flat = grad_in.reshape(-1, chans).astype(jnp.float32)
     pre_grad = (grad_flat * sig * (1.0 + pre * (1.0 - sig))).astype(jnp.bfloat16)
-    pre_grid = pre_grad.reshape(frames, height, width, chans)
-    later = passed_along(pre_grid, "tm", -1)
-    grad_ext = padded(jnp.concatenate([pre_grid, later], axis=0), (("rows", 1),), 1)
+    pre_grid = pre_grad.reshape(2 * frames, height, width, chans)
+    grad_ext = padded(pre_grid, (("rows", 1),), 1)
     flipped = jnp.transpose(kernel[::-1, ::-1, ::-1], (0, 1, 2, 4, 3)).reshape(
         3, 3, 3 * chans, chans
     )
@@ -72,13 +84,12 @@
     )
     blocks = [
         lax.dot_general(
-            pre_grad, piece, (((0,), (0,)), ((), ())), preferred_element_type=jnp.float32
+            pre_grad[:own], piece[:own], (((0,), (0,)), ((), ())), preferred_element_type=jnp.float32
         )
         for piece in patches
     ]
     partial_grad = jnp.concatenate(blocks, axis=1)
-    owned = lax.psum_scatter(partial_grad, "tm", scatter_dimension=1, tiled=True)
-    kernel_grad = lax.psum_scatter(owned, "rows", scatter_dimension=0, tiled=True)
+    kernel_grad = exchanged_scatter(partial_grad)
     return (activated, input_grad, kernel_grad)
 
 

time: 389 us -> 120 us (0.31)
  waiting for transfers between devices: 328 us -> 36.4 us
  starting transfers between devices: 14.8 us -> 46.9 us
  between operations: 14.4 us -> 1.2 us
  other arithmetic: 1.38 us -> 12.1 us
    unnamed x4 -> x0, waiting for transfers between devices: 319 us -> none
    all_to_all x0 -> x2, starting transfers between devices: none -> 30.8 us  [the longest x1 23.2 us: exchanged_scatter(): x = lax.all_to_all(x, 'rows', 0, 0).sum(axis=0)]
    all_to_all x0 -> x2, waiting for transfers between devices: none -> 26.7 us  [the longest x1 19.3 us: exchanged_scatter(): x = lax.all_to_all(x, 'rows', 0, 0).sum(axis=0)]
    unnamed x12 -> x23, local copies, waits for them, and re-layouts: 11 us -> 1.43 us
    dot_general x9, matrix products: 8.56 us -> 2.29 us  [local(): lax.dot_general(pre_grad[:own], piece[:own], (((0,), (0,)), ((), ())), pr...]
  transfers between devices with their start and end apart: 8 -> 8, of which waited for: 6 -> 5; matrix products, arithmetic and copies ran while one was open for 3% -> 12% of each run, Pallas kernels for 0% -> 0%
where the time goes in v10:
time: 120 us; the launch traced here: 119 us
  starting transfers between devices  46.9 us (39%)
  waiting for transfers between devices  36.4 us (30%)
  other arithmetic  12.1 us (10%)
  matrix products  11.4 us (10%)
  local copies, waits for them, and re-layouts  10.9 us (9%)
  between operations  1.2 us (1%)
    all_to_all x1, starting transfers between devices, exchanged_scatter(): x = lax.all_to_all(x, 'rows', 0, 0).sum(axis=0)  23.2 us
    all_to_all x1, waiting for transfers between devices, exchanged_scatter(): x = lax.all_to_all(x, 'rows', 0, 0).sum(axis=0)  19.3 us
    ppermute x2, waiting for transfers between devices, padded(): lax.ppermute(lax.slice_in_dim(block, 0, width, axis=dim), axis, backward)  9.2 us
    dot_general x16, matrix products, apply_taps(): jnp.dot(patches[index], kmat[index // 3, index % 3], preferred_element_ty...  8.47 us
    all_to_all x1, starting transfers between devices, exchanged_scatter(): x = lax.all_to_all(x, 'tm', 1, 1).sum(axis=1)  7.63 us
    all_to_all x1, waiting for transfers between devices, exchanged_scatter(): x = lax.all_to_all(x, 'tm', 1, 1).sum(axis=1)  7.44 us
    ppermute x2, starting transfers between devices, padded(): lax.ppermute(lax.slice_in_dim(block, 0, width, axis=dim), axis, backward)  6.28 us
    ppermute x2, starting transfers between devices, padded(): lax.ppermute(lax.slice_in_dim(block, block.shape[dim] - width, None, axis...  5.39 us
  transfers between devices with their start and end apart: 8, of which 5 were waited for; matrix products, arithmetic and copies ran while one was open for 12% of the time, Pallas kernels for 0%

profile of v10, /device:TPU:56, one launch (start us, length us, event | category | flops | bytes accessed | tf_op | source)
XLA Modules:
  0.0 118.8 jit_solution(1416181582716815280)
XLA Ops:
  0.6 1.1 pad_maximum_fusion.17
  1.7 1.3 %collective-permute-start.1 = (bf16[2,2,128,256]{3,2,1,0:T(8,128)(2,1)S(1)}, bf16[2,2,128,256]{3,2,1,0:T(8,128)(2,1)S(1)}, u32[]{:S(2)}, u32[]{:S(2)}) collective-permute-start(bf16[2,2,128,256]{3,2,1,0:T(8,128)(2,1)S(1)} %pad_maximum_fusion.17), channel_id=1, source_target_pairs={{128,0},{256,128},{384,256},{512,384},{640,512},{768,640},{896,768... | collective-permute-start | bytes 786440 | tf_op jit(solution)/shard_map/ppermute | solution.py:10
  3.0 3.0 %collective-permute-start = (bf16[2,2,128,128]{3,2,1,0:T(8,128)(2,1)}, bf16[2,2,128,128]{3,2,1,0:T(8,128)(2,1)S(1)}, u32[]{:S(2)}, u32[]{:S(2)}) collective-permute-start(bf16[2,2,128,128]{3,2,1,0:T(8,128)(2,1)} %param.3), channel_id=1, source_target_pairs={{0,128},{128,256},{256,384},{384,512},{512,640},{640,768},{768,896... | collective-permute-start | bytes 393224 | tf_op jit(solution)/shard_map/ppermute | solution.py:10
  6.1 0.7 fusion.60
  6.8 0.5 collective-permute-done
  7.2 0.9 pad_maximum_fusion.12
  8.2 0.8 fusion.57
  9.0 3.5 %collective-permute-start.2 = (bf16[6,1,128,128]{3,2,1,0:T(8,128)(2,1)}, bf16[6,1,128,128]{3,2,1,0:T(8,128)(2,1)}, u32[]{:S(2)}, u32[]{:S(2)}) collective-permute-start(bf16[6,1,128,128]{3,2,1,0:T(8,128)(2,1)} %get-tuple-element.53), channel_id=1, source_target_pairs={{0,1},{1,2},{2,3},{3,4},{4,5},{5,6},{6,7},{7,8},{8,9},{9,10},{10,1... | collective-permute-start | bytes 589832 | tf_op jit(solution)/shard_map/ppermute | solution.py:18
  12.5 2.4 %collective-permute-start.3 = (bf16[6,1,128,128]{3,2,1,0:T(8,128)(2,1)}, bf16[6,1,128,128]{3,2,1,0:T(8,128)(2,1)}, u32[]{:S(2)}, u32[]{:S(2)}) collective-permute-start(bf16[6,1,128,128]{3,2,1,0:T(8,128)(2,1)} %get-tuple-element.54), channel_id=1, source_target_pairs={{1,0},{2,1},{3,2},{4,3},{5,4},{6,5},{7,6},{8,7},{9,8},{10,9},{11,1... | collective-permute-start | bytes 589832 | tf_op jit(solution)/shard_map/ppermute | solution.py:21
  14.9 1.4 %copy.8 = bf16[3,3,3,128,128]{3,4,2,1,0:T(8,128)(2,1)S(1)} copy(bf16[3,3,3,128,128]{4,3,2,1,0:T(8,128)(2,1)S(1)} %copy-done.1) | data formatting | bytes 1769472 | tf_op args[1]
  16.4 1.0 pad_maximum_fusion.18
  17.4 5.6 %collective-permute-done.3 = bf16[6,1,128,128]{3,2,1,0:T(8,128)(2,1)} collective-permute-done((bf16[6,1,128,128]{3,2,1,0:T(8,128)(2,1)}, bf16[6,1,128,128]{3,2,1,0:T(8,128)(2,1)}, u32[]{:S(2)}, u32[]{:S(2)}) %collective-permute-start.3) | collective-permute-done | bytes 196640 | tf_op jit(solution)/shard_map/ppermute | solution.py:21
  23.1 1.3 %select_maximum_fusion = bf16[6,4,130,128]{3,2,1,0:T(8,128)(2,1)S(1)} fusion(bf16[6,1,128,128]{3,2,1,0:T(8,128)(2,1)} %collective-permute-done.3, bf16[6,1,128,128]{3,2,1,0:T(8,128)(2,1)} %collective-permute-done.2, bf16[2,2,128,128]{3,2,1,0:T(8,128)(2,1)S(1)} %get-tuple-element.65, bf16[2,2,128,128]{3,2,1,0:T(8,128)(2,1)S(1)} %copy-done, ...), kind=kLoop, calls=%fused_computation.32 | loop fusion | flops 7188480 | bytes 1585152 | tf_op jit(solution)/shard_map/concatenate | solution.py:22
  24.3 0.9 fusion.53
  25.3 1.1 pad_maximum_fusion.9
  27.0 0.4 pad_maximum_fusion.7
  27.5 0.8 slice-done
  29.1 0.4 fusion.40
  29.5 0.4 convolution_add_fusion.7
  29.8 0.4 convolution_add_fusion.6
  30.2 0.4 convolution_add_fusion.5
  30.6 0.4 convolution_add_fusion.4
  31.0 0.4 convolution_add_fusion.3
  31.3 0.4 convolution_add_fusion.2
  31.7 0.4 convolution_add_fusion.1
  32.1 1.5 %fusion.14 = (bf16[1024,128]{1,0:T(8,128)(2,1)S(1)}, f32[1024,128]{1,0:T(8,128)}, f32[1024,128]{1,0:T(8,128)}) fusion(bf16[4,2,128,128]{3,2,1,0:T(8,128)(2,1)S(1)} %pad_maximum_fusion.18, f32[1024,128]{1,0:T(8,128)S(1)} %convolution_add_fusion.1, bf16[1024,384]{1,0:T(8,128)(2,1)S(1)} %bitcast.154, bf16[3,3,384,128]{3,2,1,0:T(8,128)(2,1)S(1)} %bitcast.144), kind=kOutput, calls=%fused_computation.57 | convolution fusion | flops 102105088 | bytes 2981888 | tf_op jit(solution)/shard_map/dot_general | solution.py:45
  35.9 1.7 %copy.9 = f32[128,3456]{0,1:T(8,128)} copy(f32[128,3456]{1,0:T(8,128)S(1)} %convolution_dynamic-update-slice_fusion) | data formatting | bytes 3538944 | tf_op jit(solution)/shard_map/concatenate | solution.py:91
  37.6 7.6 %all-to-all-start = ((f32[128,8,432]{0,2,1:T(8,128)}), f32[128,8,432]{0,2,1:T(8,128)S(1)}, u32[]{:S(2)}, u32[]{:S(2)}) async-start(f32[128,8,432]{0,2,1:T(8,128)} %bitcast.127), calls=%async_computation | async-start | bytes 3538944 | tf_op jit(solution)/shard_map/all_to_all | solution.py:55
  45.3 1.9 %collective-permute-start.4 = (bf16[4,1,128,128]{3,2,1,0:T(8,128)(2,1)S(1)}, bf16[4,1,128,128]{3,2,1,0:T(8,128)(2,1)S(1)}, u32[]{:S(2)}, u32[]{:S(2)}) collective-permute-start(bf16[4,1,128,128]{3,2,1,0:T(8,128)(2,1)S(1)} %get-tuple-element.62), channel_id=1, source_target_pairs={{0,1},{1,2},{2,3},{3,4},{4,5},{5,6},{6,7},{7,8},{8,9},{9,10},{10,1... | collective-permute-start | bytes 393224 | tf_op jit(solution)/shard_map/ppermute | solution.py:18
  47.2 3.9 %collective-permute-start.5 = (bf16[4,1,128,128]{3,2,1,0:T(8,128)(2,1)S(1)}, bf16[4,1,128,128]{3,2,1,0:T(8,128)(2,1)S(1)}, u32[]{:S(2)}, u32[]{:S(2)}) collective-permute-start(bf16[4,1,128,128]{3,2,1,0:T(8,128)(2,1)S(1)} %get-tuple-element.63), channel_id=1, source_target_pairs={{1,0},{2,1},{3,2},{4,3},{5,4},{6,5},{7,6},{8,7},{9,8},{10,9},{11,1... | collective-permute-start | bytes 393224 | tf_op jit(solution)/shard_map/ppermute | solution.py:21
  51.1 1.7 %fusion.34 = bf16[512,128]{1,0:T(8,128)(2,1)} fusion(f32[1024,128]{1,0:T(8,128)} %get-tuple-element.46, f32[1024,128]{1,0:T(8,128)} %get-tuple-element.68), kind=kLoop, calls=%fused_computation.94 | loop fusion | flops 131072 | bytes 655360 | tf_op jit(solution)/shard_map/convert_element_type | solution.py:71
  52.8 0.7 fusion.58
  53.5 3.6 %collective-permute-done.5 = bf16[4,1,128,128]{3,2,1,0:T(8,128)(2,1)S(1)} collective-permute-done((bf16[4,1,128,128]{3,2,1,0:T(8,128)(2,1)S(1)}, bf16[4,1,128,128]{3,2,1,0:T(8,128)(2,1)S(1)}, u32[]{:S(2)}, u32[]{:S(2)}) %collective-permute-start.5) | collective-permute-done | bytes 131104 | tf_op jit(solution)/shard_map/ppermute | solution.py:21
  57.3 1.1 fusion.56
  58.4 0.8 pad_maximum_fusion.16
  60.0 0.3 convolution_add_fusion.14
  60.2 0.3 convolution_add_fusion.13
  60.5 1.0 convolution_add_fusion.12
  61.5 7.4 %all-to-all-done = f32[128,8,432]{0,2,1:T(8,128)S(1)} async-done(((f32[128,8,432]{0,2,1:T(8,128)}), f32[128,8,432]{0,2,1:T(8,128)S(1)}, u32[]{:S(2)}, u32[]{:S(2)}) %all-to-all-start) | async-done | bytes 1769504 | tf_op jit(solution)/shard_map/all_to_all | solution.py:55
  68.9 0.8 reduce_sum.18
  69.7 1.8 %copy.10 = f32[128,1,432]{2,1,0:T(1,128)} copy(f32[128,1,432]{0,2,1:T(8,128)} %bitcast.170) | data formatting | bytes 442368 | tf_op jit(solution)/shard_map/all_to_all | solution.py:56
  71.6 23.2 %all-to-all-start.1 = ((f32[128,1,432]{2,1,0:T(1,128)}), f32[128,1,432]{2,1,0:T(1,128)S(1)}, u32[]{:S(2)}, u32[]{:S(2)}) async-start(f32[128,1,432]{2,1,0:T(1,128)} %copy.10), calls=%async_computation.1 | async-start | bytes 524288 | tf_op jit(solution)/shard_map/all_to_all | solution.py:56
  94.8 1.2 %convolution_add_fusion.11 = f32[512,128]{1,0:T(8,128)S(1)} fusion(f32[512,128]{1,0:T(8,128)} %convolution_add_fusion.12, bf16[512,384]{1,0:T(8,128)(2,1)S(1)} %bitcast.167, bf16[3,3,384,128]{3,2,1,0:T(8,128)(2,1)S(1)} %bitcast.150), kind=kOutput, calls=%fused_computation.25 | convolution fusion | flops 50397184 | bytes 1015808 | tf_op jit(solution)/shard_map/dot_general | solution.py:45
  96.1 1.2 fusion.16
  97.5 0.3 convolution_add_fusion.9
  97.8 0.9 fusion.1
  98.7 19.3 %all-to-all-done.1 = f32[128,1,432]{2,1,0:T(1,128)S(1)} async-done(((f32[128,1,432]{2,1,0:T(1,128)}), f32[128,1,432]{2,1,0:T(1,128)S(1)}, u32[]{:S(2)}, u32[]{:S(2)}) %all-to-all-start.1) | async-done | bytes 221216 | tf_op jit(solution)/shard_map/all_to_all | solution.py:56
  118.0 0.8 reduce_sum.19
  (59 shorter events, 5.0 us)
Async XLA Ops:
  0.6 14.3 %copy-start.1 = (bf16[3,3,3,128,128]{4,3,2,1,0:T(8,128)(2,1)S(1)}, bf16[3,3,3,128,128]{4,3,2,1,0:T(8,128)(2,1)}, u32[]{:S(2)}) copy-start(bf16[3,3,3,128,128]{4,3,2,1,0:T(8,128)(2,1)} %param.4) | copy-start | bytes 2654212
  1.7 4.4 %collective-permute-start.1 = (bf16[2,2,128,256]{3,2,1,0:T(8,128)(2,1)S(1)}, bf16[2,2,128,256]{3,2,1,0:T(8,128)(2,1)S(1)}, u32[]{:S(2)}, u32[]{:S(2)}) collective-permute-start(bf16[2,2,128,256]{3,2,1,0:T(8,128)(2,1)S(1)} %pad_maximum_fusion.17), channel_id=1, source_target_pairs={{128,0},{256,128},{384,256},{512,384},{640,512},{768,640},{896,768... | collective-permute-start | bytes 786440 | tf_op jit(solution)/shard_map/ppermute | solution.py:10
  3.0 4.2 %collective-permute-start = (bf16[2,2,128,128]{3,2,1,0:T(8,128)(2,1)}, bf16[2,2,128,128]{3,2,1,0:T(8,128)(2,1)S(1)}, u32[]{:S(2)}, u32[]{:S(2)}) collective-permute-start(bf16[2,2,128,128]{3,2,1,0:T(8,128)(2,1)} %param.3), channel_id=1, source_target_pairs={{0,128},{128,256},{256,384},{384,512},{512,640},{640,768},{768,896... | collective-permute-start | bytes 393224 | tf_op jit(solution)/shard_map/ppermute | solution.py:10
  8.2 8.2 %copy-start.2 = (bf16[6,2,128,128]{3,2,1,0:T(8,128)(2,1)}, bf16[6,2,128,128]{3,2,1,0:T(8,128)(2,1)S(1)}, u32[]{:S(2)}) copy-start(bf16[6,2,128,128]{3,2,1,0:T(8,128)(2,1)S(1)} %pad_maximum_fusion.12) | copy-start | bytes 1179652
  9.0 8.4 %collective-permute-start.2 = (bf16[6,1,128,128]{3,2,1,0:T(8,128)(2,1)}, bf16[6,1,128,128]{3,2,1,0:T(8,128)(2,1)}, u32[]{:S(2)}, u32[]{:S(2)}) collective-permute-start(bf16[6,1,128,128]{3,2,1,0:T(8,128)(2,1)} %get-tuple-element.53), channel_id=1, source_target_pairs={{0,1},{1,2},{2,3},{3,4},{4,5},{5,6},{6,7},{7,8},{8,9},{9,10},{10,1... | collective-permute-start | bytes 589832 | tf_op jit(solution)/shard_map/ppermute | solution.py:18
  12.5 10.5 %collective-permute-start.3 = (bf16[6,1,128,128]{3,2,1,0:T(8,128)(2,1)}, bf16[6,1,128,128]{3,2,1,0:T(8,128)(2,1)}, u32[]{:S(2)}, u32[]{:S(2)}) collective-permute-start(bf16[6,1,128,128]{3,2,1,0:T(8,128)(2,1)} %get-tuple-element.54), channel_id=1, source_target_pairs={{1,0},{2,1},{3,2},{4,3},{5,4},{6,5},{7,6},{8,7},{9,8},{10,9},{11,1... | collective-permute-start | bytes 589832 | tf_op jit(solution)/shard_map/ppermute | solution.py:21
  16.3 6.8 %copy-start = (bf16[2,2,128,128]{3,2,1,0:T(8,128)(2,1)S(1)}, bf16[2,2,128,128]{3,2,1,0:T(8,128)(2,1)}, u32[]{:S(2)}) copy-start(bf16[2,2,128,128]{3,2,1,0:T(8,128)(2,1)} %param.3) | copy-start | bytes 393220
  27.4 1.0 slice-start
  37.6 31.3 %all-to-all-start = ((f32[128,8,432]{0,2,1:T(8,128)}), f32[128,8,432]{0,2,1:T(8,128)S(1)}, u32[]{:S(2)}, u32[]{:S(2)}) async-start(f32[128,8,432]{0,2,1:T(8,128)} %bitcast.127), calls=%async_computation | async-start | bytes 3538944 | tf_op jit(solution)/shard_map/all_to_all | solution.py:55
  45.3 8.3 %collective-permute-start.4 = (bf16[4,1,128,128]{3,2,1,0:T(8,128)(2,1)S(1)}, bf16[4,1,128,128]{3,2,1,0:T(8,128)(2,1)S(1)}, u32[]{:S(2)}, u32[]{:S(2)}) collective-permute-start(bf16[4,1,128,128]{3,2,1,0:T(8,128)(2,1)S(1)} %get-tuple-element.62), channel_id=1, source_target_pairs={{0,1},{1,2},{2,3},{3,4},{4,5},{5,6},{6,7},{7,8},{8,9},{9,10},{10,1... | collective-permute-start | bytes 393224 | tf_op jit(solution)/shard_map/ppermute | solution.py:18
  47.2 9.9 %collective-permute-start.5 = (bf16[4,1,128,128]{3,2,1,0:T(8,128)(2,1)S(1)}, bf16[4,1,128,128]{3,2,1,0:T(8,128)(2,1)S(1)}, u32[]{:S(2)}, u32[]{:S(2)}) collective-permute-start(bf16[4,1,128,128]{3,2,1,0:T(8,128)(2,1)S(1)} %get-tuple-element.63), channel_id=1, source_target_pairs={{1,0},{2,1},{3,2},{4,3},{5,4},{6,5},{7,6},{8,7},{9,8},{10,9},{11,1... | collective-permute-start | bytes 393224 | tf_op jit(solution)/shard_map/ppermute | solution.py:21
  57.1 1.3 %copy-start.4 = (bf16[4,1,128,128]{3,2,1,0:T(8,128)(2,1)}, bf16[4,1,128,128]{3,2,1,0:T(8,128)(2,1)S(1)}, u32[]{:S(2)}) copy-start(bf16[4,1,128,128]{3,2,1,0:T(8,128)(2,1)S(1)} %collective-permute-done.5) | copy-start | bytes 393220
  61.5 33.3 %copy-start.3 = (bf16[2,2,128,384]{3,2,1,0:T(8,128)(2,1)S(1)}, bf16[2,2,128,384]{3,2,1,0:T(8,128)(2,1)}, u32[]{:S(2)}) copy-start(bf16[2,2,128,384]{3,2,1,0:T(8,128)(2,1)} %pad_maximum_fusion.16) | copy-start | bytes 1179652
  69.7 26.3 %copy-start.5 = (bf16[4,1,128,128]{3,2,1,0:T(8,128)(2,1)S(1)}, bf16[4,1,128,128]{3,2,1,0:T(8,128)(2,1)}, u32[]{:S(2)}) copy-start(bf16[4,1,128,128]{3,2,1,0:T(8,128)(2,1)} %copy-done.4) | copy-start | bytes 393220
  69.7 26.3 %copy-start.6 = (bf16[2,2,128,128]{3,2,1,0:T(8,128)(2,1)S(1)}, bf16[2,2,128,128]{3,2,1,0:T(8,128)(2,1)}, u32[]{:S(2)}) copy-start(bf16[2,2,128,128]{3,2,1,0:T(8,128)(2,1)} %get-tuple-element.27) | copy-start | bytes 393220
  69.7 26.3 %copy-start.7 = (bf16[2,2,128,128]{3,2,1,0:T(8,128)(2,1)S(1)}, bf16[2,2,128,128]{3,2,1,0:T(8,128)(2,1)}, u32[]{:S(2)}) copy-start(bf16[2,2,128,128]{3,2,1,0:T(8,128)(2,1)} %get-tuple-element.30) | copy-start | bytes 393220
  71.6 46.5 %all-to-all-start.1 = ((f32[128,1,432]{2,1,0:T(1,128)}), f32[128,1,432]{2,1,0:T(1,128)S(1)}, u32[]{:S(2)}, u32[]{:S(2)}) async-start(f32[128,1,432]{2,1,0:T(1,128)} %copy.10), calls=%async_computation.1 | async-start | bytes 524288 | tf_op jit(solution)/shard_map/all_to_all | solution.py:56
  96.0 1.5 %copy-start.8 = (bf16[2,2,128,128]{3,2,1,0:T(8,128)(2,1)S(1)}, bf16[2,2,128,128]{3,2,1,0:T(8,128)(2,1)}, u32[]{:S(2)}) copy-start(bf16[2,2,128,128]{3,2,1,0:T(8,128)(2,1)} %get-tuple-element.28) | copy-start | bytes 393220
  96.0 1.5 %copy-start.9 = (bf16[2,2,128,128]{3,2,1,0:T(8,128)(2,1)S(1)}, bf16[2,2,128,128]{3,2,1,0:T(8,128)(2,1)}, u32[]{:S(2)}) copy-start(bf16[2,2,128,128]{3,2,1,0:T(8,128)(2,1)} %get-tuple-element.29) | copy-start | bytes 393220
  96.0 1.5 %copy-start.10 = (bf16[512,128]{1,0:T(8,128)(2,1)S(1)}, bf16[512,128]{1,0:T(8,128)(2,1)}, u32[]{:S(2)}) copy-start(bf16[512,128]{1,0:T(8,128)(2,1)} %get-tuple-element.57) | copy-start | bytes 393220

commit v11 on v1

--- a/solution.py
+++ b/solution.py
@@ -48,6 +48,15 @@
     return total
 
 
+def exchanged_scatter(partial_t):
+    cols, outs = partial_t.shape
+    parts = lax.axis_size("tm")
+    x = partial_t.reshape(parts, cols // parts, outs)
+    x = lax.all_to_all(x, "tm", 0, 0).sum(axis=0)
+    x = lax.all_to_all(x.T, "rows", 0, 0).sum(axis=0)
+    return x.reshape(1, -1)
+
+
 def local(video, kernel, cotangent):
     frames, height, width, chans = video.shape
     forward_mat = kernel.reshape(3, 3, 3 * chans, chans)
@@ -72,13 +81,12 @@
     )
     blocks = [
         lax.dot_general(
-            pre_grad, piece, (((0,), (0,)), ((), ())), preferred_element_type=jnp.float32
+            piece, pre_grad, (((0,), (0,)), ((), ())), preferred_element_type=jnp.float32
         )
         for piece in patches
     ]
-    partial_grad = jnp.concatenate(blocks, axis=1)
-    owned = lax.psum_scatter(partial_grad, "tm", scatter_dimension=1, tiled=True)
-    kernel_grad = lax.psum_scatter(owned, "rows", scatter_dimension=0, tiled=True)
+    partial_grad = jnp.concatenate(blocks, axis=0)
+    kernel_grad = exchanged_scatter(partial_grad)
     return (activated, input_grad, kernel_grad)
 
 

time: 389 us -> 119 us (0.31)
  waiting for transfers between devices: 328 us -> 46.1 us
  starting transfers between devices: 14.8 us -> 47.5 us
  between operations: 14.4 us -> 1.09 us
  matrix products: 14.7 us -> 9.58 us
    unnamed x4 -> x0, waiting for transfers between devices: 319 us -> none
    all_to_all x0 -> x2, waiting for transfers between devices: none -> 37.8 us  [the longest x1 19.6 us: exchanged_scatter(): x = lax.all_to_all(x.T, 'rows', 0, 0).sum(axis=0)]
    all_to_all x0 -> x2, starting transfers between devices: none -> 32.8 us  [the longest x1 24.2 us: exchanged_scatter(): x = lax.all_to_all(x.T, 'rows', 0, 0).sum(axis=0)]
    unnamed x12 -> x14, local copies, waits for them, and re-layouts: 11 us -> 4.51 us
    dot_general x9, matrix products: 8.56 us -> 2.74 us  [local(): lax.dot_general(piece, pre_grad, (((0,), (0,)), ((), ())), preferred_elem...]
  transfers between devices with their start and end apart: 8 -> 8, of which waited for: 6 -> 5; matrix products, arithmetic and copies ran while one was open for 3% -> 10% of each run, Pallas kernels for 0% -> 0%
where the time goes in v11:
time: 119 us; the launch traced here: 118 us
  starting transfers between devices  47.5 us (40%)
  waiting for transfers between devices  46.1 us (39%)
  matrix products  9.58 us (8%)
  local copies, waits for them, and re-layouts  9.34 us (8%)
  other arithmetic  4.29 us (4%)
    all_to_all x1, starting transfers between devices, exchanged_scatter(): x = lax.all_to_all(x.T, 'rows', 0, 0).sum(axis=0)  24.2 us
    all_to_all x1, waiting for transfers between devices, exchanged_scatter(): x = lax.all_to_all(x.T, 'rows', 0, 0).sum(axis=0)  19.6 us
    all_to_all x1, waiting for transfers between devices, exchanged_scatter(): x = lax.all_to_all(x, 'tm', 0, 0).sum(axis=0)  18.2 us
    all_to_all x1, starting transfers between devices, exchanged_scatter(): x = lax.all_to_all(x, 'tm', 0, 0).sum(axis=0)  8.64 us
    dot_general x16, matrix products, apply_taps(): jnp.dot(patches[index], kmat[index // 3, index % 3], preferred_element_ty...  6.33 us
    ppermute x2, starting transfers between devices, padded(): lax.ppermute(lax.slice_in_dim(block, 0, width, axis=dim), axis, backward)  6.23 us
    ppermute x2, starting transfers between devices, padded(): lax.ppermute(lax.slice_in_dim(block, block.shape[dim] - width, None, axis...  5.46 us
    ppermute x2, waiting for transfers between devices, padded(): lax.ppermute(lax.slice_in_dim(block, 0, width, axis=dim), axis, backward)  4.52 us
  transfers between devices with their start and end apart: 8, of which 5 were waited for; matrix products, arithmetic and copies ran while one was open for 10% of the time, Pallas kernels for 0%

profile of v11, /device:TPU:56, one launch (start us, length us, event | category | flops | bytes accessed | tf_op | source)
XLA Modules:
  0.0 117.9 jit_solution(10373596799393362830)
XLA Ops:
  0.6 1.7 %collective-permute-start = (bf16[2,2,128,128]{3,2,1,0:T(8,128)(2,1)}, bf16[2,2,128,128]{3,2,1,0:T(8,128)(2,1)S(1)}, u32[]{:S(2)}, u32[]{:S(2)}) collective-permute-start(bf16[2,2,128,128]{3,2,1,0:T(8,128)(2,1)} %param.3), channel_id=1, source_target_pairs={{0,128},{128,256},{256,384},{384,512},{512,640},{640,768},{768,896... | collective-permute-start | bytes 393224 | tf_op jit(solution)/shard_map/ppermute | solution.py:10
  2.4 1.2 collective-permute-done
  3.6 0.9 constant_dynamic-update-slice_fusion
  4.5 3.5 %collective-permute-start.1 = (bf16[4,1,128,128]{3,2,1,0:T(8,128)(2,1)S(1)}, bf16[4,1,128,128]{3,2,1,0:T(8,128)(2,1)S(1)}, u32[]{:S(2)}, u32[]{:S(2)}) collective-permute-start(bf16[4,1,128,128]{3,2,1,0:T(8,128)(2,1)S(1)} %get-tuple-element.60), channel_id=1, source_target_pairs={{0,1},{1,2},{2,3},{3,4},{4,5},{5,6},{6,7},{7,8},{8,9},{9,10},{10,1... | collective-permute-start | bytes 393224 | tf_op jit(solution)/shard_map/ppermute | solution.py:18
  8.0 2.4 %collective-permute-start.2 = (bf16[4,1,128,128]{3,2,1,0:T(8,128)(2,1)S(1)}, bf16[4,1,128,128]{3,2,1,0:T(8,128)(2,1)S(1)}, u32[]{:S(2)}, u32[]{:S(2)}) collective-permute-start(bf16[4,1,128,128]{3,2,1,0:T(8,128)(2,1)S(1)} %get-tuple-element.61), channel_id=1, source_target_pairs={{1,0},{2,1},{3,2},{4,3},{5,4},{6,5},{7,6},{8,7},{9,8},{10,9},{11,1... | collective-permute-start | bytes 393224 | tf_op jit(solution)/shard_map/ppermute | solution.py:21
  10.4 2.0 %copy.8 = bf16[3,3,3,128,128]{3,4,2,1,0:T(8,128)(2,1)S(1)} copy(bf16[3,3,3,128,128]{4,3,2,1,0:T(8,128)(2,1)} %param.4) | data formatting | bytes 1769472 | tf_op args[1]
  12.5 4.5 %collective-permute-done.2 = bf16[4,1,128,128]{3,2,1,0:T(8,128)(2,1)S(1)} collective-permute-done((bf16[4,1,128,128]{3,2,1,0:T(8,128)(2,1)S(1)}, bf16[4,1,128,128]{3,2,1,0:T(8,128)(2,1)S(1)}, u32[]{:S(2)}, u32[]{:S(2)}) %collective-permute-start.2) | collective-permute-done | bytes 131104 | tf_op jit(solution)/shard_map/ppermute | solution.py:21
  17.2 0.4 fusion.26
  17.8 0.9 copy-done
  19.1 0.3 convolution_add_fusion.15
  19.4 0.3 convolution_add_fusion.14
  20.1 0.3 convolution_add_fusion.12
  21.0 0.3 convolution_add_fusion.10
  21.2 0.3 convolution_add_fusion.9
  21.6 1.0 fusion.15
  22.6 0.3 convolution_dynamic-update-slice_fusion.8
  22.9 0.3 convolution_dynamic-update-slice_fusion.7
  23.2 0.3 convolution_dynamic-update-slice_fusion.6
  23.5 0.3 convolution_dynamic-update-slice_fusion.5
  23.9 0.3 convolution_dynamic-update-slice_fusion.4
  24.2 0.3 convolution_dynamic-update-slice_fusion.3
  24.5 0.3 convolution_dynamic-update-slice_fusion.2
  24.8 1.3 %collective-permute-start.3 = (bf16[2,2,128,128]{3,2,1,0:T(8,128)(2,1)S(1)}, bf16[2,2,128,128]{3,2,1,0:T(8,128)(2,1)S(1)}, u32[]{:S(2)}, u32[]{:S(2)}) collective-permute-start(bf16[2,2,128,128]{3,2,1,0:T(8,128)(2,1)S(1)} %bitcast.125), channel_id=1, source_target_pairs={{128,0},{256,128},{384,256},{512,384},{640,512},{768,640},{896,768... | collective-permute-start | bytes 393224 | tf_op jit(solution)/shard_map/ppermute | solution.py:10
  26.1 0.3 convolution_dynamic-update-slice_fusion.1
  26.4 2.5 %collective-permute-done.3 = bf16[2,2,128,128]{3,2,1,0:T(8,128)(2,1)S(1)} collective-permute-done((bf16[2,2,128,128]{3,2,1,0:T(8,128)(2,1)S(1)}, bf16[2,2,128,128]{3,2,1,0:T(8,128)(2,1)S(1)}, u32[]{:S(2)}, u32[]{:S(2)}) %collective-permute-start.3) | collective-permute-done | bytes 131104 | tf_op jit(solution)/shard_map/ppermute | solution.py:10
  29.0 2.0 %collective-permute-start.4 = (bf16[4,1,128,128]{3,2,1,0:T(8,128)(2,1)S(1)}, bf16[4,1,128,128]{3,2,1,0:T(8,128)(2,1)S(1)}, u32[]{:S(2)}, u32[]{:S(2)}) collective-permute-start(bf16[4,1,128,128]{3,2,1,0:T(8,128)(2,1)S(1)} %get-tuple-element.51), channel_id=1, source_target_pairs={{0,1},{1,2},{2,3},{3,4},{4,5},{5,6},{6,7},{7,8},{8,9},{9,10},{10,1... | collective-permute-start | bytes 393224 | tf_op jit(solution)/shard_map/ppermute | solution.py:18
  30.9 3.9 %collective-permute-start.5 = (bf16[4,1,128,128]{3,2,1,0:T(8,128)(2,1)S(1)}, bf16[4,1,128,128]{3,2,1,0:T(8,128)(2,1)S(1)}, u32[]{:S(2)}, u32[]{:S(2)}) collective-permute-start(bf16[4,1,128,128]{3,2,1,0:T(8,128)(2,1)S(1)} %get-tuple-element.52), channel_id=1, source_target_pairs={{1,0},{2,1},{3,2},{4,3},{5,4},{6,5},{7,6},{8,7},{9,8},{10,9},{11,1... | collective-permute-start | bytes 393224 | tf_op jit(solution)/shard_map/ppermute | solution.py:21
  34.8 0.3 convolution_dynamic-update-slice_fusion
  35.1 1.2 %copy-done.1 = f32[3456,128]{1,0:T(8,128)} copy-done((f32[3456,128]{1,0:T(8,128)}, f32[3456,128]{1,0:T(8,128)S(1)}, u32[]{:S(2)}) %copy-start.1) | copy-done | bytes 1769496
  36.4 8.6 %all-to-all-start = ((f32[8,432,128]{2,1,0:T(8,128)}), f32[8,432,128]{2,1,0:T(8,128)S(1)}, u32[]{:S(2)}, u32[]{:S(2)}) async-start(f32[8,432,128]{2,1,0:T(8,128)} %bitcast.164), calls=%async_computation | async-start | bytes 3538944 | tf_op jit(solution)/shard_map/all_to_all | solution.py:55
  45.1 0.7 fusion.27
  45.9 1.1 fusion.25
  47.1 0.7 fusion.28
  48.2 0.3 fusion.22
  48.4 0.3 convolution_add_fusion.7
  49.0 0.3 convolution_add_fusion.5
  49.2 0.3 convolution_add_fusion.4
  49.5 1.0 convolution_add_fusion.3
  50.5 18.2 %all-to-all-done = f32[8,432,128]{2,1,0:T(8,128)S(1)} async-done(((f32[8,432,128]{2,1,0:T(8,128)}), f32[8,432,128]{2,1,0:T(8,128)S(1)}, u32[]{:S(2)}, u32[]{:S(2)}) %all-to-all-start) | async-done | bytes 1769504 | tf_op jit(solution)/shard_map/all_to_all | solution.py:55
  68.8 0.8 copy.9
  69.7 24.2 %all-to-all-start.1 = ((f32[128,1,432]{2,1,0:T(1,128)}), f32[128,1,432]{2,1,0:T(1,128)S(1)}, u32[]{:S(2)}, u32[]{:S(2)}) async-start(f32[128,1,432]{2,1,0:T(1,128)} %copy.9), calls=%async_computation.1 | async-start | bytes 524288 | tf_op jit(solution)/shard_map/all_to_all | solution.py:56
  93.8 1.1 pad_maximum_fusion.17
  94.9 1.0 pad_maximum_fusion.15
  96.0 0.3 convolution_add_fusion.2
  96.2 0.3 convolution_add_fusion.1
  96.5 0.9 fusion
  97.4 19.6 %all-to-all-done.1 = f32[128,1,432]{2,1,0:T(1,128)S(1)} async-done(((f32[128,1,432]{2,1,0:T(1,128)}), f32[128,1,432]{2,1,0:T(1,128)S(1)}, u32[]{:S(2)}, u32[]{:S(2)}) %all-to-all-start.1) | async-done | bytes 221216 | tf_op jit(solution)/shard_map/all_to_all | solution.py:56
  117.1 0.8 reduce_sum.19
  (35 shorter events, 2.8 us)
Async XLA Ops:
  0.6 2.9 %collective-permute-start = (bf16[2,2,128,128]{3,2,1,0:T(8,128)(2,1)}, bf16[2,2,128,128]{3,2,1,0:T(8,128)(2,1)S(1)}, u32[]{:S(2)}, u32[]{:S(2)}) collective-permute-start(bf16[2,2,128,128]{3,2,1,0:T(8,128)(2,1)} %param.3), channel_id=1, source_target_pairs={{0,128},{128,256},{256,384},{384,512},{512,640},{640,768},{768,896... | collective-permute-start | bytes 393224 | tf_op jit(solution)/shard_map/ppermute | solution.py:10
  4.5 7.9 %collective-permute-start.1 = (bf16[4,1,128,128]{3,2,1,0:T(8,128)(2,1)S(1)}, bf16[4,1,128,128]{3,2,1,0:T(8,128)(2,1)S(1)}, u32[]{:S(2)}, u32[]{:S(2)}) collective-permute-start(bf16[4,1,128,128]{3,2,1,0:T(8,128)(2,1)S(1)} %get-tuple-element.60), channel_id=1, source_target_pairs={{0,1},{1,2},{2,3},{3,4},{4,5},{5,6},{6,7},{7,8},{8,9},{9,10},{10,1... | collective-permute-start | bytes 393224 | tf_op jit(solution)/shard_map/ppermute | solution.py:18
  8.0 9.0 %collective-permute-start.2 = (bf16[4,1,128,128]{3,2,1,0:T(8,128)(2,1)S(1)}, bf16[4,1,128,128]{3,2,1,0:T(8,128)(2,1)S(1)}, u32[]{:S(2)}, u32[]{:S(2)}) collective-permute-start(bf16[4,1,128,128]{3,2,1,0:T(8,128)(2,1)S(1)} %get-tuple-element.61), channel_id=1, source_target_pairs={{1,0},{2,1},{3,2},{4,3},{5,4},{6,5},{7,6},{8,7},{9,8},{10,9},{11,1... | collective-permute-start | bytes 393224 | tf_op jit(solution)/shard_map/ppermute | solution.py:21
  17.6 1.2 copy-start
  19.7 0.9 copy-start.3
  20.7 0.9 copy-start.5
  24.8 4.1 %collective-permute-start.3 = (bf16[2,2,128,128]{3,2,1,0:T(8,128)(2,1)S(1)}, bf16[2,2,128,128]{3,2,1,0:T(8,128)(2,1)S(1)}, u32[]{:S(2)}, u32[]{:S(2)}) collective-permute-start(bf16[2,2,128,128]{3,2,1,0:T(8,128)(2,1)S(1)} %bitcast.125), channel_id=1, source_target_pairs={{128,0},{256,128},{384,256},{512,384},{640,512},{768,640},{896,768... | collective-permute-start | bytes 393224 | tf_op jit(solution)/shard_map/ppermute | solution.py:10
  29.0 16.0 %collective-permute-start.4 = (bf16[4,1,128,128]{3,2,1,0:T(8,128)(2,1)S(1)}, bf16[4,1,128,128]{3,2,1,0:T(8,128)(2,1)S(1)}, u32[]{:S(2)}, u32[]{:S(2)}) collective-permute-start(bf16[4,1,128,128]{3,2,1,0:T(8,128)(2,1)S(1)} %get-tuple-element.51), channel_id=1, source_target_pairs={{0,1},{1,2},{2,3},{3,4},{4,5},{5,6},{6,7},{7,8},{8,9},{9,10},{10,1... | collective-permute-start | bytes 393224 | tf_op jit(solution)/shard_map/ppermute | solution.py:18
  30.9 14.1 %collective-permute-start.5 = (bf16[4,1,128,128]{3,2,1,0:T(8,128)(2,1)S(1)}, bf16[4,1,128,128]{3,2,1,0:T(8,128)(2,1)S(1)}, u32[]{:S(2)}, u32[]{:S(2)}) collective-permute-start(bf16[4,1,128,128]{3,2,1,0:T(8,128)(2,1)S(1)} %get-tuple-element.52), channel_id=1, source_target_pairs={{1,0},{2,1},{3,2},{4,3},{5,4},{6,5},{7,6},{8,7},{9,8},{10,9},{11,1... | collective-permute-start | bytes 393224 | tf_op jit(solution)/shard_map/ppermute | solution.py:21
  35.1 1.2 %copy-start.1 = (f32[3456,128]{1,0:T(8,128)}, f32[3456,128]{1,0:T(8,128)S(1)}, u32[]{:S(2)}) copy-start(f32[3456,128]{1,0:T(8,128)S(1)} %convolution_dynamic-update-slice_fusion) | copy-start | bytes 5308420
  36.4 32.3 %all-to-all-start = ((f32[8,432,128]{2,1,0:T(8,128)}), f32[8,432,128]{2,1,0:T(8,128)S(1)}, u32[]{:S(2)}, u32[]{:S(2)}) async-start(f32[8,432,128]{2,1,0:T(8,128)} %bitcast.164), calls=%async_computation | async-start | bytes 3538944 | tf_op jit(solution)/shard_map/all_to_all | solution.py:55
  50.5 44.4 %copy-start.4 = (bf16[2,2,128,128]{3,2,1,0:T(8,128)(2,1)S(1)}, bf16[2,2,128,128]{3,2,1,0:T(8,128)(2,1)}, u32[]{:S(2)}) copy-start(bf16[2,2,128,128]{3,2,1,0:T(8,128)(2,1)} %get-tuple-element.6) | copy-start | bytes 393220
  68.8 27.1 %copy-start.2 = (f32[512,128]{1,0:T(8,128)S(1)}, f32[512,128]{1,0:T(8,128)}, u32[]{:S(2)}) copy-start(f32[512,128]{1,0:T(8,128)} %convolution_add_fusion.3) | copy-start | bytes 786436
  69.7 47.4 %all-to-all-start.1 = ((f32[128,1,432]{2,1,0:T(1,128)}), f32[128,1,432]{2,1,0:T(1,128)S(1)}, u32[]{:S(2)}, u32[]{:S(2)}) async-start(f32[128,1,432]{2,1,0:T(1,128)} %copy.9), calls=%async_computation.1 | async-start | bytes 524288 | tf_op jit(solution)/shard_map/all_to_all | solution.py:56

commit v12 on v1

--- a/solution.py
+++ b/solution.py
@@ -48,6 +48,14 @@
     return total
 
 
+def exchanged_scatter(partial_grad):
+    outs, cols = partial_grad.shape
+    parts = lax.axis_size("tm")
+    x = lax.all_to_all(partial_grad, "rows", 0, 0).sum(axis=0)
+    x = lax.all_to_all(x.reshape(parts, cols // parts), "tm", 0, 0).sum(axis=0)
+    return x.reshape(1, -1)
+
+
 def local(video, kernel, cotangent):
     frames, height, width, chans = video.shape
     forward_mat = kernel.reshape(3, 3, 3 * chans, chans)
@@ -77,8 +85,7 @@
         for piece in patches
     ]
     partial_grad = jnp.concatenate(blocks, axis=1)
-    owned = lax.psum_scatter(partial_grad, "tm", scatter_dimension=1, tiled=True)
-    kernel_grad = lax.psum_scatter(owned, "rows", scatter_dimension=0, tiled=True)
+    kernel_grad = exchanged_scatter(partial_grad)
     return (activated, input_grad, kernel_grad)
 
 

time: 389 us -> 152 us (0.39)
  waiting for transfers between devices: 328 us -> 82.7 us
  starting transfers between devices: 14.8 us -> 44.1 us
  between operations: 14.4 us -> 1.06 us
  matrix products: 14.7 us -> 10.1 us
    unnamed x4 -> x0, waiting for transfers between devices: 319 us -> none
    ppermute x2, waiting for transfers between devices: 0.01 us -> 66.8 us  [padded(): lax.ppermute(lax.slice_in_dim(block, block.shape[dim] - width, None, axis...]
    all_to_all x0 -> x2, starting transfers between devices: none -> 29.2 us  [the longest x1 23.2 us: exchanged_scatter(): x = lax.all_to_all(partial_grad, 'rows', 0, 0).sum(axis=0)]
    unnamed x12 -> x10, local copies, waits for them, and re-layouts: 11 us -> 4.21 us
    dot_general x9, matrix products: 8.56 us -> 2.27 us  [local(): lax.dot_general(pre_grad, piece, (((0,), (0,)), ((), ())), preferred_elem...]
  transfers between devices with their start and end apart: 8 -> 8, of which waited for: 6 -> 8; matrix products, arithmetic and copies ran while one was open for 3% -> 6% of each run, Pallas kernels for 0% -> 0%
where the time goes in v12:
time: 152 us
  waiting for transfers between devices  82.7 us (54%)
  starting transfers between devices  44.1 us (29%)
  local copies, waits for them, and re-layouts  11 us (7%)
  matrix products  10.1 us (7%)
  other arithmetic  2.98 us (2%)
    ppermute x2, waiting for transfers between devices, padded(): lax.ppermute(lax.slice_in_dim(block, block.shape[dim] - width, None, axis...  66.8 us
    all_to_all x1, starting transfers between devices, exchanged_scatter(): x = lax.all_to_all(partial_grad, 'rows', 0, 0).sum(axis=0)  23.2 us
    ppermute x2, waiting for transfers between devices, padded(): lax.ppermute(lax.slice_in_dim(block, 0, width, axis=dim), axis, backward)  8.79 us
    dot_general x16, matrix products, apply_taps(): jnp.dot(patches[index], kmat[index // 3, index % 3], preferred_element_ty...  7.27 us
    ppermute x2, starting transfers between devices, padded(): lax.ppermute(lax.slice_in_dim(block, block.shape[dim] - width, None, axis...  6.86 us
    all_to_all x1, starting transfers between devices, exchanged_scatter(): x = lax.all_to_all(x.reshape(parts, cols // parts), 'tm', 0, 0).sum(axis=0)  5.95 us
    ppermute x2, starting transfers between devices, padded(): lax.ppermute(lax.slice_in_dim(block, 0, width, axis=dim), axis, backward)  5.01 us
    unnamed x10, local copies, waits for them, and re-layouts  4.21 us
  transfers between devices with their start and end apart: 8, of which 8 were waited for; matrix products, arithmetic and copies ran while one was open for 6% of the time, Pallas kernels for 0%

profile of v12, /device:TPU:56, one launch (start us, length us, event | category | flops | bytes accessed | tf_op | source)
XLA Modules:
  0.0 151.9 jit_solution(4152095684387034838)
XLA Ops:
  0.6 1.7 %collective-permute-start = (bf16[2,2,128,128]{3,2,1,0:T(8,128)(2,1)}, bf16[2,2,128,128]{3,2,1,0:T(8,128)(2,1)S(1)}, u32[]{:S(2)}, u32[]{:S(2)}) collective-permute-start(bf16[2,2,128,128]{3,2,1,0:T(8,128)(2,1)} %param.3), channel_id=1, source_target_pairs={{0,128},{128,256},{256,384},{384,512},{512,640},{640,768},{768,896... | collective-permute-start | bytes 393224 | tf_op jit(solution)/shard_map/ppermute | solution.py:10
  2.4 1.2 collective-permute-done
  3.6 0.9 constant_dynamic-update-slice_fusion
  4.5 3.5 %collective-permute-start.1 = (bf16[4,1,128,128]{3,2,1,0:T(8,128)(2,1)S(1)}, bf16[4,1,128,128]{3,2,1,0:T(8,128)(2,1)S(1)}, u32[]{:S(2)}, u32[]{:S(2)}) collective-permute-start(bf16[4,1,128,128]{3,2,1,0:T(8,128)(2,1)S(1)} %get-tuple-element.60), channel_id=1, source_target_pairs={{0,1},{1,2},{2,3},{3,4},{4,5},{5,6},{6,7},{7,8},{8,9},{9,10},{10,1... | collective-permute-start | bytes 393224 | tf_op jit(solution)/shard_map/ppermute | solution.py:18
  8.0 2.4 %collective-permute-start.2 = (bf16[4,1,128,128]{3,2,1,0:T(8,128)(2,1)S(1)}, bf16[4,1,128,128]{3,2,1,0:T(8,128)(2,1)S(1)}, u32[]{:S(2)}, u32[]{:S(2)}) collective-permute-start(bf16[4,1,128,128]{3,2,1,0:T(8,128)(2,1)S(1)} %get-tuple-element.61), channel_id=1, source_target_pairs={{1,0},{2,1},{3,2},{4,3},{5,4},{6,5},{7,6},{8,7},{9,8},{10,9},{11,1... | collective-permute-start | bytes 393224 | tf_op jit(solution)/shard_map/ppermute | solution.py:21
  10.4 1.0 collective-permute-done.1
  11.4 5.6 %collective-permute-done.2 = bf16[4,1,128,128]{3,2,1,0:T(8,128)(2,1)S(1)} collective-permute-done((bf16[4,1,128,128]{3,2,1,0:T(8,128)(2,1)S(1)}, bf16[4,1,128,128]{3,2,1,0:T(8,128)(2,1)S(1)}, u32[]{:S(2)}, u32[]{:S(2)}) %collective-permute-start.2) | collective-permute-done | bytes 131104 | tf_op jit(solution)/shard_map/ppermute | solution.py:21
  17.2 0.5 fusion.26
  17.9 0.9 copy-done.1
  18.8 0.3 fusion.23
  19.2 0.3 convolution_add_fusion.15
  19.5 0.3 convolution_add_fusion.14
  19.9 0.3 convolution_add_fusion.13
  20.2 0.3 convolution_add_fusion.12
  20.8 0.3 convolution_add_fusion.11
  21.1 0.3 convolution_add_fusion.10
  21.3 0.3 convolution_add_fusion.9
  21.7 1.0 fusion.15
  23.0 0.3 convolution_dynamic-update-slice_fusion.7
  23.2 0.3 convolution_dynamic-update-slice_fusion.6
  23.5 0.3 convolution_dynamic-update-slice_fusion.5
  24.2 0.3 convolution_dynamic-update-slice_fusion.2
  25.0 3.1 %copy.12 = f32[128,1,3456]{2,1,0:T(1,128)} copy(f32[128,1,3456]{2,0,1:T(8,128)S(1)} %bitcast.161) | data formatting | bytes 3538944 | tf_op jit(solution)/shard_map/all_to_all | solution.py:54
  28.1 23.2 %all-to-all-start = ((f32[128,1,3456]{2,1,0:T(1,128)}), f32[128,1,3456]{2,1,0:T(1,128)S(1)}, u32[]{:S(2)}, u32[]{:S(2)}) async-start(f32[128,1,3456]{2,1,0:T(1,128)} %copy.12), calls=%async_computation | async-start | bytes 3538944 | tf_op jit(solution)/shard_map/all_to_all | solution.py:54
  51.3 1.3 collective-permute-start.3
  52.6 2.3 %collective-permute-done.3 = bf16[2,2,128,128]{3,2,1,0:T(8,128)(2,1)S(1)} collective-permute-done((bf16[2,2,128,128]{3,2,1,0:T(8,128)(2,1)S(1)}, bf16[2,2,128,128]{3,2,1,0:T(8,128)(2,1)S(1)}, u32[]{:S(2)}, u32[]{:S(2)}) %collective-permute-start.3) | collective-permute-done | bytes 131104 | tf_op jit(solution)/shard_map/ppermute | solution.py:10
  54.9 3.4 %collective-permute-start.4 = (bf16[4,1,128,128]{3,2,1,0:T(8,128)(2,1)S(1)}, bf16[4,1,128,128]{3,2,1,0:T(8,128)(2,1)S(1)}, u32[]{:S(2)}, u32[]{:S(2)}) collective-permute-start(bf16[4,1,128,128]{3,2,1,0:T(8,128)(2,1)S(1)} %get-tuple-element.51), channel_id=1, source_target_pairs={{0,1},{1,2},{2,3},{3,4},{4,5},{5,6},{6,7},{7,8},{8,9},{9,10},{10,1... | collective-permute-start | bytes 393224 | tf_op jit(solution)/shard_map/ppermute | solution.py:18
  58.3 2.7 %collective-permute-start.5 = (bf16[4,1,128,128]{3,2,1,0:T(8,128)(2,1)S(1)}, bf16[4,1,128,128]{3,2,1,0:T(8,128)(2,1)S(1)}, u32[]{:S(2)}, u32[]{:S(2)}) collective-permute-start(bf16[4,1,128,128]{3,2,1,0:T(8,128)(2,1)S(1)} %get-tuple-element.52), channel_id=1, source_target_pairs={{1,0},{2,1},{3,2},{4,3},{5,4},{6,5},{7,6},{8,7},{9,8},{10,9},{11,1... | collective-permute-start | bytes 393224 | tf_op jit(solution)/shard_map/ppermute | solution.py:21
  61.0 2.0 %copy.11 = bf16[3,3,3,128,128]{3,4,2,1,0:T(8,128)(2,1)S(1)} copy(bf16[3,3,3,128,128]{4,3,2,1,0:T(8,128)(2,1)} %param.4) | data formatting | bytes 1769472 | tf_op args[1]
  63.0 1.0 rev.3
  64.0 65.8 %collective-permute-done.4 = bf16[4,1,128,128]{3,2,1,0:T(8,128)(2,1)S(1)} collective-permute-done((bf16[4,1,128,128]{3,2,1,0:T(8,128)(2,1)S(1)}, bf16[4,1,128,128]{3,2,1,0:T(8,128)(2,1)S(1)}, u32[]{:S(2)}, u32[]{:S(2)}) %collective-permute-start.4) | collective-permute-done | bytes 131104 | tf_op jit(solution)/shard_map/ppermute | solution.py:18
  129.8 3.2 %collective-permute-done.5 = bf16[4,1,128,128]{3,2,1,0:T(8,128)(2,1)S(1)} collective-permute-done((bf16[4,1,128,128]{3,2,1,0:T(8,128)(2,1)S(1)}, bf16[4,1,128,128]{3,2,1,0:T(8,128)(2,1)S(1)}, u32[]{:S(2)}, u32[]{:S(2)}) %collective-permute-start.5) | collective-permute-done | bytes 131104 | tf_op jit(solution)/shard_map/ppermute | solution.py:21
  133.2 0.5 fusion.25
  134.3 0.9 copy-done
  135.2 0.3 fusion.22
  135.5 0.3 convolution_add_fusion.7
  135.8 0.3 convolution_add_fusion.6
  136.0 0.3 convolution_add_fusion.5
  136.3 0.3 convolution_add_fusion.4
  136.6 0.3 convolution_add_fusion.3
  136.9 0.3 convolution_add_fusion.2
  137.1 1.0 convolution_add_fusion.1
  138.2 1.0 reduce_sum.18
  139.2 0.7 all_to_all.14
  139.9 5.9 %all-to-all-start.1 = ((f32[8,1,432]{2,1,0:T(1,128)}), f32[8,1,432]{2,1,0:T(1,128)S(1)}, u32[]{:S(2)}, u32[]{:S(2)}) async-start(f32[8,1,432]{2,1,0:T(1,128)} %all_to_all.14), calls=%async_computation.1 | async-start | bytes 32768 | tf_op jit(solution)/shard_map/all_to_all | solution.py:55
  145.9 1.9 %fusion = bf16[512,128]{1,0:T(8,128)(2,1)} fusion(f32[512,128]{1,0:T(8,128)} %convolution_add_fusion.1, bf16[512,384]{1,0:T(8,128)(2,1)S(1)} %bitcast.164, bf16[3,3,384,128]{3,2,1,0:T(8,128)(2,1)S(1)} %bitcast.151), kind=kOutput, calls=%fused_computation.27 | convolution fusion | flops 50462720 | bytes 884736 | tf_op jit(solution)/shard_map/dot_general | solution.py:45
  147.8 3.5 %all-to-all-done.1 = f32[8,1,432]{2,1,0:T(1,128)S(1)} async-done(((f32[8,1,432]{2,1,0:T(1,128)}), f32[8,1,432]{2,1,0:T(1,128)S(1)}, u32[]{:S(2)}, u32[]{:S(2)}) %all-to-all-start.1) | async-done | bytes 13856 | tf_op jit(solution)/shard_map/all_to_all | solution.py:55
  151.2 0.6 reduce_sum.19
  (32 shorter events, 3.2 us)
Async XLA Ops:
  0.6 2.9 %collective-permute-start = (bf16[2,2,128,128]{3,2,1,0:T(8,128)(2,1)}, bf16[2,2,128,128]{3,2,1,0:T(8,128)(2,1)S(1)}, u32[]{:S(2)}, u32[]{:S(2)}) collective-permute-start(bf16[2,2,128,128]{3,2,1,0:T(8,128)(2,1)} %param.3), channel_id=1, source_target_pairs={{0,128},{128,256},{256,384},{384,512},{512,640},{640,768},{768,896... | collective-permute-start | bytes 393224 | tf_op jit(solution)/shard_map/ppermute | solution.py:10
  4.5 6.9 %collective-permute-start.1 = (bf16[4,1,128,128]{3,2,1,0:T(8,128)(2,1)S(1)}, bf16[4,1,128,128]{3,2,1,0:T(8,128)(2,1)S(1)}, u32[]{:S(2)}, u32[]{:S(2)}) collective-permute-start(bf16[4,1,128,128]{3,2,1,0:T(8,128)(2,1)S(1)} %get-tuple-element.60), channel_id=1, source_target_pairs={{0,1},{1,2},{2,3},{3,4},{4,5},{5,6},{6,7},{7,8},{8,9},{9,10},{10,1... | collective-permute-start | bytes 393224 | tf_op jit(solution)/shard_map/ppermute | solution.py:18
  8.0 9.0 %collective-permute-start.2 = (bf16[4,1,128,128]{3,2,1,0:T(8,128)(2,1)S(1)}, bf16[4,1,128,128]{3,2,1,0:T(8,128)(2,1)S(1)}, u32[]{:S(2)}, u32[]{:S(2)}) collective-permute-start(bf16[4,1,128,128]{3,2,1,0:T(8,128)(2,1)S(1)} %get-tuple-element.61), channel_id=1, source_target_pairs={{1,0},{2,1},{3,2},{4,3},{5,4},{6,5},{7,6},{8,7},{9,8},{10,9},{11,1... | collective-permute-start | bytes 393224 | tf_op jit(solution)/shard_map/ppermute | solution.py:21
  17.7 1.2 copy-start.1
  19.8 0.9 copy-start.2
  20.8 0.9 copy-start.3
  28.1 110.2 %all-to-all-start = ((f32[128,1,3456]{2,1,0:T(1,128)}), f32[128,1,3456]{2,1,0:T(1,128)S(1)}, u32[]{:S(2)}, u32[]{:S(2)}) async-start(f32[128,1,3456]{2,1,0:T(1,128)} %copy.12), calls=%async_computation | async-start | bytes 3538944 | tf_op jit(solution)/shard_map/all_to_all | solution.py:54
  51.3 3.6 %collective-permute-start.3 = (bf16[2,2,128,128]{3,2,1,0:T(8,128)(2,1)S(1)}, bf16[2,2,128,128]{3,2,1,0:T(8,128)(2,1)S(1)}, u32[]{:S(2)}, u32[]{:S(2)}) collective-permute-start(bf16[2,2,128,128]{3,2,1,0:T(8,128)(2,1)S(1)} %bitcast.122), channel_id=1, source_target_pairs={{128,0},{256,128},{384,256},{512,384},{640,512},{768,640},{896,768... | collective-permute-start | bytes 393224 | tf_op jit(solution)/shard_map/ppermute | solution.py:10
  54.9 74.8 %collective-permute-start.4 = (bf16[4,1,128,128]{3,2,1,0:T(8,128)(2,1)S(1)}, bf16[4,1,128,128]{3,2,1,0:T(8,128)(2,1)S(1)}, u32[]{:S(2)}, u32[]{:S(2)}) collective-permute-start(bf16[4,1,128,128]{3,2,1,0:T(8,128)(2,1)S(1)} %get-tuple-element.51), channel_id=1, source_target_pairs={{0,1},{1,2},{2,3},{3,4},{4,5},{5,6},{6,7},{7,8},{8,9},{9,10},{10,1... | collective-permute-start | bytes 393224 | tf_op jit(solution)/shard_map/ppermute | solution.py:18
  58.3 74.6 %collective-permute-start.5 = (bf16[4,1,128,128]{3,2,1,0:T(8,128)(2,1)S(1)}, bf16[4,1,128,128]{3,2,1,0:T(8,128)(2,1)S(1)}, u32[]{:S(2)}, u32[]{:S(2)}) collective-permute-start(bf16[4,1,128,128]{3,2,1,0:T(8,128)(2,1)S(1)} %get-tuple-element.52), channel_id=1, source_target_pairs={{1,0},{2,1},{3,2},{4,3},{5,4},{6,5},{7,6},{8,7},{9,8},{10,9},{11,1... | collective-permute-start | bytes 393224 | tf_op jit(solution)/shard_map/ppermute | solution.py:21
  134.1 1.2 copy-start
  139.9 11.3 %all-to-all-start.1 = ((f32[8,1,432]{2,1,0:T(1,128)}), f32[8,1,432]{2,1,0:T(1,128)S(1)}, u32[]{:S(2)}, u32[]{:S(2)}) async-start(f32[8,1,432]{2,1,0:T(1,128)} %all_to_all.14), calls=%async_computation.1 | async-start | bytes 32768 | tf_op jit(solution)/shard_map/all_to_all | solution.py:55

commit v13 on v10

--- a/solution.py
+++ b/solution.py
@@ -48,12 +48,12 @@
     return total
 
 
-def exchanged_scatter(partial_grad):
-    outs, cols = partial_grad.shape
+def exchanged_scatter(partial_t):
+    cols, outs = partial_t.shape
     parts = lax.axis_size("tm")
-    x = partial_grad.reshape(outs, parts, cols // parts)
-    x = lax.all_to_all(x, "tm", 1, 1).sum(axis=1)
-    x = lax.all_to_all(x, "rows", 0, 0).sum(axis=0)
+    x = partial_t.reshape(parts, cols // parts, outs)
+    x = lax.all_to_all(x, "tm", 0, 0).sum(axis=0)
+    x = lax.all_to_all(x.T, "rows", 0, 0).sum(axis=0)
     return x.reshape(1, -1)
 
 
@@ -84,11 +84,11 @@
     )
     blocks = [
         lax.dot_general(
-            pre_grad[:own], piece[:own], (((0,), (0,)), ((), ())), preferred_element_type=jnp.float32
+            piece[:own], pre_grad[:own], (((0,), (0,)), ((), ())), preferred_element_type=jnp.float32
         )
         for piece in patches
     ]
-    partial_grad = jnp.concatenate(blocks, axis=1)
+    partial_grad = jnp.concatenate(blocks, axis=0)
     kernel_grad = exchanged_scatter(partial_grad)
     return (activated, input_grad, kernel_grad)
 

time: 120 us -> 120 us (level)
    concatenate x1 -> x0, local copies, waits for them, and re-layouts: 1.73 us -> none  [local(): partial_grad = jnp.concatenate(blocks, axis=1)]
    unnamed x23 -> x25, local copies, waits for them, and re-layouts: 1.43 us -> 2.66 us
where the time goes in v13:
time: 120 us; the launch traced here: 119 us
  starting transfers between devices  46.9 us (39%)
  waiting for transfers between devices  36.4 us (30%)
  other arithmetic  12.1 us (10%)
  matrix products  11.8 us (10%)
  local copies, waits for them, and re-layouts  10.4 us (9%)
  between operations  1.22 us (1%)
    all_to_all x1, starting transfers between devices, exchanged_scatter(): x = lax.all_to_all(x.T, 'rows', 0, 0).sum(axis=0)  23.2 us
    all_to_all x1, waiting for transfers between devices, exchanged_scatter(): x = lax.all_to_all(x.T, 'rows', 0, 0).sum(axis=0)  19.3 us
    ppermute x2, waiting for transfers between devices, padded(): lax.ppermute(lax.slice_in_dim(block, 0, width, axis=dim), axis, backward)  9.2 us
    dot_general x16, matrix products, apply_taps(): jnp.dot(patches[index], kmat[index // 3, index % 3], preferred_element_ty...  8.47 us
    all_to_all x1, starting transfers between devices, exchanged_scatter(): x = lax.all_to_all(x, 'tm', 0, 0).sum(axis=0)  7.63 us
    all_to_all x1, waiting for transfers between devices, exchanged_scatter(): x = lax.all_to_all(x, 'tm', 0, 0).sum(axis=0)  7.42 us
    ppermute x2, starting transfers between devices, padded(): lax.ppermute(lax.slice_in_dim(block, 0, width, axis=dim), axis, backward)  6.28 us
    ppermute x2, starting transfers between devices, padded(): lax.ppermute(lax.slice_in_dim(block, block.shape[dim] - width, None, axis...  5.39 us
  transfers between devices with their start and end apart: 8, of which 5 were waited for; matrix products, arithmetic and copies ran while one was open for 12% of the time, Pallas kernels for 0%

profile of v13, /device:TPU:56, one launch (start us, length us, event | category | flops | bytes accessed | tf_op | source)
XLA Modules:
  0.0 118.8 jit_solution(11622974822056922134)
XLA Ops:
  0.6 1.1 pad_maximum_fusion.17
  1.7 1.3 %collective-permute-start.1 = (bf16[2,2,128,256]{3,2,1,0:T(8,128)(2,1)S(1)}, bf16[2,2,128,256]{3,2,1,0:T(8,128)(2,1)S(1)}, u32[]{:S(2)}, u32[]{:S(2)}) collective-permute-start(bf16[2,2,128,256]{3,2,1,0:T(8,128)(2,1)S(1)} %pad_maximum_fusion.17), channel_id=1, source_target_pairs={{128,0},{256,128},{384,256},{512,384},{640,512},{768,640},{896,768... | collective-permute-start | bytes 786440 | tf_op jit(solution)/shard_map/ppermute | solution.py:10
  3.0 3.0 %collective-permute-start = (bf16[2,2,128,128]{3,2,1,0:T(8,128)(2,1)}, bf16[2,2,128,128]{3,2,1,0:T(8,128)(2,1)S(1)}, u32[]{:S(2)}, u32[]{:S(2)}) collective-permute-start(bf16[2,2,128,128]{3,2,1,0:T(8,128)(2,1)} %param.3), channel_id=1, source_target_pairs={{0,128},{128,256},{256,384},{384,512},{512,640},{640,768},{768,896... | collective-permute-start | bytes 393224 | tf_op jit(solution)/shard_map/ppermute | solution.py:10
  6.1 0.7 fusion.60
  6.8 0.5 collective-permute-done
  7.2 0.9 pad_maximum_fusion.12
  8.2 0.8 fusion.57
  9.0 3.5 %collective-permute-start.2 = (bf16[6,1,128,128]{3,2,1,0:T(8,128)(2,1)}, bf16[6,1,128,128]{3,2,1,0:T(8,128)(2,1)}, u32[]{:S(2)}, u32[]{:S(2)}) collective-permute-start(bf16[6,1,128,128]{3,2,1,0:T(8,128)(2,1)} %get-tuple-element.53), channel_id=1, source_target_pairs={{0,1},{1,2},{2,3},{3,4},{4,5},{5,6},{6,7},{7,8},{8,9},{9,10},{10,1... | collective-permute-start | bytes 589832 | tf_op jit(solution)/shard_map/ppermute | solution.py:18
  12.5 2.4 %collective-permute-start.3 = (bf16[6,1,128,128]{3,2,1,0:T(8,128)(2,1)}, bf16[6,1,128,128]{3,2,1,0:T(8,128)(2,1)}, u32[]{:S(2)}, u32[]{:S(2)}) collective-permute-start(bf16[6,1,128,128]{3,2,1,0:T(8,128)(2,1)} %get-tuple-element.54), channel_id=1, source_target_pairs={{1,0},{2,1},{3,2},{4,3},{5,4},{6,5},{7,6},{8,7},{9,8},{10,9},{11,1... | collective-permute-start | bytes 589832 | tf_op jit(solution)/shard_map/ppermute | solution.py:21
  14.9 1.4 %copy.8 = bf16[3,3,3,128,128]{3,4,2,1,0:T(8,128)(2,1)S(1)} copy(bf16[3,3,3,128,128]{4,3,2,1,0:T(8,128)(2,1)S(1)} %copy-done.1) | data formatting | bytes 1769472 | tf_op args[1]
  16.4 1.0 pad_maximum_fusion.18
  17.4 5.6 %collective-permute-done.3 = bf16[6,1,128,128]{3,2,1,0:T(8,128)(2,1)} collective-permute-done((bf16[6,1,128,128]{3,2,1,0:T(8,128)(2,1)}, bf16[6,1,128,128]{3,2,1,0:T(8,128)(2,1)}, u32[]{:S(2)}, u32[]{:S(2)}) %collective-permute-start.3) | collective-permute-done | bytes 196640 | tf_op jit(solution)/shard_map/ppermute | solution.py:21
  23.1 1.3 %select_maximum_fusion = bf16[6,4,130,128]{3,2,1,0:T(8,128)(2,1)S(1)} fusion(bf16[6,1,128,128]{3,2,1,0:T(8,128)(2,1)} %collective-permute-done.3, bf16[6,1,128,128]{3,2,1,0:T(8,128)(2,1)} %collective-permute-done.2, bf16[2,2,128,128]{3,2,1,0:T(8,128)(2,1)S(1)} %get-tuple-element.65, bf16[2,2,128,128]{3,2,1,0:T(8,128)(2,1)S(1)} %copy-done, ...), kind=kLoop, calls=%fused_computation.32 | loop fusion | flops 7188480 | bytes 1585152 | tf_op jit(solution)/shard_map/concatenate | solution.py:22
  24.3 0.9 fusion.53
  25.3 1.1 pad_maximum_fusion.9
  27.0 0.4 pad_maximum_fusion.7
  27.5 0.8 slice-done
  29.1 0.4 fusion.40
  29.5 0.4 convolution_add_fusion.7
  29.8 0.4 convolution_add_fusion.6
  30.2 0.4 convolution_add_fusion.5
  30.6 0.4 convolution_add_fusion.4
  31.0 0.4 convolution_add_fusion.3
  31.3 0.4 convolution_add_fusion.2
  31.7 0.4 convolution_add_fusion.1
  32.1 1.4 %fusion.14 = (bf16[1024,128]{1,0:T(8,128)(2,1)S(1)}, f32[1024,128]{1,0:T(8,128)}, f32[1024,128]{1,0:T(8,128)}) fusion(bf16[4,2,128,128]{3,2,1,0:T(8,128)(2,1)S(1)} %pad_maximum_fusion.18, f32[1024,128]{1,0:T(8,128)S(1)} %convolution_add_fusion.1, bf16[1024,384]{1,0:T(8,128)(2,1)S(1)} %bitcast.156, bf16[3,3,384,128]{3,2,1,0:T(8,128)(2,1)S(1)} %bitcast.145), kind=kOutput, calls=%fused_computation.57 | convolution fusion | flops 102105088 | bytes 2981888 | tf_op jit(solution)/shard_map/dot_general | solution.py:45
  33.8 0.3 convolution_dynamic-update-slice_fusion.7
  34.2 0.3 convolution_dynamic-update-slice_fusion.6
  34.8 0.3 convolution_dynamic-update-slice_fusion.4
  36.4 1.2 %copy-done.3 = f32[3456,128]{1,0:T(8,128)} copy-done((f32[3456,128]{1,0:T(8,128)}, f32[3456,128]{1,0:T(8,128)S(1)}, u32[]{:S(2)}) %copy-start.3) | copy-done | bytes 1769496
  37.6 7.6 %all-to-all-start = ((f32[8,432,128]{2,1,0:T(8,128)}), f32[8,432,128]{2,1,0:T(8,128)S(1)}, u32[]{:S(2)}, u32[]{:S(2)}) async-start(f32[8,432,128]{2,1,0:T(8,128)} %bitcast.155), calls=%async_computation | async-start | bytes 3538944 | tf_op jit(solution)/shard_map/all_to_all | solution.py:55
  45.3 1.9 %collective-permute-start.4 = (bf16[4,1,128,128]{3,2,1,0:T(8,128)(2,1)S(1)}, bf16[4,1,128,128]{3,2,1,0:T(8,128)(2,1)S(1)}, u32[]{:S(2)}, u32[]{:S(2)}) collective-permute-start(bf16[4,1,128,128]{3,2,1,0:T(8,128)(2,1)S(1)} %get-tuple-element.62), channel_id=1, source_target_pairs={{0,1},{1,2},{2,3},{3,4},{4,5},{5,6},{6,7},{7,8},{8,9},{9,10},{10,1... | collective-permute-start | bytes 393224 | tf_op jit(solution)/shard_map/ppermute | solution.py:18
  47.2 3.9 %collective-permute-start.5 = (bf16[4,1,128,128]{3,2,1,0:T(8,128)(2,1)S(1)}, bf16[4,1,128,128]{3,2,1,0:T(8,128)(2,1)S(1)}, u32[]{:S(2)}, u32[]{:S(2)}) collective-permute-start(bf16[4,1,128,128]{3,2,1,0:T(8,128)(2,1)S(1)} %get-tuple-element.63), channel_id=1, source_target_pairs={{1,0},{2,1},{3,2},{4,3},{5,4},{6,5},{7,6},{8,7},{9,8},{10,9},{11,1... | collective-permute-start | bytes 393224 | tf_op jit(solution)/shard_map/ppermute | solution.py:21
  51.1 1.7 %fusion.34 = bf16[512,128]{1,0:T(8,128)(2,1)} fusion(f32[1024,128]{1,0:T(8,128)} %get-tuple-element.46, f32[1024,128]{1,0:T(8,128)} %get-tuple-element.68), kind=kLoop, calls=%fused_computation.94 | loop fusion | flops 131072 | bytes 655360 | tf_op jit(solution)/shard_map/convert_element_type | solution.py:71
  52.8 0.7 fusion.58
  53.5 3.6 %collective-permute-done.5 = bf16[4,1,128,128]{3,2,1,0:T(8,128)(2,1)S(1)} collective-permute-done((bf16[4,1,128,128]{3,2,1,0:T(8,128)(2,1)S(1)}, bf16[4,1,128,128]{3,2,1,0:T(8,128)(2,1)S(1)}, u32[]{:S(2)}, u32[]{:S(2)}) %collective-permute-start.5) | collective-permute-done | bytes 131104 | tf_op jit(solution)/shard_map/ppermute | solution.py:21
  57.3 1.1 fusion.56
  58.5 0.8 pad_maximum_fusion.16
  60.5 1.0 convolution_add_fusion.12
  61.5 7.4 %all-to-all-done = f32[8,432,128]{2,1,0:T(8,128)S(1)} async-done(((f32[8,432,128]{2,1,0:T(8,128)}), f32[8,432,128]{2,1,0:T(8,128)S(1)}, u32[]{:S(2)}, u32[]{:S(2)}) %all-to-all-start) | async-done | bytes 1769504 | tf_op jit(solution)/shard_map/all_to_all | solution.py:55
  68.9 0.8 reduce_sum.18
  69.7 1.8 %copy.9 = f32[128,1,432]{2,1,0:T(1,128)} copy(f32[128,1,432]{0,2,1:T(8,128)} %bitcast.172) | data formatting | bytes 442368 | tf_op jit(solution)/shard_map/all_to_all | solution.py:56
  71.6 23.2 %all-to-all-start.1 = ((f32[128,1,432]{2,1,0:T(1,128)}), f32[128,1,432]{2,1,0:T(1,128)S(1)}, u32[]{:S(2)}, u32[]{:S(2)}) async-start(f32[128,1,432]{2,1,0:T(1,128)} %copy.9), calls=%async_computation.1 | async-start | bytes 524288 | tf_op jit(solution)/shard_map/all_to_all | solution.py:56
  94.8 1.2 %convolution_add_fusion.11 = f32[512,128]{1,0:T(8,128)S(1)} fusion(f32[512,128]{1,0:T(8,128)} %convolution_add_fusion.12, bf16[512,384]{1,0:T(8,128)(2,1)S(1)} %bitcast.169, bf16[3,3,384,128]{3,2,1,0:T(8,128)(2,1)S(1)} %bitcast.151), kind=kOutput, calls=%fused_computation.25 | convolution fusion | flops 50397184 | bytes 1015808 | tf_op jit(solution)/shard_map/dot_general | solution.py:45
  96.1 1.2 fusion.16
  97.8 0.9 fusion.1
  98.7 19.3 %all-to-all-done.1 = f32[128,1,432]{2,1,0:T(1,128)S(1)} async-done(((f32[128,1,432]{2,1,0:T(1,128)}), f32[128,1,432]{2,1,0:T(1,128)S(1)}, u32[]{:S(2)}, u32[]{:S(2)}) %all-to-all-start.1) | async-done | bytes 221216 | tf_op jit(solution)/shard_map/all_to_all | solution.py:56
  118.0 0.8 reduce_sum.19
  (60 shorter events, 5.3 us)
Async XLA Ops:
  0.6 14.3 %copy-start.1 = (bf16[3,3,3,128,128]{4,3,2,1,0:T(8,128)(2,1)S(1)}, bf16[3,3,3,128,128]{4,3,2,1,0:T(8,128)(2,1)}, u32[]{:S(2)}) copy-start(bf16[3,3,3,128,128]{4,3,2,1,0:T(8,128)(2,1)} %param.4) | copy-start | bytes 2654212
  1.7 4.4 %collective-permute-start.1 = (bf16[2,2,128,256]{3,2,1,0:T(8,128)(2,1)S(1)}, bf16[2,2,128,256]{3,2,1,0:T(8,128)(2,1)S(1)}, u32[]{:S(2)}, u32[]{:S(2)}) collective-permute-start(bf16[2,2,128,256]{3,2,1,0:T(8,128)(2,1)S(1)} %pad_maximum_fusion.17), channel_id=1, source_target_pairs={{128,0},{256,128},{384,256},{512,384},{640,512},{768,640},{896,768... | collective-permute-start | bytes 786440 | tf_op jit(solution)/shard_map/ppermute | solution.py:10
  3.0 4.2 %collective-permute-start = (bf16[2,2,128,128]{3,2,1,0:T(8,128)(2,1)}, bf16[2,2,128,128]{3,2,1,0:T(8,128)(2,1)S(1)}, u32[]{:S(2)}, u32[]{:S(2)}) collective-permute-start(bf16[2,2,128,128]{3,2,1,0:T(8,128)(2,1)} %param.3), channel_id=1, source_target_pairs={{0,128},{128,256},{256,384},{384,512},{512,640},{640,768},{768,896... | collective-permute-start | bytes 393224 | tf_op jit(solution)/shard_map/ppermute | solution.py:10
  8.2 8.2 %copy-start.2 = (bf16[6,2,128,128]{3,2,1,0:T(8,128)(2,1)}, bf16[6,2,128,128]{3,2,1,0:T(8,128)(2,1)S(1)}, u32[]{:S(2)}) copy-start(bf16[6,2,128,128]{3,2,1,0:T(8,128)(2,1)S(1)} %pad_maximum_fusion.12) | copy-start | bytes 1179652
  9.0 8.4 %collective-permute-start.2 = (bf16[6,1,128,128]{3,2,1,0:T(8,128)(2,1)}, bf16[6,1,128,128]{3,2,1,0:T(8,128)(2,1)}, u32[]{:S(2)}, u32[]{:S(2)}) collective-permute-start(bf16[6,1,128,128]{3,2,1,0:T(8,128)(2,1)} %get-tuple-element.53), channel_id=1, source_target_pairs={{0,1},{1,2},{2,3},{3,4},{4,5},{5,6},{6,7},{7,8},{8,9},{9,10},{10,1... | collective-permute-start | bytes 589832 | tf_op jit(solution)/shard_map/ppermute | solution.py:18
  12.5 10.5 %collective-permute-start.3 = (bf16[6,1,128,128]{3,2,1,0:T(8,128)(2,1)}, bf16[6,1,128,128]{3,2,1,0:T(8,128)(2,1)}, u32[]{:S(2)}, u32[]{:S(2)}) collective-permute-start(bf16[6,1,128,128]{3,2,1,0:T(8,128)(2,1)} %get-tuple-element.54), channel_id=1, source_target_pairs={{1,0},{2,1},{3,2},{4,3},{5,4},{6,5},{7,6},{8,7},{9,8},{10,9},{11,1... | collective-permute-start | bytes 589832 | tf_op jit(solution)/shard_map/ppermute | solution.py:21
  16.3 6.8 %copy-start = (bf16[2,2,128,128]{3,2,1,0:T(8,128)(2,1)S(1)}, bf16[2,2,128,128]{3,2,1,0:T(8,128)(2,1)}, u32[]{:S(2)}) copy-start(bf16[2,2,128,128]{3,2,1,0:T(8,128)(2,1)} %param.3) | copy-start | bytes 393220
  27.4 1.0 slice-start
  36.4 1.2 %copy-start.3 = (f32[3456,128]{1,0:T(8,128)}, f32[3456,128]{1,0:T(8,128)S(1)}, u32[]{:S(2)}) copy-start(f32[3456,128]{1,0:T(8,128)S(1)} %convolution_dynamic-update-slice_fusion) | copy-start | bytes 5308420
  37.6 31.3 %all-to-all-start = ((f32[8,432,128]{2,1,0:T(8,128)}), f32[8,432,128]{2,1,0:T(8,128)S(1)}, u32[]{:S(2)}, u32[]{:S(2)}) async-start(f32[8,432,128]{2,1,0:T(8,128)} %bitcast.155), calls=%async_computation | async-start | bytes 3538944 | tf_op jit(solution)/shard_map/all_to_all | solution.py:55
  45.3 8.3 %collective-permute-start.4 = (bf16[4,1,128,128]{3,2,1,0:T(8,128)(2,1)S(1)}, bf16[4,1,128,128]{3,2,1,0:T(8,128)(2,1)S(1)}, u32[]{:S(2)}, u32[]{:S(2)}) collective-permute-start(bf16[4,1,128,128]{3,2,1,0:T(8,128)(2,1)S(1)} %get-tuple-element.62), channel_id=1, source_target_pairs={{0,1},{1,2},{2,3},{3,4},{4,5},{5,6},{6,7},{7,8},{8,9},{9,10},{10,1... | collective-permute-start | bytes 393224 | tf_op jit(solution)/shard_map/ppermute | solution.py:18
  47.2 9.9 %collective-permute-start.5 = (bf16[4,1,128,128]{3,2,1,0:T(8,128)(2,1)S(1)}, bf16[4,1,128,128]{3,2,1,0:T(8,128)(2,1)S(1)}, u32[]{:S(2)}, u32[]{:S(2)}) collective-permute-start(bf16[4,1,128,128]{3,2,1,0:T(8,128)(2,1)S(1)} %get-tuple-element.63), channel_id=1, source_target_pairs={{1,0},{2,1},{3,2},{4,3},{5,4},{6,5},{7,6},{8,7},{9,8},{10,9},{11,1... | collective-permute-start | bytes 393224 | tf_op jit(solution)/shard_map/ppermute | solution.py:21
  57.1 1.3 %copy-start.5 = (bf16[4,1,128,128]{3,2,1,0:T(8,128)(2,1)}, bf16[4,1,128,128]{3,2,1,0:T(8,128)(2,1)S(1)}, u32[]{:S(2)}) copy-start(bf16[4,1,128,128]{3,2,1,0:T(8,128)(2,1)S(1)} %collective-permute-done.5) | copy-start | bytes 393220
  61.5 33.3 %copy-start.4 = (bf16[2,2,128,384]{3,2,1,0:T(8,128)(2,1)S(1)}, bf16[2,2,128,384]{3,2,1,0:T(8,128)(2,1)}, u32[]{:S(2)}) copy-start(bf16[2,2,128,384]{3,2,1,0:T(8,128)(2,1)} %pad_maximum_fusion.16) | copy-start | bytes 1179652
  69.7 26.3 %copy-start.6 = (bf16[4,1,128,128]{3,2,1,0:T(8,128)(2,1)S(1)}, bf16[4,1,128,128]{3,2,1,0:T(8,128)(2,1)}, u32[]{:S(2)}) copy-start(bf16[4,1,128,128]{3,2,1,0:T(8,128)(2,1)} %copy-done.5) | copy-start | bytes 393220
  69.7 26.3 %copy-start.7 = (bf16[2,2,128,128]{3,2,1,0:T(8,128)(2,1)S(1)}, bf16[2,2,128,128]{3,2,1,0:T(8,128)(2,1)}, u32[]{:S(2)}) copy-start(bf16[2,2,128,128]{3,2,1,0:T(8,128)(2,1)} %get-tuple-element.27) | copy-start | bytes 393220
  69.7 26.3 %copy-start.8 = (bf16[2,2,128,128]{3,2,1,0:T(8,128)(2,1)S(1)}, bf16[2,2,128,128]{3,2,1,0:T(8,128)(2,1)}, u32[]{:S(2)}) copy-start(bf16[2,2,128,128]{3,2,1,0:T(8,128)(2,1)} %get-tuple-element.30) | copy-start | bytes 393220
  71.6 46.5 %all-to-all-start.1 = ((f32[128,1,432]{2,1,0:T(1,128)}), f32[128,1,432]{2,1,0:T(1,128)S(1)}, u32[]{:S(2)}, u32[]{:S(2)}) async-start(f32[128,1,432]{2,1,0:T(1,128)} %copy.9), calls=%async_computation.1 | async-start | bytes 524288 | tf_op jit(solution)/shard_map/all_to_all | solution.py:56
  96.0 1.5 %copy-start.9 = (bf16[2,2,128,128]{3,2,1,0:T(8,128)(2,1)S(1)}, bf16[2,2,128,128]{3,2,1,0:T(8,128)(2,1)}, u32[]{:S(2)}) copy-start(bf16[2,2,128,128]{3,2,1,0:T(8,128)(2,1)} %get-tuple-element.28) | copy-start | bytes 393220
  96.0 1.5 %copy-start.10 = (bf16[2,2,128,128]{3,2,1,0:T(8,128)(2,1)S(1)}, bf16[2,2,128,128]{3,2,1,0:T(8,128)(2,1)}, u32[]{:S(2)}) copy-start(bf16[2,2,128,128]{3,2,1,0:T(8,128)(2,1)} %get-tuple-element.29) | copy-start | bytes 393220
  96.0 1.5 %copy-start.11 = (bf16[512,128]{1,0:T(8,128)(2,1)S(1)}, bf16[512,128]{1,0:T(8,128)(2,1)}, u32[]{:S(2)}) copy-start(bf16[512,128]{1,0:T(8,128)(2,1)} %get-tuple-element.57) | copy-start | bytes 393220
